TPU v7x, 512 devices: a whole 4x8x8 slice. The times are simulated.
512 devices in a mesh: segment: 16 (over z, core), mp: 32 (over y, x).
Axes of the slice: x: 4, y: 8, z: 8, core: 2. Of those that a mesh axis runs over, the one named last changes fastest.
Arguments:
- rows: bfloat16 [16, 2, 128, 8192], P('segment', None, None, 'mp'), may hold values from -6 to 6
- carry: bfloat16 [16, 128, 8192], P('segment', None, 'mp'), may hold values from -6 to 6
- weights: bfloat16 [16, 2, 8192, 4096], P('segment', None, None, 'mp'), may hold values from -1.1932427 to 1.1932427
- neighbours: int32 [16, 2, 2, 2], P('segment'), may hold values from 0 to 7, all different within a row
Outputs:
- passed: bfloat16 [16, 128, 8192], P('segment', None, 'mp')
- returned: bfloat16 [16, 128, 8192], P('segment', None, 'mp')
- kv_grad: bfloat16 [1024, 2, 4096], P(None, None, 'mp')
Inputs may be any that keep to these rules, and one draw needn't show every extreme that they name: Each group's 2 neighbours are different pool blocks; pool blocks are numbered by encoder segment in order, then by row.
All inputs are finite; a program needn't handle non-finite values.
Results may differ from a plain program's by a relative error of at most 0.02.
The roundings to bfloat16 on the way count: a program that leaves them out, or rounds other values in their place, can miss the bound.
Values may be sent and summed in bfloat16 or wider, within the bound.
No kernel may reach another device: no remote copies, remote signals or barrier semaphores. Data moves between devices by JAX's collectives and lax.ppermute only.
A program may use at most 64 MiB of HBM per device.

v0:
```python
import math

import jax
import jax.numpy as jnp
from jax import lax
from jax.sharding import PartitionSpec as P

GROUP = 64
NBLEN = 128
NEIGH = 2


def from_behind(x, axis, by):
    devices = lax.axis_size(axis)
    return lax.ppermute(x, axis, [(i, (i + by) % devices) for i in range(devices)])


def attend(queries, key_rows, score_scale):
    scores = (
        jnp.einsum("cqd,ckd->cqk", queries, key_rows, preferred_element_type=jnp.float32)
        * score_scale
    )
    soft = jax.nn.softmax(scores, axis=-1)
    return (soft, soft.astype(jnp.bfloat16))


def attend_back(queries, key_rows, value_rows, soft, rounded, upstream, score_scale):
    d_soft = jnp.einsum("cqd,ckd->cqk", upstream, value_rows, preferred_element_type=jnp.float32)
    grad_values = jnp.einsum("cqk,cqd->ckd", rounded, upstream, preferred_element_type=jnp.float32)
    d_scores = soft * (d_soft - jnp.sum(d_soft * soft, axis=-1, keepdims=True))
    grad_queries = (
        jnp.einsum("cqk,ckd->cqd", d_scores, key_rows.astype(jnp.float32)) * score_scale
    ).astype(jnp.bfloat16)
    grad_keys = jnp.einsum("cqk,cqd->ckd", d_scores, queries.astype(jnp.float32)) * score_scale
    return (grad_queries, grad_keys, grad_values)


def per_device(rows, carry, weights, neighbours):
    segments = lax.axis_size("segment")
    encoders = segments // 4
    first_encoder = segments - encoders
    is_encoder = lax.axis_index("segment") >= first_encoder
    local_rows = rows[0]
    local_carry = carry[0]
    full_rows, full_carry = (
        lax.all_gather(local_rows, "mp", axis=2, tiled=True),
        lax.all_gather(local_carry, "mp", axis=1, tiled=True),
    )
    tokens = local_rows.shape[1]
    width = full_rows.shape[2]
    head = weights.shape[3]
    w_query = weights[0, 0]
    w_out = weights[0, 1]

    def encode():
        flat = full_rows.reshape(2 * tokens, width)
        keyval = jnp.concatenate(
            [
                jnp.dot(flat, w_query, preferred_element_type=jnp.float32),
                jnp.dot(flat, w_out, preferred_element_type=jnp.float32),
            ],
            axis=-1,
        ).astype(jnp.bfloat16)
        return (keyval, jnp.zeros((2 * tokens, head), jnp.bfloat16))

    def decode():
        queries = jnp.dot(
            full_rows.reshape(2 * tokens, width), w_query, preferred_element_type=jnp.float32
        ).astype(jnp.bfloat16)
        return (jnp.zeros((2 * tokens, 2 * head), jnp.bfloat16), queries)

    encoded, queries = lax.cond(is_encoder, encode, decode)
    per_encoder = 2 * tokens // NBLEN
    pool_blocks = encoders * per_encoder
    collected = lax.all_gather(encoded, "segment", axis=0, tiled=True)
    pool = collected[first_encoder * 2 * tokens :].reshape(pool_blocks, NBLEN, 2 * head)
    groups = tokens // GROUP
    local_nbr = neighbours[0]
    score_scale = 1.0 / math.sqrt(head)
    query_blocks = queries.reshape(2, groups, GROUP, head)

    def fetch(batch):
        picked = pool[local_nbr[batch]].reshape(groups, NEIGH * NBLEN, 2 * head)
        return (picked[..., :head], picked[..., head:])

    keys_fwd, values_fwd = fetch(0)
    soft_fwd, rounded_fwd = attend(query_blocks[0], keys_fwd, score_scale)
    mixed = jnp.einsum(
        "cqk,ckd->cqd", rounded_fwd, values_fwd, preferred_element_type=jnp.float32
    ).astype(jnp.bfloat16)
    mixed_flat = mixed.reshape(tokens, head)
    piece = w_out
    out_sum = (
        lax.psum_scatter(
            lax.dot_general(
                piece, mixed_flat, (((1,), (1,)), ((), ())), preferred_element_type=jnp.float32
            ).astype(jnp.bfloat16),
            "mp",
            scatter_dimension=0,
            tiled=True,
        )
        .astype(jnp.float32)
        .T
    )
    forward_rows = (local_rows[0].astype(jnp.float32) + out_sum).astype(jnp.bfloat16)
    forward_rows = jnp.where(is_encoder, local_carry, forward_rows)
    passed = from_behind(forward_rows[None], "segment", 1)
    upstream = (
        jnp.dot(full_carry, w_out, preferred_element_type=jnp.float32)
        .astype(jnp.bfloat16)
        .reshape(groups, GROUP, head)
    )
    keys_back, values_back = fetch(1)
    soft_back, rounded_back = attend(query_blocks[1], keys_back, score_scale)
    grad_queries, grad_keys, grad_values = attend_back(
        query_blocks[1], keys_back, values_back, soft_back, rounded_back, upstream, score_scale
    )
    grad_flat = grad_queries.reshape(tokens, head)
    piece = w_query
    grad_input = (
        lax.psum_scatter(
            lax.dot_general(
                piece, grad_flat, (((1,), (1,)), ((), ())), preferred_element_type=jnp.float32
            ).astype(jnp.bfloat16),
            "mp",
            scatter_dimension=0,
            tiled=True,
        )
        .astype(jnp.float32)
        .T
    )
    back = local_carry.astype(jnp.float32) + grad_input
    back_rows = jnp.where(is_encoder, local_carry, back.astype(jnp.bfloat16))
    returned = from_behind(back_rows[None], "segment", -1)
    onehot = (
        local_nbr[1][..., None] == jnp.arange(pool_blocks, dtype=jnp.int32)[None, None, :]
    ).astype(jnp.float32)
    grad_keyval = jnp.concatenate([grad_keys, grad_values], axis=-1).reshape(
        groups, NEIGH, NBLEN, 2 * head
    )
    contrib = jnp.einsum("cbp,cbrf->prf", onehot, grad_keyval)
    contrib = jnp.where(is_encoder, jnp.zeros_like(contrib), contrib)
    pooled = lax.psum(contrib.astype(jnp.bfloat16), "segment").astype(jnp.float32)
    kv_grad = pooled.reshape(pool_blocks * NBLEN, 2, head).astype(jnp.bfloat16)
    return (passed, returned, kv_grad)


def solution(mesh):
    placed = (
        P("segment", None, None, "mp"),
        P("segment", None, "mp"),
        P("segment", None, None, "mp"),
        P("segment", None, None, None),
    )
    return jax.shard_map(
        per_device,
        mesh=mesh,
        in_specs=placed,
        out_specs=(P("segment", None, "mp"), P("segment", None, "mp"), P(None, None, "mp")),
        check_vma=False,
    )
```

profile of v0, /device:TPU:1, one launch (start us, length us, event | category | flops | bytes accessed | tf_op | source)
XLA Modules:
  0.0 812.3 jit_solution(813906581693303927)
XLA Ops:
  7.2 0.7 all-gather.8.cloned.1.call-update
  7.9 0.7 all-gather.10.cloned.1.call-update
  8.7 3.8 slice_bitcast_fusion
  12.5 89.2 %all-gather.8.cloned.1.call-done = bf16[1,2,128,8192]{3,2,1,0:T(8,128)(2,1)} async-done(((bf16[1,2,128,256]{3,2,1,0:T(8,128)(2,1)}), bf16[1,2,128,8192]{3,2,1,0:T(8,128)(2,1)}) %all-gather.8.cloned.1.call-update) | async-done | bytes 4194320 | tf_op jit(solution)/shard_map/all_gather | solution.py:46
  101.8 3.5 conditional.1
  101.8 3.4 convolution_convert_fusion
  105.3 0.6 copy-done.1
  106.1 79.5 %all-gather.10.cloned.1.call-done = bf16[1,128,8192]{2,1,0:T(8,128)(2,1)} async-done(((bf16[1,128,256]{2,1,0:T(8,128)(2,1)}), bf16[1,128,8192]{2,1,0:T(8,128)(2,1)}) %all-gather.10.cloned.1.call-update) | async-done | bytes 2097168 | tf_op jit(solution)/shard_map/all_gather | solution.py:47
  185.7 2.9 fusion.13
  188.6 45.9 %all-gather.6.cloned.1.call-done = bf16[4096,256]{1,0:T(8,128)(2,1)} async-done(((bf16[256,256]{1,0:T(8,128)(2,1)}), bf16[4096,256]{1,0:T(8,128)(2,1)}) %all-gather.6.cloned.1.call-update) | async-done | bytes 2097168 | tf_op jit(solution)/shard_map/all_gather | solution.py:75
  234.5 1.1 slice.67
  235.6 0.6 gather_fusion.1
  236.3 0.4 fusion.37
  236.9 0.3 fusion.12
  237.3 3.7 fusion.3
  241.1 0.6 gather_fusion
  242.0 0.3 convolution_convert_fusion.5
  242.4 3.6 fusion.2
  246.1 0.3 fusion.28
  246.5 0.4 convolution_multiply_fusion
  247.0 0.5 copy.12
  247.5 0.5 fusion.7
  248.0 0.6 copy.13
  248.6 1.0 convert_element_type.80
  249.6 205.3 %reduce-scatter.5.cloned.1.call-done = bf16[256,128]{0,1:T(8,128)(2,1)} async-done(((bf16[8192,128]{0,1:T(8,128)(2,1)}), bf16[256,128]{0,1:T(8,128)(2,1)}) %reduce-scatter.5.cloned.1.call-update) | async-done | bytes 65552 | tf_op jit(solution)/shard_map/reduce_scatter | solution.py:121
  454.9 224.9 %reduce-scatter.3.cloned.1.call-done = bf16[256,128]{0,1:T(8,128)(2,1)} async-done(((bf16[8192,128]{0,1:T(8,128)(2,1)}), bf16[256,128]{0,1:T(8,128)(2,1)}) %reduce-scatter.3.cloned.1.call-update) | async-done | bytes 65552 | tf_op jit(solution)/shard_map/reduce_scatter | solution.py:94
  679.8 0.9 fusion.25
  680.7 6.9 collective-permute-start
  687.6 114.5 %all-reduce.2.cloned.1.call-done = bf16[1024,2,128]{0,2,1:T(8,128)(2,1)} async-done(((bf16[1024,2,128]{0,2,1:T(8,128)(2,1)}), bf16[1024,2,128]{0,2,1:T(8,128)(2,1)}) %all-reduce.2.cloned.1.call-update) | async-done | bytes 524304 | tf_op jit(solution)/shard_map/psum | solution.py:143
  802.1 2.0 copy.14
  804.1 0.6 copy.25
  804.8 0.6 copy.26
  (35 shorter events, 1.5 us)
Async XLA Ops:
  7.2 94.6 %all-gather.8.cloned.1.call-start = ((), (), s32[]{:S(2)}) async-start(), calls=%async_computation.6 | async-start | bytes 4325376 | tf_op jit(solution)/shard_map/all_gather | solution.py:46
  7.9 177.8 %all-gather.10.cloned.1.call-start = ((), (), s32[]{:S(2)}) async-start(), calls=%async_computation.7 | async-start | bytes 2162688 | tf_op jit(solution)/shard_map/all_gather | solution.py:47
  8.6 225.9 %all-gather.6.cloned.1.call-start = ((), (), s32[]{:S(2)}) async-start(), calls=%async_computation.2 | async-start | bytes 2228224 | tf_op jit(solution)/shard_map/all_gather | solution.py:75
  101.8 4.2 copy-start.4
  105.3 0.7 copy-start.1
  106.0 348.9 %reduce-scatter.5.cloned.1.call-start = ((), (), s32[]{:S(2)}) async-start(), calls=%async_computation.4 | async-start | bytes 2162688 | tf_op jit(solution)/shard_map/reduce_scatter | solution.py:121
  241.0 438.8 %reduce-scatter.3.cloned.1.call-start = ((), (), s32[]{:S(2)}) async-start(), calls=%async_computation.3 | async-start | bytes 2162688 | tf_op jit(solution)/shard_map/reduce_scatter | solution.py:94
  246.0 556.2 %all-reduce.2.cloned.1.call-start = ((), (), s32[]{:S(2)}) async-start(), calls=%async_computation.5 | async-start | bytes 1048576 | tf_op jit(solution)/shard_map/psum | solution.py:143
  247.5 432.3 %copy-start.2 = (bf16[1,2,128,256]{3,2,1,0:T(8,128)(2,1)S(1)}, bf16[1,2,128,256]{3,2,1,0:T(8,128)(2,1)}, u32[]{:S(2)}) copy-start(bf16[1,2,128,256]{3,2,1,0:T(8,128)(2,1)} %param.6) | copy-start | bytes 393220
  247.5 432.3 %copy-start.3 = (bf16[1,128,256]{2,1,0:T(8,128)(2,1)S(1)}, bf16[1,128,256]{2,1,0:T(8,128)(2,1)}, u32[]{:S(2)}) copy-start(bf16[1,128,256]{2,1,0:T(8,128)(2,1)} %param.7) | copy-start | bytes 196612
  680.7 123.5 %collective-permute-start = (bf16[1,128,256]{2,1,0:T(8,128)(2,1)S(1)}, bf16[1,128,256]{2,1,0:T(8,128)(2,1)S(1)}, u32[]{:S(2)}, u32[]{:S(2)}) collective-permute-start(bf16[1,128,256]{2,1,0:T(8,128)(2,1)S(1)} %get-tuple-element.53), channel_id=1, source_target_pairs={{0,32},{32,64},{64,96},{96,128},{128,160},{160,192},{192,224},{224... | collective-permute-start | bytes 196616 | tf_op jit(solution)/shard_map/ppermute | solution.py:15
  687.6 116.5 %collective-permute-start.1 = (bf16[1,128,256]{2,1,0:T(8,128)(2,1)S(1)}, bf16[1,128,256]{2,1,0:T(8,128)(2,1)S(1)}, u32[]{:S(2)}, u32[]{:S(2)}) collective-permute-start(bf16[1,128,256]{2,1,0:T(8,128)(2,1)S(1)} %get-tuple-element.52), channel_id=1, source_target_pairs={{0,480},{32,0},{64,32},{96,64},{128,96},{160,128},{192,160},{224,1... | collective-permute-start | bytes 196616 | tf_op jit(solution)/shard_map/ppermute | solution.py:15
Sparse Core Ops, SparseCore 0:
  11.0 90.6 all-gather.7
  104.8 80.7 all-gather.9
  188.4 46.0 all-gather.5
  241.1 213.7 reduce-scatter.4
  459.8 219.9 reduce-scatter.2
  682.5 119.5 all-reduce.1
where the time goes:
time: 813 us; the launch traced here: 812 us
  waiting for transfers between devices  761 us (94%)
  matrix products  16.1 us (2%)
  between operations  14.3 us (2%)
  local copies, waits for them, and re-layouts  12.4 us (2%)
    reduce_scatter x1, waiting for transfers between devices, per_device(): lax.psum_scatter(lax.dot_general(piece, mixed_flat, (((1,), (1,)), ((), (...  225 us
    reduce_scatter x1, waiting for transfers between devices, per_device(): lax.psum_scatter(lax.dot_general(piece, grad_flat, (((1,), (1,)), ((), ()...  205 us
    psum x1, waiting for transfers between devices, per_device(): lax.psum(contrib.astype(jnp.bfloat16), 'segment').astype(jnp.float32)  115 us
    all_gather x1, waiting for transfers between devices, per_device(): lax.all_gather(local_rows, 'mp', axis=2, tiled=True)  89.2 us
    all_gather x1, waiting for transfers between devices, per_device(): lax.all_gather(local_carry, 'mp', axis=1, tiled=True)  79.5 us
    all_gather x1, waiting for transfers between devices, per_device(): collected = lax.all_gather(encoded, 'segment', axis=0, tiled=True)  45.9 us
  transfers between devices with their start and end apart: 8, of which 6 were waited for; matrix products, arithmetic and copies ran while one was open for 3% of the time, Pallas kernels for 0%

commit v1 on v0

--- a/solution.py
+++ b/solution.py
@@ -33,6 +33,22 @@
     ).astype(jnp.bfloat16)
     grad_keys = jnp.einsum("cqk,cqd->ckd", d_scores, queries.astype(jnp.float32)) * score_scale
     return (grad_queries, grad_keys, grad_values)
+
+
+def head_sum(term, axis):
+    devices = lax.axis_size(axis)
+    parts = term.astype(jnp.bfloat16).reshape(devices, term.shape[0] // devices, term.shape[1])
+    moved = lax.all_to_all(parts, axis, 0, 0, tiled=True)
+    return jnp.sum(moved.astype(jnp.float32), axis=0).T
+
+
+def segment_sum(contrib, axis):
+    devices = lax.axis_size(axis)
+    parts = contrib.reshape(devices, contrib.shape[0] // devices, contrib.shape[1])
+    moved = lax.all_to_all(parts, axis, 0, 0, tiled=True)
+    summed = jnp.sum(moved.astype(jnp.float32), axis=0).astype(jnp.bfloat16)
+    spread = jnp.broadcast_to(summed[None], (devices,) + summed.shape)
+    return lax.all_to_all(spread, axis, 0, 0, tiled=True).reshape(contrib.shape)
 
 
 def per_device(rows, carry, weights, neighbours):
@@ -90,17 +106,9 @@
     ).astype(jnp.bfloat16)
     mixed_flat = mixed.reshape(tokens, head)
     piece = w_out
-    out_sum = (
-        lax.psum_scatter(
-            lax.dot_general(
-                piece, mixed_flat, (((1,), (1,)), ((), ())), preferred_element_type=jnp.float32
-            ).astype(jnp.bfloat16),
-            "mp",
-            scatter_dimension=0,
-            tiled=True,
-        )
-        .astype(jnp.float32)
-        .T
+    out_sum = head_sum(
+        lax.dot_general(piece, mixed_flat, (((1,), (1,)), ((), ())), preferred_element_type=jnp.float32),
+        "mp",
     )
     forward_rows = (local_rows[0].astype(jnp.float32) + out_sum).astype(jnp.bfloat16)
     forward_rows = jnp.where(is_encoder, local_carry, forward_rows)
@@ -117,17 +125,9 @@
     )
     grad_flat = grad_queries.reshape(tokens, head)
     piece = w_query
-    grad_input = (
-        lax.psum_scatter(
-            lax.dot_general(
-                piece, grad_flat, (((1,), (1,)), ((), ())), preferred_element_type=jnp.float32
-            ).astype(jnp.bfloat16),
-            "mp",
-            scatter_dimension=0,
-            tiled=True,
-        )
-        .astype(jnp.float32)
-        .T
+    grad_input = head_sum(
+        lax.dot_general(piece, grad_flat, (((1,), (1,)), ((), ())), preferred_element_type=jnp.float32),
+        "mp",
     )
     back = local_carry.astype(jnp.float32) + grad_input
     back_rows = jnp.where(is_encoder, local_carry, back.astype(jnp.bfloat16))
@@ -140,8 +140,8 @@
     )
     contrib = jnp.einsum("cbp,cbrf->prf", onehot, grad_keyval)
     contrib = jnp.where(is_encoder, jnp.zeros_like(contrib), contrib)
-    pooled = lax.psum(contrib.astype(jnp.bfloat16), "segment").astype(jnp.float32)
-    kv_grad = pooled.reshape(pool_blocks * NBLEN, 2, head).astype(jnp.bfloat16)
+    pooled = segment_sum(contrib.astype(jnp.bfloat16).reshape(pool_blocks * NBLEN, 2 * head), "segment")
+    kv_grad = pooled.reshape(pool_blocks * NBLEN, 2, head)
     return (passed, returned, kv_grad)
 
 

time: 813 us -> 409 us (0.50)
  waiting for transfers between devices: 761 us -> 336 us
  starting transfers between devices: 7.19 us -> 26.6 us
    reduce_scatter x2 -> x0, waiting for transfers between devices: 430 us -> none  [the longest x1 225 us: per_device(): lax.psum_scatter(lax.dot_general(piece, mixed_flat, (((1,), (1,)), ((), (...]
    all_to_all x0 -> x4, waiting for transfers between devices: none -> 120 us  [the longest x2 93.8 us: head_sum(): moved = lax.all_to_all(parts, axis, 0, 0, tiled=True)]
    psum x1 -> x0, waiting for transfers between devices: 115 us -> none  [per_device(): lax.psum(contrib.astype(jnp.bfloat16), 'segment').astype(jnp.float32)]
    all_to_all x0 -> x4, starting transfers between devices: none -> 24.9 us  [the longest x2 14.4 us: head_sum(): moved = lax.all_to_all(parts, axis, 0, 0, tiled=True)]
  transfers between devices with their start and end apart: 8 -> 9, of which waited for: 6 -> 7; matrix products, arithmetic and copies ran while one was open for 3% -> 6% of each run, Pallas kernels for 0% -> 0%
where the time goes in v1:
time: 409 us; the launch traced here: 408 us
  waiting for transfers between devices  336 us (82%)
  starting transfers between devices  26.6 us (7%)
  local copies, waits for them, and re-layouts  14.6 us (4%)
  between operations  14 us (3%)
  matrix products  13.5 us (3%)
    all_to_all x2, waiting for transfers between devices, head_sum(): moved = lax.all_to_all(parts, axis, 0, 0, tiled=True)  93.8 us
    all_gather x1, waiting for transfers between devices, per_device(): lax.all_gather(local_rows, 'mp', axis=2, tiled=True)  89.2 us
    all_gather x1, waiting for transfers between devices, per_device(): lax.all_gather(local_carry, 'mp', axis=1, tiled=True)  79.5 us
    all_gather x1, waiting for transfers between devices, per_device(): collected = lax.all_gather(encoded, 'segment', axis=0, tiled=True)  45.9 us
    all_to_all x2, starting transfers between devices, head_sum(): moved = lax.all_to_all(parts, axis, 0, 0, tiled=True)  14.4 us
    all_to_all x1, waiting for transfers between devices, segment_sum(): return lax.all_to_all(spread, axis, 0, 0, tiled=True).reshape(contrib.shape)  13.4 us
    all_to_all x1, waiting for transfers between devices, segment_sum(): moved = lax.all_to_all(parts, axis, 0, 0, tiled=True)  13.1 us
  transfers between devices with their start and end apart: 9, of which 7 were waited for; matrix products, arithmetic and copies ran while one was open for 6% of the time, Pallas kernels for 0%

profile of v1, /device:TPU:1, one launch (start us, length us, event | category | flops | bytes accessed | tf_op | source)
XLA Modules:
  0.0 407.9 jit_solution(1906226420023038693)
XLA Ops:
  7.2 0.7 all-gather.8.cloned.1.call-update
  7.9 0.7 all-gather.10.cloned.1.call-update
  8.7 3.8 slice_bitcast_fusion
  12.5 89.2 %all-gather.8.cloned.1.call-done = bf16[1,2,128,8192]{3,2,1,0:T(8,128)(2,1)} async-done(((bf16[1,2,128,256]{3,2,1,0:T(8,128)(2,1)}), bf16[1,2,128,8192]{3,2,1,0:T(8,128)(2,1)}) %all-gather.8.cloned.1.call-update) | async-done | bytes 4194320 | tf_op jit(solution)/shard_map/all_gather | solution.py:62
  101.8 3.5 conditional.1
  101.8 3.4 convolution_convert_fusion
  105.3 0.6 copy-done.1
  106.2 79.5 %all-gather.10.cloned.1.call-done = bf16[1,128,8192]{2,1,0:T(8,128)(2,1)} async-done(((bf16[1,128,256]{2,1,0:T(8,128)(2,1)}), bf16[1,128,8192]{2,1,0:T(8,128)(2,1)}) %all-gather.10.cloned.1.call-update) | async-done | bytes 2097168 | tf_op jit(solution)/shard_map/all_gather | solution.py:63
  185.7 2.9 fusion.11
  188.6 45.9 %all-gather.6.cloned.1.call-done = bf16[4096,256]{1,0:T(8,128)(2,1)} async-done(((bf16[256,256]{1,0:T(8,128)(2,1)}), bf16[4096,256]{1,0:T(8,128)(2,1)}) %all-gather.6.cloned.1.call-update) | async-done | bytes 2097168 | tf_op jit(solution)/shard_map/all_gather | solution.py:91
  234.5 1.1 slice.67
  235.6 0.6 gather_fusion.1
  238.8 0.9 copy.19
  239.7 4.4 %all-to-all-start.2 = ((bf16[16,64,256]{2,1,0:T(8,128)(2,1)}), bf16[16,64,256]{2,1,0:T(8,128)(2,1)S(1)}, u32[]{:S(2)}, u32[]{:S(2)}) async-start(bf16[16,64,256]{2,1,0:T(8,128)(2,1)} %bitcast.28), calls=%async_computation.2 | async-start | bytes 1048576 | tf_op jit(solution)/shard_map/all_to_all | solution.py:48
  244.5 2.3 convolution_convert_fusion.3
  246.8 1.6 copy.25
  248.4 13.1 %all-to-all-done.2 = bf16[16,64,256]{2,1,0:T(8,128)(2,1)S(1)} async-done(((bf16[16,64,256]{2,1,0:T(8,128)(2,1)}), bf16[16,64,256]{2,1,0:T(8,128)(2,1)S(1)}, u32[]{:S(2)}, u32[]{:S(2)}) %all-to-all-start.2) | async-done | bytes 524320 | tf_op jit(solution)/shard_map/all_to_all | solution.py:48
  261.5 9.3 %all-to-all-start.1 = ((bf16[32,256,128]{1,2,0:T(8,128)(2,1)}), bf16[32,256,128]{1,2,0:T(8,128)(2,1)S(1)}, u32[]{:S(2)}, u32[]{:S(2)}) async-start(bf16[32,256,128]{1,2,0:T(8,128)(2,1)} %bitcast.105), calls=%async_computation.1 | async-start | bytes 4194304 | tf_op jit(solution)/shard_map/all_to_all | solution.py:41
  270.8 0.6 gather_fusion
  272.1 2.3 convolution_convert_fusion.4
  274.4 1.6 copy.26
  276.0 45.4 %all-to-all-done.1 = bf16[32,256,128]{1,2,0:T(8,128)(2,1)S(1)} async-done(((bf16[32,256,128]{1,2,0:T(8,128)(2,1)}), bf16[32,256,128]{1,2,0:T(8,128)(2,1)S(1)}, u32[]{:S(2)}, u32[]{:S(2)}) %all-to-all-start.1) | async-done | bytes 2097184 | tf_op jit(solution)/shard_map/all_to_all | solution.py:41
  321.4 5.1 %all-to-all-start = ((bf16[32,256,128]{1,2,0:T(8,128)(2,1)}), bf16[32,256,128]{1,2,0:T(8,128)(2,1)}, u32[]{:S(2)}, u32[]{:S(2)}) async-start(bf16[32,256,128]{1,2,0:T(8,128)(2,1)} %bitcast.106), calls=%async_computation | async-start | bytes 4194304 | tf_op jit(solution)/shard_map/all_to_all | solution.py:41
  326.7 48.3 %all-to-all-done = bf16[32,256,128]{1,2,0:T(8,128)(2,1)} async-done(((bf16[32,256,128]{1,2,0:T(8,128)(2,1)}), bf16[32,256,128]{1,2,0:T(8,128)(2,1)}, u32[]{:S(2)}, u32[]{:S(2)}) %all-to-all-start) | async-done | bytes 2097184 | tf_op jit(solution)/shard_map/all_to_all | solution.py:41
  375.0 0.8 broadcast_in_dim.11
  375.9 6.0 %all-to-all-start.3 = ((bf16[16,64,256]{2,1,0:T(8,128)(2,1)}), bf16[16,64,256]{2,1,0:T(8,128)(2,1)S(1)}, u32[]{:S(2)}, u32[]{:S(2)}) async-start(bf16[16,64,256]{2,1,0:T(8,128)(2,1)} %broadcast_in_dim.11), calls=%async_computation.3 | async-start | bytes 1048576 | tf_op jit(solution)/shard_map/all_to_all | solution.py:51
  382.2 1.9 convert_reduce_fusion.1
  384.1 1.7 collective-permute-start
  385.8 13.4 %all-to-all-done.3 = bf16[16,64,256]{2,1,0:T(8,128)(2,1)S(1)} async-done(((bf16[16,64,256]{2,1,0:T(8,128)(2,1)}), bf16[16,64,256]{2,1,0:T(8,128)(2,1)S(1)}, u32[]{:S(2)}, u32[]{:S(2)}) %all-to-all-start.3) | async-done | bytes 524320 | tf_op jit(solution)/shard_map/all_to_all | solution.py:51
  399.2 0.9 reshape_reshape.7
  400.2 0.6 copy.35
  400.8 0.6 copy.36
  (39 shorter events, 4.5 us)
Async XLA Ops:
  7.2 94.6 %all-gather.8.cloned.1.call-start = ((), (), s32[]{:S(2)}) async-start(), calls=%async_computation.5 | async-start | bytes 4325376 | tf_op jit(solution)/shard_map/all_gather | solution.py:62
  7.9 177.8 %all-gather.10.cloned.1.call-start = ((), (), s32[]{:S(2)}) async-start(), calls=%async_computation.6 | async-start | bytes 2162688 | tf_op jit(solution)/shard_map/all_gather | solution.py:63
  8.6 225.9 %all-gather.6.cloned.1.call-start = ((), (), s32[]{:S(2)}) async-start(), calls=%async_computation.4 | async-start | bytes 2228224 | tf_op jit(solution)/shard_map/all_gather | solution.py:91
  101.8 4.2 %copy-start.4 = (s32[1,2,2,2]{3,2,1,0:T(2,128)S(1)}, s32[1,2,2,2]{3,2,1,0:T(2,128)}, u32[]{:S(2)}) copy-start(s32[1,2,2,2]{3,2,1,0:T(2,128)} %param.9) | copy-start | bytes 100
  105.3 0.7 copy-start.1
  239.7 21.7 %all-to-all-start.2 = ((bf16[16,64,256]{2,1,0:T(8,128)(2,1)}), bf16[16,64,256]{2,1,0:T(8,128)(2,1)S(1)}, u32[]{:S(2)}, u32[]{:S(2)}) async-start(bf16[16,64,256]{2,1,0:T(8,128)(2,1)} %bitcast.28), calls=%async_computation.2 | async-start | bytes 1048576 | tf_op jit(solution)/shard_map/all_to_all | solution.py:48
  261.5 60.0 %all-to-all-start.1 = ((bf16[32,256,128]{1,2,0:T(8,128)(2,1)}), bf16[32,256,128]{1,2,0:T(8,128)(2,1)S(1)}, u32[]{:S(2)}, u32[]{:S(2)}) async-start(bf16[32,256,128]{1,2,0:T(8,128)(2,1)} %bitcast.105), calls=%async_computation.1 | async-start | bytes 4194304 | tf_op jit(solution)/shard_map/all_to_all | solution.py:41
  321.4 53.6 %all-to-all-start = ((bf16[32,256,128]{1,2,0:T(8,128)(2,1)}), bf16[32,256,128]{1,2,0:T(8,128)(2,1)}, u32[]{:S(2)}, u32[]{:S(2)}) async-start(bf16[32,256,128]{1,2,0:T(8,128)(2,1)} %bitcast.106), calls=%async_computation | async-start | bytes 4194304 | tf_op jit(solution)/shard_map/all_to_all | solution.py:41
  375.9 23.4 %all-to-all-start.3 = ((bf16[16,64,256]{2,1,0:T(8,128)(2,1)}), bf16[16,64,256]{2,1,0:T(8,128)(2,1)S(1)}, u32[]{:S(2)}, u32[]{:S(2)}) async-start(bf16[16,64,256]{2,1,0:T(8,128)(2,1)} %broadcast_in_dim.11), calls=%async_computation.3 | async-start | bytes 1048576 | tf_op jit(solution)/shard_map/all_to_all | solution.py:51
  381.9 2.2 copy-start.2
  381.9 2.2 copy-start.3
  384.1 16.0 %collective-permute-start = (bf16[1,128,256]{2,1,0:T(8,128)(2,1)S(1)}, bf16[1,128,256]{2,1,0:T(8,128)(2,1)S(1)}, u32[]{:S(2)}, u32[]{:S(2)}) collective-permute-start(bf16[1,128,256]{2,1,0:T(8,128)(2,1)S(1)} %get-tuple-element.53), channel_id=1, source_target_pairs={{0,32},{32,64},{64,96},{96,128},{128,160},{160,192},{192,224},{224... | collective-permute-start | bytes 196616 | tf_op jit(solution)/shard_map/ppermute | solution.py:15
  385.8 14.4 %collective-permute-start.1 = (bf16[1,128,256]{2,1,0:T(8,128)(2,1)S(1)}, bf16[1,128,256]{2,1,0:T(8,128)(2,1)S(1)}, u32[]{:S(2)}, u32[]{:S(2)}) collective-permute-start(bf16[1,128,256]{2,1,0:T(8,128)(2,1)S(1)} %get-tuple-element.52), channel_id=1, source_target_pairs={{0,480},{32,0},{64,32},{96,64},{128,96},{160,128},{192,160},{224,1... | collective-permute-start | bytes 196616 | tf_op jit(solution)/shard_map/ppermute | solution.py:15
Sparse Core Ops, SparseCore 0:
  11.0 90.6 all-gather.7
  104.8 80.8 all-gather.9
  188.4 46.0 all-gather.5

commit v2 on v1

--- a/solution.py
+++ b/solution.py
@@ -58,10 +58,10 @@
     is_encoder = lax.axis_index("segment") >= first_encoder
     local_rows = rows[0]
     local_carry = carry[0]
-    full_rows, full_carry = (
-        lax.all_gather(local_rows, "mp", axis=2, tiled=True),
-        lax.all_gather(local_carry, "mp", axis=1, tiled=True),
+    gathered = lax.all_gather(
+        jnp.concatenate([local_rows, local_carry[None]], axis=0), "mp", axis=2, tiled=True
     )
+    full_rows, full_carry = gathered[:2], gathered[2]
     tokens = local_rows.shape[1]
     width = full_rows.shape[2]
     head = weights.shape[3]

time: 409 us -> 338 us (0.83)
  waiting for transfers between devices: 336 us -> 263 us
    all_gather x2 -> x1, waiting for transfers between devices: 169 us -> 99.5 us  [per_device(): lax.all_gather(jnp.concatenate([local_rows, local_carry[None]], axis=0),...]
  transfers between devices with their start and end apart: 9 -> 8, of which waited for: 7 -> 6; matrix products, arithmetic and copies ran while one was open for 6% -> 6% of each run, Pallas kernels for 0% -> 0%
where the time goes in v2:
time: 338 us; the launch traced here: 337 us
  waiting for transfers between devices  263 us (78%)
  starting transfers between devices  26.7 us (8%)
  local copies, waits for them, and re-layouts  17.5 us (5%)
  between operations  14.2 us (4%)
  matrix products  11.3 us (3%)
  other arithmetic  4.51 us (1%)
    all_gather x1, waiting for transfers between devices, per_device(): lax.all_gather(jnp.concatenate([local_rows, local_carry[None]], axis=0),...  99.5 us
    all_to_all x2, waiting for transfers between devices, head_sum(): moved = lax.all_to_all(parts, axis, 0, 0, tiled=True)  93.8 us
    all_gather x1, waiting for transfers between devices, per_device(): collected = lax.all_gather(encoded, 'segment', axis=0, tiled=True)  43.4 us
    all_to_all x2, starting transfers between devices, head_sum(): moved = lax.all_to_all(parts, axis, 0, 0, tiled=True)  14.4 us
    all_to_all x1, waiting for transfers between devices, segment_sum(): return lax.all_to_all(spread, axis, 0, 0, tiled=True).reshape(contrib.shape)  13.3 us
    all_to_all x1, waiting for transfers between devices, segment_sum(): moved = lax.all_to_all(parts, axis, 0, 0, tiled=True)  13.1 us
  transfers between devices with their start and end apart: 8, of which 6 were waited for; matrix products, arithmetic and copies ran while one was open for 6% of the time, Pallas kernels for 0%

profile of v2, /device:TPU:1, one launch (start us, length us, event | category | flops | bytes accessed | tf_op | source)
XLA Modules:
  0.0 337.4 jit_solution(13399274811268162969)
XLA Ops:
  7.2 1.6 pad_maximum_fusion.2
  8.9 3.8 %slice_bitcast_fusion.2 = (bf16[8192,128]{1,0:T(8,128)(2,1)}, bf16[8192,128]{1,0:T(8,128)(2,1)S(1)}) fusion(bf16[1,2,8192,128]{3,2,1,0:T(8,128)(2,1)} %param.8), kind=kLoop, calls=%fused_computation.16 | loop fusion | bytes 8388608 | tf_op jit(solution)/shard_map/squeeze | solution.py:69
  12.8 99.5 %all-gather.3.cloned.1.call-done = bf16[3,128,8192]{2,1,0:T(8,128)(2,1)} async-done(((bf16[3,128,256]{2,1,0:T(8,128)(2,1)}), bf16[3,128,8192]{2,1,0:T(8,128)(2,1)}) %all-gather.3.cloned.1.call-update) | async-done | bytes 6291472 | tf_op jit(solution)/shard_map/all_gather | solution.py:61
  112.3 2.2 slice-done
  114.4 0.7 copy-done
  115.1 1.3 conditional.1
  115.1 1.3 convolution_convert_fusion
  116.5 0.6 copy-done.1
  117.3 2.9 fusion.10
  120.3 43.4 %all-gather.5.cloned.1.call-done = bf16[4096,256]{1,0:T(8,128)(2,1)} async-done(((bf16[256,256]{1,0:T(8,128)(2,1)}), bf16[4096,256]{1,0:T(8,128)(2,1)}) %all-gather.5.cloned.1.call-update) | async-done | bytes 2097168 | tf_op jit(solution)/shard_map/all_gather | solution.py:91
  163.6 1.1 slice.76
  164.7 0.6 gather_fusion.1
  167.9 0.9 copy.19
  168.8 4.4 %all-to-all-start.2 = ((bf16[16,64,256]{2,1,0:T(8,128)(2,1)}), bf16[16,64,256]{2,1,0:T(8,128)(2,1)S(1)}, u32[]{:S(2)}, u32[]{:S(2)}) async-start(bf16[16,64,256]{2,1,0:T(8,128)(2,1)} %bitcast.28), calls=%async_computation.2 | async-start | bytes 1048576 | tf_op jit(solution)/shard_map/all_to_all | solution.py:48
  173.6 2.3 convolution_convert_fusion.3
  175.9 1.6 copy.25
  177.5 13.1 %all-to-all-done.2 = bf16[16,64,256]{2,1,0:T(8,128)(2,1)S(1)} async-done(((bf16[16,64,256]{2,1,0:T(8,128)(2,1)}), bf16[16,64,256]{2,1,0:T(8,128)(2,1)S(1)}, u32[]{:S(2)}, u32[]{:S(2)}) %all-to-all-start.2) | async-done | bytes 524320 | tf_op jit(solution)/shard_map/all_to_all | solution.py:48
  190.6 9.3 %all-to-all-start.1 = ((bf16[32,256,128]{1,2,0:T(8,128)(2,1)}), bf16[32,256,128]{1,2,0:T(8,128)(2,1)S(1)}, u32[]{:S(2)}, u32[]{:S(2)}) async-start(bf16[32,256,128]{1,2,0:T(8,128)(2,1)} %bitcast.103), calls=%async_computation.1 | async-start | bytes 4194304 | tf_op jit(solution)/shard_map/all_to_all | solution.py:41
  199.9 0.6 gather_fusion
  201.2 2.3 convolution_convert_fusion.4
  203.5 1.6 copy.26
  205.1 45.4 %all-to-all-done.1 = bf16[32,256,128]{1,2,0:T(8,128)(2,1)S(1)} async-done(((bf16[32,256,128]{1,2,0:T(8,128)(2,1)}), bf16[32,256,128]{1,2,0:T(8,128)(2,1)S(1)}, u32[]{:S(2)}, u32[]{:S(2)}) %all-to-all-start.1) | async-done | bytes 2097184 | tf_op jit(solution)/shard_map/all_to_all | solution.py:41
  250.5 5.1 %all-to-all-start = ((bf16[32,256,128]{1,2,0:T(8,128)(2,1)}), bf16[32,256,128]{1,2,0:T(8,128)(2,1)}, u32[]{:S(2)}, u32[]{:S(2)}) async-start(bf16[32,256,128]{1,2,0:T(8,128)(2,1)} %bitcast.104), calls=%async_computation | async-start | bytes 4194304 | tf_op jit(solution)/shard_map/all_to_all | solution.py:41
  255.8 48.3 %all-to-all-done = bf16[32,256,128]{1,2,0:T(8,128)(2,1)} async-done(((bf16[32,256,128]{1,2,0:T(8,128)(2,1)}), bf16[32,256,128]{1,2,0:T(8,128)(2,1)}, u32[]{:S(2)}, u32[]{:S(2)}) %all-to-all-start) | async-done | bytes 2097184 | tf_op jit(solution)/shard_map/all_to_all | solution.py:41
  304.1 0.8 broadcast_in_dim.11
  305.0 6.0 %all-to-all-start.3 = ((bf16[16,64,256]{2,1,0:T(8,128)(2,1)}), bf16[16,64,256]{2,1,0:T(8,128)(2,1)S(1)}, u32[]{:S(2)}, u32[]{:S(2)}) async-start(bf16[16,64,256]{2,1,0:T(8,128)(2,1)} %broadcast_in_dim.11), calls=%async_computation.3 | async-start | bytes 1048576 | tf_op jit(solution)/shard_map/all_to_all | solution.py:51
  311.3 1.9 convert_reduce_fusion.1
  313.5 1.5 collective-permute-start
  315.0 13.3 %all-to-all-done.3 = bf16[16,64,256]{2,1,0:T(8,128)(2,1)S(1)} async-done(((bf16[16,64,256]{2,1,0:T(8,128)(2,1)}), bf16[16,64,256]{2,1,0:T(8,128)(2,1)S(1)}, u32[]{:S(2)}, u32[]{:S(2)}) %all-to-all-start.3) | async-done | bytes 524320 | tf_op jit(solution)/shard_map/all_to_all | solution.py:51
  328.3 0.9 reshape_reshape.7
  329.3 0.6 copy.35
  329.9 0.6 copy.36
  (41 shorter events, 4.7 us)
Async XLA Ops:
  7.2 105.1 %all-gather.3.cloned.1.call-start = ((), (), s32[]{:S(2)}) async-start(), calls=%async_computation.4 | async-start | bytes 6488064 | tf_op jit(solution)/shard_map/all_gather | solution.py:61
  8.9 154.8 %all-gather.5.cloned.1.call-start = ((), (), s32[]{:S(2)}) async-start(), calls=%async_computation.5 | async-start | bytes 2228224 | tf_op jit(solution)/shard_map/all_gather | solution.py:91
  112.3 2.2 slice-start
  112.3 2.9 copy-start
  115.1 2.0 copy-start.4
  116.4 0.7 copy-start.1
  168.8 21.7 %all-to-all-start.2 = ((bf16[16,64,256]{2,1,0:T(8,128)(2,1)}), bf16[16,64,256]{2,1,0:T(8,128)(2,1)S(1)}, u32[]{:S(2)}, u32[]{:S(2)}) async-start(bf16[16,64,256]{2,1,0:T(8,128)(2,1)} %bitcast.28), calls=%async_computation.2 | async-start | bytes 1048576 | tf_op jit(solution)/shard_map/all_to_all | solution.py:48
  190.6 60.0 %all-to-all-start.1 = ((bf16[32,256,128]{1,2,0:T(8,128)(2,1)}), bf16[32,256,128]{1,2,0:T(8,128)(2,1)S(1)}, u32[]{:S(2)}, u32[]{:S(2)}) async-start(bf16[32,256,128]{1,2,0:T(8,128)(2,1)} %bitcast.103), calls=%async_computation.1 | async-start | bytes 4194304 | tf_op jit(solution)/shard_map/all_to_all | solution.py:41
  250.5 53.6 %all-to-all-start = ((bf16[32,256,128]{1,2,0:T(8,128)(2,1)}), bf16[32,256,128]{1,2,0:T(8,128)(2,1)}, u32[]{:S(2)}, u32[]{:S(2)}) async-start(bf16[32,256,128]{1,2,0:T(8,128)(2,1)} %bitcast.104), calls=%async_computation | async-start | bytes 4194304 | tf_op jit(solution)/shard_map/all_to_all | solution.py:41
  305.0 23.4 %all-to-all-start.3 = ((bf16[16,64,256]{2,1,0:T(8,128)(2,1)}), bf16[16,64,256]{2,1,0:T(8,128)(2,1)S(1)}, u32[]{:S(2)}, u32[]{:S(2)}) async-start(bf16[16,64,256]{2,1,0:T(8,128)(2,1)} %broadcast_in_dim.11), calls=%async_computation.3 | async-start | bytes 1048576 | tf_op jit(solution)/shard_map/all_to_all | solution.py:51
  311.0 2.2 copy-start.2
  311.0 2.2 copy-start.3
  313.3 16.0 %collective-permute-start.1 = (bf16[1,128,256]{2,1,0:T(8,128)(2,1)S(1)}, bf16[1,128,256]{2,1,0:T(8,128)(2,1)S(1)}, u32[]{:S(2)}, u32[]{:S(2)}) collective-permute-start(bf16[1,128,256]{2,1,0:T(8,128)(2,1)S(1)} %get-tuple-element.52), channel_id=1, source_target_pairs={{0,480},{32,0},{64,32},{96,64},{128,96},{160,128},{192,160},{224,1... | collective-permute-start | bytes 196616 | tf_op jit(solution)/shard_map/ppermute | solution.py:15
  313.5 15.8 %collective-permute-start = (bf16[1,128,256]{2,1,0:T(8,128)(2,1)S(1)}, bf16[1,128,256]{2,1,0:T(8,128)(2,1)S(1)}, u32[]{:S(2)}, u32[]{:S(2)}) collective-permute-start(bf16[1,128,256]{2,1,0:T(8,128)(2,1)S(1)} %get-tuple-element.53), channel_id=1, source_target_pairs={{0,32},{32,64},{64,96},{96,128},{128,160},{160,192},{192,224},{224... | collective-permute-start | bytes 196616 | tf_op jit(solution)/shard_map/ppermute | solution.py:15
Sparse Core Ops, SparseCore 0:
  11.6 100.5 all-gather.2
  117.3 46.3 all-gather.4

commit v3 on v2

--- a/solution.py
+++ b/solution.py
@@ -35,11 +35,9 @@
     return (grad_queries, grad_keys, grad_values)
 
 
-def head_sum(term, axis):
-    devices = lax.axis_size(axis)
-    parts = term.astype(jnp.bfloat16).reshape(devices, term.shape[0] // devices, term.shape[1])
-    moved = lax.all_to_all(parts, axis, 0, 0, tiled=True)
-    return jnp.sum(moved.astype(jnp.float32), axis=0).T
+def head_sum(vectors, matrix):
+    terms = jnp.einsum("htd,hfd->htf", vectors, matrix, preferred_element_type=jnp.float32)
+    return jnp.sum(terms.astype(jnp.bfloat16).astype(jnp.float32), axis=0)
 
 
 def segment_sum(contrib, axis):
@@ -67,6 +65,14 @@
     head = weights.shape[3]
     w_query = weights[0, 0]
     w_out = weights[0, 1]
+    features = width // lax.axis_size("mp")
+    w_mine = lax.all_to_all(
+        weights[0].reshape(2, lax.axis_size("mp"), features, head).transpose(1, 0, 2, 3),
+        "mp",
+        0,
+        0,
+        tiled=True,
+    )
 
     def encode():
         flat = full_rows.reshape(2 * tokens, width)
@@ -105,14 +111,6 @@
         "cqk,ckd->cqd", rounded_fwd, values_fwd, preferred_element_type=jnp.float32
     ).astype(jnp.bfloat16)
     mixed_flat = mixed.reshape(tokens, head)
-    piece = w_out
-    out_sum = head_sum(
-        lax.dot_general(piece, mixed_flat, (((1,), (1,)), ((), ())), preferred_element_type=jnp.float32),
-        "mp",
-    )
-    forward_rows = (local_rows[0].astype(jnp.float32) + out_sum).astype(jnp.bfloat16)
-    forward_rows = jnp.where(is_encoder, local_carry, forward_rows)
-    passed = from_behind(forward_rows[None], "segment", 1)
     upstream = (
         jnp.dot(full_carry, w_out, preferred_element_type=jnp.float32)
         .astype(jnp.bfloat16)
@@ -124,11 +122,16 @@
         query_blocks[1], keys_back, values_back, soft_back, rounded_back, upstream, score_scale
     )
     grad_flat = grad_queries.reshape(tokens, head)
-    piece = w_query
-    grad_input = head_sum(
-        lax.dot_general(piece, grad_flat, (((1,), (1,)), ((), ())), preferred_element_type=jnp.float32),
-        "mp",
+    heads = lax.axis_size("mp")
+    small = jnp.stack([mixed_flat, grad_flat])
+    every = lax.all_to_all(
+        jnp.broadcast_to(small[None], (heads,) + small.shape), "mp", 0, 0, tiled=True
     )
+    out_sum = head_sum(every[:, 0], w_mine[:, 1])
+    grad_input = head_sum(every[:, 1], w_mine[:, 0])
+    forward_rows = (local_rows[0].astype(jnp.float32) + out_sum).astype(jnp.bfloat16)
+    forward_rows = jnp.where(is_encoder, local_carry, forward_rows)
+    passed = from_behind(forward_rows[None], "segment", 1)
     back = local_carry.astype(jnp.float32) + grad_input
     back_rows = jnp.where(is_encoder, local_carry, back.astype(jnp.bfloat16))
     returned = from_behind(back_rows[None], "segment", -1)

time: 338 us -> 336 us (level)
  waiting for transfers between devices: 263 us -> 256 us
  local copies, waits for them, and re-layouts: 17.5 us -> 20.9 us
    all_to_all x2, waiting for transfers between devices: 93.8 us -> 50.6 us  [the longest x1 50.6 us: per_device(): lax.all_to_all(jnp.broadcast_to(small[None], (heads,) + small.shape), 'mp...]
    all_gather x1, waiting for transfers between devices: 99.5 us -> 134 us  [per_device(): lax.all_gather(jnp.concatenate([local_rows, local_carry[None]], axis=0),...]
    all_to_all x2, starting transfers between devices: 14.4 us -> 19.9 us  [the longest x1 10.6 us: per_device(): lax.all_to_all(weights[0].reshape(2, lax.axis_size('mp'), features, head)...]
    transpose x0 -> x1, local copies, waits for them, and re-layouts: none -> 4.77 us  [per_device(): weights[0].reshape(2, lax.axis_size('mp'), features, head)]
  transfers between devices with their start and end apart: 8 -> 8, of which waited for: 6 -> 5; matrix products, arithmetic and copies ran while one was open for 6% -> 8% of each run, Pallas kernels for 0% -> 0%
where the time goes in v3:
time: 336 us; the launch traced here: 335 us
  waiting for transfers between devices  256 us (76%)
  starting transfers between devices  29.6 us (9%)
  local copies, waits for them, and re-layouts  20.9 us (6%)
  between operations  14.3 us (4%)
  matrix products  11.4 us (3%)
    all_gather x1, waiting for transfers between devices, per_device(): lax.all_gather(jnp.concatenate([local_rows, local_carry[None]], axis=0),...  134 us
    all_to_all x1, waiting for transfers between devices, per_device(): lax.all_to_all(jnp.broadcast_to(small[None], (heads,) + small.shape), 'mp...  50.6 us
    all_gather x1, waiting for transfers between devices, per_device(): collected = lax.all_gather(encoded, 'segment', axis=0, tiled=True)  46.1 us
    all_to_all x1, waiting for transfers between devices, segment_sum(): moved = lax.all_to_all(parts, axis, 0, 0, tiled=True)  15.7 us
    all_to_all x1, starting transfers between devices, per_device(): lax.all_to_all(weights[0].reshape(2, lax.axis_size('mp'), features, head)...  10.6 us
    all_to_all x1, waiting for transfers between devices, segment_sum(): return lax.all_to_all(spread, axis, 0, 0, tiled=True).reshape(contrib.shape)  10.2 us
    all_to_all x1, starting transfers between devices, per_device(): lax.all_to_all(jnp.broadcast_to(small[None], (heads,) + small.shape), 'mp...  9.26 us
  transfers between devices with their start and end apart: 8, of which 5 were waited for; matrix products, arithmetic and copies ran while one was open for 8% of the time, Pallas kernels for 0%

profile of v3, /device:TPU:1, one launch (start us, length us, event | category | flops | bytes accessed | tf_op | source)
XLA Modules:
  0.0 334.9 jit_solution(12077202758018153209)
XLA Ops:
  7.2 1.6 pad_maximum_fusion.2
  8.9 4.8 %copy.24 = bf16[32,2,256,128]{3,2,1,0:T(8,128)(2,1)} copy(bf16[32,2,256,128]{3,2,0,1:T(8,128)(2,1)} %bitcast.105) | data formatting | bytes 8388608 | tf_op jit(solution)/shard_map/transpose | solution.py:70
  13.6 10.6 %all-to-all-start.1 = ((bf16[32,2,256,128]{3,2,1,0:T(8,128)(2,1)}), bf16[32,2,256,128]{3,2,1,0:T(8,128)(2,1)}, u32[]{:S(2)}, u32[]{:S(2)}) async-start(bf16[32,2,256,128]{3,2,1,0:T(8,128)(2,1)} %copy.24), calls=%async_computation.1 | async-start | bytes 8388608 | tf_op jit(solution)/shard_map/all_to_all | solution.py:69
  24.3 3.8 %slice_bitcast_fusion.6 = (bf16[8192,128]{1,0:T(8,128)(2,1)}, bf16[8192,128]{1,0:T(8,128)(2,1)S(1)}) fusion(bf16[1,2,8192,128]{3,2,1,0:T(8,128)(2,1)} %param.8), kind=kLoop, calls=%fused_computation.16 | loop fusion | bytes 8388608 | tf_op jit(solution)/shard_map/squeeze | solution.py:67
  28.2 133.7 %all-gather.3.cloned.1.call-done = bf16[3,128,8192]{2,1,0:T(8,128)(2,1)} async-done(((bf16[3,128,256]{2,1,0:T(8,128)(2,1)}), bf16[3,128,8192]{2,1,0:T(8,128)(2,1)}) %all-gather.3.cloned.1.call-update) | async-done | bytes 6291472 | tf_op jit(solution)/shard_map/all_gather | solution.py:59
  161.8 2.2 slice-done
  164.0 0.7 copy-done
  164.7 1.3 conditional.1
  164.7 1.3 convolution_convert_fusion
  166.0 0.6 copy-done.1
  167.0 2.9 fusion.12
  169.9 46.1 %all-gather.5.cloned.1.call-done = bf16[4096,256]{1,0:T(8,128)(2,1)} async-done(((bf16[256,256]{1,0:T(8,128)(2,1)}), bf16[4096,256]{1,0:T(8,128)(2,1)}) %all-gather.5.cloned.1.call-update) | async-done | bytes 2097168 | tf_op jit(solution)/shard_map/all_gather | solution.py:97
  216.0 1.1 slice.92
  217.1 0.6 gather_fusion.1
  219.3 0.5 copy.29
  219.8 0.5 fusion.6
  220.3 0.9 copy.30
  221.2 4.4 %all-to-all-start.2 = ((bf16[16,64,256]{2,1,0:T(8,128)(2,1)}), bf16[16,64,256]{2,1,0:T(8,128)(2,1)S(1)}, u32[]{:S(2)}, u32[]{:S(2)}) async-start(bf16[16,64,256]{2,1,0:T(8,128)(2,1)} %bitcast.29), calls=%async_computation.2 | async-start | bytes 1048576 | tf_op jit(solution)/shard_map/all_to_all | solution.py:46
  225.6 0.6 gather_fusion
  227.2 15.7 %all-to-all-done.2 = bf16[16,64,256]{2,1,0:T(8,128)(2,1)S(1)} async-done(((bf16[16,64,256]{2,1,0:T(8,128)(2,1)}), bf16[16,64,256]{2,1,0:T(8,128)(2,1)S(1)}, u32[]{:S(2)}, u32[]{:S(2)}) %all-to-all-start.2) | async-done | bytes 524320 | tf_op jit(solution)/shard_map/all_to_all | solution.py:46
  242.9 1.9 broadcast_in_dim.6
  244.8 9.3 %all-to-all-start = ((bf16[32,2,128,128]{3,2,1,0:T(8,128)(2,1)}), bf16[32,2,128,128]{3,2,1,0:T(8,128)(2,1)S(1)}, u32[]{:S(2)}, u32[]{:S(2)}) async-start(bf16[32,2,128,128]{3,2,1,0:T(8,128)(2,1)} %broadcast_in_dim.6), calls=%async_computation | async-start | bytes 4194304 | tf_op jit(solution)/shard_map/all_to_all | solution.py:127
  254.1 50.6 %all-to-all-done = bf16[32,2,128,128]{3,2,1,0:T(8,128)(2,1)S(1)} async-done(((bf16[32,2,128,128]{3,2,1,0:T(8,128)(2,1)}), bf16[32,2,128,128]{3,2,1,0:T(8,128)(2,1)S(1)}, u32[]{:S(2)}, u32[]{:S(2)}) %all-to-all-start) | async-done | bytes 2097184 | tf_op jit(solution)/shard_map/all_to_all | solution.py:127
  304.8 0.8 broadcast_in_dim.8
  305.6 3.5 %all-to-all-start.3 = ((bf16[16,64,256]{2,1,0:T(8,128)(2,1)}), bf16[16,64,256]{2,1,0:T(8,128)(2,1)S(1)}, u32[]{:S(2)}, u32[]{:S(2)}) async-start(bf16[16,64,256]{2,1,0:T(8,128)(2,1)} %broadcast_in_dim.8), calls=%async_computation.3 | async-start | bytes 1048576 | tf_op jit(solution)/shard_map/all_to_all | solution.py:49
  309.1 2.3 convert_reduce_fusion.1
  311.4 2.4 convert_reduce_fusion
  313.9 1.7 collective-permute-start
  315.6 10.2 %all-to-all-done.3 = bf16[16,64,256]{2,1,0:T(8,128)(2,1)S(1)} async-done(((bf16[16,64,256]{2,1,0:T(8,128)(2,1)}), bf16[16,64,256]{2,1,0:T(8,128)(2,1)S(1)}, u32[]{:S(2)}, u32[]{:S(2)}) %all-to-all-start.3) | async-done | bytes 524320 | tf_op jit(solution)/shard_map/all_to_all | solution.py:49
  325.9 0.9 reshape_reshape.7
  326.8 0.6 copy.44
  327.4 0.6 copy.45
  (40 shorter events, 3.2 us)
Async XLA Ops:
  7.2 154.7 %all-gather.3.cloned.1.call-start = ((), (), s32[]{:S(2)}) async-start(), calls=%async_computation.4 | async-start | bytes 6488064 | tf_op jit(solution)/shard_map/all_gather | solution.py:59
  13.6 207.5 %all-to-all-start.1 = ((bf16[32,2,256,128]{3,2,1,0:T(8,128)(2,1)}), bf16[32,2,256,128]{3,2,1,0:T(8,128)(2,1)}, u32[]{:S(2)}, u32[]{:S(2)}) async-start(bf16[32,2,256,128]{3,2,1,0:T(8,128)(2,1)} %copy.24), calls=%async_computation.1 | async-start | bytes 8388608 | tf_op jit(solution)/shard_map/all_to_all | solution.py:69
  24.3 191.7 %all-gather.5.cloned.1.call-start = ((), (), s32[]{:S(2)}) async-start(), calls=%async_computation.5 | async-start | bytes 2228224 | tf_op jit(solution)/shard_map/all_gather | solution.py:97
  161.8 2.2 slice-start
  161.8 2.9 copy-start
  164.7 2.0 copy-start.4
  166.0 0.7 copy-start.1
  221.2 21.7 %all-to-all-start.2 = ((bf16[16,64,256]{2,1,0:T(8,128)(2,1)}), bf16[16,64,256]{2,1,0:T(8,128)(2,1)S(1)}, u32[]{:S(2)}, u32[]{:S(2)}) async-start(bf16[16,64,256]{2,1,0:T(8,128)(2,1)} %bitcast.29), calls=%async_computation.2 | async-start | bytes 1048576 | tf_op jit(solution)/shard_map/all_to_all | solution.py:46
  244.8 60.0 %all-to-all-start = ((bf16[32,2,128,128]{3,2,1,0:T(8,128)(2,1)}), bf16[32,2,128,128]{3,2,1,0:T(8,128)(2,1)S(1)}, u32[]{:S(2)}, u32[]{:S(2)}) async-start(bf16[32,2,128,128]{3,2,1,0:T(8,128)(2,1)} %broadcast_in_dim.6), calls=%async_computation | async-start | bytes 4194304 | tf_op jit(solution)/shard_map/all_to_all | solution.py:127
  305.6 20.3 %all-to-all-start.3 = ((bf16[16,64,256]{2,1,0:T(8,128)(2,1)}), bf16[16,64,256]{2,1,0:T(8,128)(2,1)S(1)}, u32[]{:S(2)}, u32[]{:S(2)}) async-start(bf16[16,64,256]{2,1,0:T(8,128)(2,1)} %broadcast_in_dim.8), calls=%async_computation.3 | async-start | bytes 1048576 | tf_op jit(solution)/shard_map/all_to_all | solution.py:49
  311.4 2.4 copy-start.2
  311.4 2.4 copy-start.3
  313.8 12.9 %collective-permute-start.1 = (bf16[1,128,256]{2,1,0:T(8,128)(2,1)S(1)}, bf16[1,128,256]{2,1,0:T(8,128)(2,1)S(1)}, u32[]{:S(2)}, u32[]{:S(2)}) collective-permute-start(bf16[1,128,256]{2,1,0:T(8,128)(2,1)S(1)} %get-tuple-element.55), channel_id=1, source_target_pairs={{0,480},{32,0},{64,32},{96,64},{128,96},{160,128},{192,160},{224,1... | collective-permute-start | bytes 196616 | tf_op jit(solution)/shard_map/ppermute | solution.py:15
  313.9 12.9 %collective-permute-start = (bf16[1,128,256]{2,1,0:T(8,128)(2,1)S(1)}, bf16[1,128,256]{2,1,0:T(8,128)(2,1)S(1)}, u32[]{:S(2)}, u32[]{:S(2)}) collective-permute-start(bf16[1,128,256]{2,1,0:T(8,128)(2,1)S(1)} %get-tuple-element.56), channel_id=1, source_target_pairs={{0,32},{32,64},{64,96},{96,128},{128,160},{160,192},{192,224},{224... | collective-permute-start | bytes 196616 | tf_op jit(solution)/shard_map/ppermute | solution.py:15
Sparse Core Ops, SparseCore 0:
  11.6 150.1 all-gather.2
  166.8 49.1 all-gather.4

commit v4 on v2

--- a/solution.py
+++ b/solution.py
@@ -1,9 +1,12 @@
+import functools
 import math
+
+import numpy as np
 
 import jax
 import jax.numpy as jnp
 from jax import lax
-from jax.sharding import PartitionSpec as P
+from jax.sharding import Mesh, PartitionSpec as P
 
 GROUP = 64
 NBLEN = 128
@@ -51,16 +54,16 @@
     return lax.all_to_all(spread, axis, 0, 0, tiled=True).reshape(contrib.shape)
 
 
-def per_device(rows, carry, weights, neighbours):
+def per_device(mp, stages, rows, carry, weights, neighbours):
     segments = lax.axis_size("segment")
     encoders = segments // 4
     first_encoder = segments - encoders
     is_encoder = lax.axis_index("segment") >= first_encoder
     local_rows = rows[0]
     local_carry = carry[0]
-    gathered = lax.all_gather(
-        jnp.concatenate([local_rows, local_carry[None]], axis=0), "mp", axis=2, tiled=True
-    )
+    gathered = jnp.concatenate([local_rows, local_carry[None]], axis=0)
+    for stage in stages:
+        gathered = lax.all_gather(gathered, stage, axis=2, tiled=True)
     full_rows, full_carry = gathered[:2], gathered[2]
     tokens = local_rows.shape[1]
     width = full_rows.shape[2]
@@ -108,7 +111,7 @@
     piece = w_out
     out_sum = head_sum(
         lax.dot_general(piece, mixed_flat, (((1,), (1,)), ((), ())), preferred_element_type=jnp.float32),
-        "mp",
+        mp,
     )
     forward_rows = (local_rows[0].astype(jnp.float32) + out_sum).astype(jnp.bfloat16)
     forward_rows = jnp.where(is_encoder, local_carry, forward_rows)
@@ -127,7 +130,7 @@
     piece = w_query
     grad_input = head_sum(
         lax.dot_general(piece, grad_flat, (((1,), (1,)), ((), ())), preferred_element_type=jnp.float32),
-        "mp",
+        mp,
     )
     back = local_carry.astype(jnp.float32) + grad_input
     back_rows = jnp.where(is_encoder, local_carry, back.astype(jnp.bfloat16))
@@ -145,17 +148,40 @@
     return (passed, returned, kv_grad)
 
 
+def split_mp(mesh):
+    devices = mesh.devices
+    try:
+        xs = [d.coords[0] for d in devices[0]]
+        ys = [d.coords[1] for d in devices[0]]
+    except (AttributeError, TypeError, IndexError):
+        return None
+    wide = len(set(xs))
+    tall = devices.shape[1] // wide
+    if wide * tall != devices.shape[1] or wide == 1 or tall == 1:
+        return None
+    grid_x = np.array(xs).reshape(tall, wide)
+    grid_y = np.array(ys).reshape(tall, wide)
+    if not ((grid_x == grid_x[:1]).all() and (grid_y == grid_y[:, :1]).all()):
+        return None
+    return Mesh(devices.reshape(devices.shape[0], tall, wide), ("segment", "my", "mx"))
+
+
 def solution(mesh):
+    split = split_mp(mesh)
+    if split is None:
+        inner, mp, stages = mesh, "mp", ("mp",)
+    else:
+        inner, mp, stages = split, ("my", "mx"), ("mx", "my")
     placed = (
-        P("segment", None, None, "mp"),
-        P("segment", None, "mp"),
-        P("segment", None, None, "mp"),
+        P("segment", None, None, mp),
+        P("segment", None, mp),
+        P("segment", None, None, mp),
         P("segment", None, None, None),
     )
     return jax.shard_map(
-        per_device,
-        mesh=mesh,
+        functools.partial(per_device, mp, stages),
+        mesh=inner,
         in_specs=placed,
-        out_specs=(P("segment", None, "mp"), P("segment", None, "mp"), P(None, None, "mp")),
+        out_specs=(P("segment", None, mp), P("segment", None, mp), P(None, None, mp)),
         check_vma=False,
     )

time: 338 us -> 328 us (0.970)
  waiting for transfers between devices: 263 us -> 240 us
  blocking collectives: 0 us -> 13.3 us
    all_gather x1, waiting for transfers between devices: 99.5 us -> 79.7 us  [per_device(): gathered = lax.all_gather(gathered, stage, axis=2, tiled=True)]
    all_gather x0 -> x1, blocking collectives: none -> 13.3 us  [per_device(): gathered = lax.all_gather(gathered, stage, axis=2, tiled=True)]
where the time goes in v4:
time: 328 us; the launch traced here: 327 us
  waiting for transfers between devices  240 us (73%)
  starting transfers between devices  26.7 us (8%)
  local copies, waits for them, and re-layouts  17.5 us (5%)
  between operations  14.3 us (4%)
  blocking collectives  13.3 us (4%)
  matrix products  11.3 us (3%)
  other arithmetic  3.84 us (1%)
    all_to_all x2, waiting for transfers between devices, head_sum(): moved = lax.all_to_all(parts, axis, 0, 0, tiled=True)  93.8 us
    all_gather x1, waiting for transfers between devices, per_device(): gathered = lax.all_gather(gathered, stage, axis=2, tiled=True)  79.7 us
    all_gather x1, waiting for transfers between devices, per_device(): collected = lax.all_gather(encoded, 'segment', axis=0, tiled=True)  40.2 us
    all_to_all x2, starting transfers between devices, head_sum(): moved = lax.all_to_all(parts, axis, 0, 0, tiled=True)  14.4 us
    all_gather x1, blocking collectives, per_device(): gathered = lax.all_gather(gathered, stage, axis=2, tiled=True)  13.3 us
    all_to_all x1, waiting for transfers between devices, segment_sum(): return lax.all_to_all(spread, axis, 0, 0, tiled=True).reshape(contrib.shape)  13.3 us
    all_to_all x1, waiting for transfers between devices, segment_sum(): moved = lax.all_to_all(parts, axis, 0, 0, tiled=True)  13.1 us
  transfers between devices with their start and end apart: 8, of which 6 were waited for; matrix products, arithmetic and copies ran while one was open for 6% of the time, Pallas kernels for 0%

profile of v4, /device:TPU:1, one launch (start us, length us, event | category | flops | bytes accessed | tf_op | source)
XLA Modules:
  0.0 327.0 jit_solution(12358565042529949686)
XLA Ops:
  7.2 1.0 pad_maximum_fusion.2
  8.2 13.3 %all_gather.9 = bf16[3,128,1024]{2,1,0:T(8,128)(2,1)} all-gather(bf16[3,128,256]{2,1,0:T(8,128)(2,1)S(1)} %pad_maximum_fusion.2), channel_id=1, replica_groups=mesh['segment'=16,'my'=8,'mx'=4] {'mx'}, dimensions={2}, use_global_device_ids=true | all-gather | bytes 983040 | tf_op jit(solution)/shard_map/all_gather | solution.py:66
  21.6 3.8 %slice_bitcast_fusion.2 = (bf16[8192,128]{1,0:T(8,128)(2,1)}, bf16[8192,128]{1,0:T(8,128)(2,1)S(1)}) fusion(bf16[1,2,8192,128]{3,2,1,0:T(8,128)(2,1)} %param.8), kind=kLoop, calls=%fused_computation.16 | loop fusion | bytes 8388608 | tf_op jit(solution)/shard_map/squeeze | solution.py:72
  25.4 79.7 %all-gather.3.cloned.1.call-done = bf16[3,128,8192]{2,1,0:T(8,128)(2,1)} async-done(((bf16[3,128,1024]{2,1,0:T(8,128)(2,1)}), bf16[3,128,8192]{2,1,0:T(8,128)(2,1)}) %all-gather.3.cloned.1.call-update) | async-done | bytes 6291472 | tf_op jit(solution)/shard_map/all_gather | solution.py:66
  105.1 2.2 slice-done
  107.3 0.7 copy-done
  108.0 1.3 conditional.1
  108.0 1.3 convolution_convert_fusion
  109.3 0.6 copy-done.1
  110.2 2.9 fusion.10
  113.1 40.2 %all-gather.5.cloned.1.call-done = bf16[4096,256]{1,0:T(8,128)(2,1)} async-done(((bf16[256,256]{1,0:T(8,128)(2,1)}), bf16[4096,256]{1,0:T(8,128)(2,1)}) %all-gather.5.cloned.1.call-update) | async-done | bytes 2097168 | tf_op jit(solution)/shard_map/all_gather | solution.py:94
  153.3 1.1 slice.76
  154.4 0.6 gather_fusion.1
  157.6 0.9 copy.19
  158.5 4.4 %all-to-all-start.2 = ((bf16[16,64,256]{2,1,0:T(8,128)(2,1)}), bf16[16,64,256]{2,1,0:T(8,128)(2,1)S(1)}, u32[]{:S(2)}, u32[]{:S(2)}) async-start(bf16[16,64,256]{2,1,0:T(8,128)(2,1)} %bitcast.28), calls=%async_computation.2 | async-start | bytes 1048576 | tf_op jit(solution)/shard_map/all_to_all | solution.py:51
  163.3 2.3 convolution_convert_fusion.3
  165.6 1.6 copy.25
  167.1 13.1 %all-to-all-done.2 = bf16[16,64,256]{2,1,0:T(8,128)(2,1)S(1)} async-done(((bf16[16,64,256]{2,1,0:T(8,128)(2,1)}), bf16[16,64,256]{2,1,0:T(8,128)(2,1)S(1)}, u32[]{:S(2)}, u32[]{:S(2)}) %all-to-all-start.2) | async-done | bytes 524320 | tf_op jit(solution)/shard_map/all_to_all | solution.py:51
  180.2 9.3 %all-to-all-start.1 = ((bf16[32,256,128]{1,2,0:T(8,128)(2,1)}), bf16[32,256,128]{1,2,0:T(8,128)(2,1)S(1)}, u32[]{:S(2)}, u32[]{:S(2)}) async-start(bf16[32,256,128]{1,2,0:T(8,128)(2,1)} %bitcast.103), calls=%async_computation.1 | async-start | bytes 4194304 | tf_op jit(solution)/shard_map/all_to_all | solution.py:44
  190.8 2.3 convolution_convert_fusion.4
  193.2 1.6 copy.26
  194.8 45.4 %all-to-all-done.1 = bf16[32,256,128]{1,2,0:T(8,128)(2,1)S(1)} async-done(((bf16[32,256,128]{1,2,0:T(8,128)(2,1)}), bf16[32,256,128]{1,2,0:T(8,128)(2,1)S(1)}, u32[]{:S(2)}, u32[]{:S(2)}) %all-to-all-start.1) | async-done | bytes 2097184 | tf_op jit(solution)/shard_map/all_to_all | solution.py:44
  240.2 5.1 %all-to-all-start = ((bf16[32,256,128]{1,2,0:T(8,128)(2,1)}), bf16[32,256,128]{1,2,0:T(8,128)(2,1)}, u32[]{:S(2)}, u32[]{:S(2)}) async-start(bf16[32,256,128]{1,2,0:T(8,128)(2,1)} %bitcast.104), calls=%async_computation | async-start | bytes 4194304 | tf_op jit(solution)/shard_map/all_to_all | solution.py:44
  245.4 48.3 %all-to-all-done = bf16[32,256,128]{1,2,0:T(8,128)(2,1)} async-done(((bf16[32,256,128]{1,2,0:T(8,128)(2,1)}), bf16[32,256,128]{1,2,0:T(8,128)(2,1)}, u32[]{:S(2)}, u32[]{:S(2)}) %all-to-all-start) | async-done | bytes 2097184 | tf_op jit(solution)/shard_map/all_to_all | solution.py:44
  293.8 0.8 broadcast_in_dim.11
  294.6 6.0 %all-to-all-start.3 = ((bf16[16,64,256]{2,1,0:T(8,128)(2,1)}), bf16[16,64,256]{2,1,0:T(8,128)(2,1)S(1)}, u32[]{:S(2)}, u32[]{:S(2)}) async-start(bf16[16,64,256]{2,1,0:T(8,128)(2,1)} %broadcast_in_dim.11), calls=%async_computation.3 | async-start | bytes 1048576 | tf_op jit(solution)/shard_map/all_to_all | solution.py:54
  301.0 1.9 convert_reduce_fusion.1
  303.1 1.5 collective-permute-start
  304.7 13.3 %all-to-all-done.3 = bf16[16,64,256]{2,1,0:T(8,128)(2,1)S(1)} async-done(((bf16[16,64,256]{2,1,0:T(8,128)(2,1)}), bf16[16,64,256]{2,1,0:T(8,128)(2,1)S(1)}, u32[]{:S(2)}, u32[]{:S(2)}) %all-to-all-start.3) | async-done | bytes 524320 | tf_op jit(solution)/shard_map/all_to_all | solution.py:54
  318.0 0.9 reshape_reshape.7
  318.9 0.6 copy.35
  319.6 0.6 copy.36
  (42 shorter events, 5.3 us)
Async XLA Ops:
  7.2 97.9 %all-gather.3.cloned.1.call-start = ((), (), s32[]{:S(2)}) async-start(), calls=%async_computation.4 | async-start | bytes 7077888 | tf_op jit(solution)/shard_map/all_gather | solution.py:66
  21.5 131.8 %all-gather.5.cloned.1.call-start = ((), (), s32[]{:S(2)}) async-start(), calls=%async_computation.5 | async-start | bytes 2228224 | tf_op jit(solution)/shard_map/all_gather | solution.py:94
  105.1 2.2 slice-start
  105.1 2.9 copy-start
  108.0 2.0 copy-start.4
  109.3 0.7 copy-start.1
  158.5 21.7 %all-to-all-start.2 = ((bf16[16,64,256]{2,1,0:T(8,128)(2,1)}), bf16[16,64,256]{2,1,0:T(8,128)(2,1)S(1)}, u32[]{:S(2)}, u32[]{:S(2)}) async-start(bf16[16,64,256]{2,1,0:T(8,128)(2,1)} %bitcast.28), calls=%async_computation.2 | async-start | bytes 1048576 | tf_op jit(solution)/shard_map/all_to_all | solution.py:51
  180.2 60.0 %all-to-all-start.1 = ((bf16[32,256,128]{1,2,0:T(8,128)(2,1)}), bf16[32,256,128]{1,2,0:T(8,128)(2,1)S(1)}, u32[]{:S(2)}, u32[]{:S(2)}) async-start(bf16[32,256,128]{1,2,0:T(8,128)(2,1)} %bitcast.103), calls=%async_computation.1 | async-start | bytes 4194304 | tf_op jit(solution)/shard_map/all_to_all | solution.py:44
  240.2 53.6 %all-to-all-start = ((bf16[32,256,128]{1,2,0:T(8,128)(2,1)}), bf16[32,256,128]{1,2,0:T(8,128)(2,1)}, u32[]{:S(2)}, u32[]{:S(2)}) async-start(bf16[32,256,128]{1,2,0:T(8,128)(2,1)} %bitcast.104), calls=%async_computation | async-start | bytes 4194304 | tf_op jit(solution)/shard_map/all_to_all | solution.py:44
  294.6 23.4 %all-to-all-start.3 = ((bf16[16,64,256]{2,1,0:T(8,128)(2,1)}), bf16[16,64,256]{2,1,0:T(8,128)(2,1)S(1)}, u32[]{:S(2)}, u32[]{:S(2)}) async-start(bf16[16,64,256]{2,1,0:T(8,128)(2,1)} %broadcast_in_dim.11), calls=%async_computation.3 | async-start | bytes 1048576 | tf_op jit(solution)/shard_map/all_to_all | solution.py:54
  300.7 2.2 copy-start.2
  300.7 2.2 copy-start.3
  302.9 16.0 %collective-permute-start.1 = (bf16[1,128,256]{2,1,0:T(8,128)(2,1)S(1)}, bf16[1,128,256]{2,1,0:T(8,128)(2,1)S(1)}, u32[]{:S(2)}, u32[]{:S(2)}) collective-permute-start(bf16[1,128,256]{2,1,0:T(8,128)(2,1)S(1)} %get-tuple-element.52), channel_id=1, source_target_pairs={{0,480},{32,0},{64,32},{96,64},{128,96},{160,128},{192,160},{224,1... | collective-permute-start | bytes 196616 | tf_op jit(solution)/shard_map/ppermute | solution.py:18
  303.1 15.8 %collective-permute-start = (bf16[1,128,256]{2,1,0:T(8,128)(2,1)S(1)}, bf16[1,128,256]{2,1,0:T(8,128)(2,1)S(1)}, u32[]{:S(2)}, u32[]{:S(2)}) collective-permute-start(bf16[1,128,256]{2,1,0:T(8,128)(2,1)S(1)} %get-tuple-element.53), channel_id=1, source_target_pairs={{0,32},{32,64},{64,96},{96,128},{128,160},{160,192},{192,224},{224... | collective-permute-start | bytes 196616 | tf_op jit(solution)/shard_map/ppermute | solution.py:18
Sparse Core Ops, SparseCore 0:
  21.7 83.3 all-gather.2
  110.1 43.1 all-gather.4

commit v5 on v4

--- a/solution.py
+++ b/solution.py
@@ -38,11 +38,12 @@
     return (grad_queries, grad_keys, grad_values)
 
 
-def head_sum(term, axis):
+def head_sum(terms, axis):
     devices = lax.axis_size(axis)
-    parts = term.astype(jnp.bfloat16).reshape(devices, term.shape[0] // devices, term.shape[1])
+    count, width, tokens = terms.shape
+    parts = terms.astype(jnp.bfloat16).reshape(count, devices, width // devices, tokens).transpose(1, 0, 2, 3)
     moved = lax.all_to_all(parts, axis, 0, 0, tiled=True)
-    return jnp.sum(moved.astype(jnp.float32), axis=0).T
+    return jnp.sum(moved.astype(jnp.float32), axis=0).transpose(0, 2, 1)
 
 
 def segment_sum(contrib, axis):
@@ -108,14 +109,6 @@
         "cqk,ckd->cqd", rounded_fwd, values_fwd, preferred_element_type=jnp.float32
     ).astype(jnp.bfloat16)
     mixed_flat = mixed.reshape(tokens, head)
-    piece = w_out
-    out_sum = head_sum(
-        lax.dot_general(piece, mixed_flat, (((1,), (1,)), ((), ())), preferred_element_type=jnp.float32),
-        mp,
-    )
-    forward_rows = (local_rows[0].astype(jnp.float32) + out_sum).astype(jnp.bfloat16)
-    forward_rows = jnp.where(is_encoder, local_carry, forward_rows)
-    passed = from_behind(forward_rows[None], "segment", 1)
     upstream = (
         jnp.dot(full_carry, w_out, preferred_element_type=jnp.float32)
         .astype(jnp.bfloat16)
@@ -127,11 +120,16 @@
         query_blocks[1], keys_back, values_back, soft_back, rounded_back, upstream, score_scale
     )
     grad_flat = grad_queries.reshape(tokens, head)
-    piece = w_query
-    grad_input = head_sum(
-        lax.dot_general(piece, grad_flat, (((1,), (1,)), ((), ())), preferred_element_type=jnp.float32),
-        mp,
+    terms = jnp.stack(
+        [
+            lax.dot_general(w_out, mixed_flat, (((1,), (1,)), ((), ())), preferred_element_type=jnp.float32),
+            lax.dot_general(w_query, grad_flat, (((1,), (1,)), ((), ())), preferred_element_type=jnp.float32),
+        ]
     )
+    out_sum, grad_input = head_sum(terms, mp)
+    forward_rows = (local_rows[0].astype(jnp.float32) + out_sum).astype(jnp.bfloat16)
+    forward_rows = jnp.where(is_encoder, local_carry, forward_rows)
+    passed = from_behind(forward_rows[None], "segment", 1)
     back = local_carry.astype(jnp.float32) + grad_input
     back_rows = jnp.where(is_encoder, local_carry, back.astype(jnp.bfloat16))
     returned = from_behind(back_rows[None], "segment", -1)

time: 328 us -> 320 us (0.976)
  starting transfers between devices: 26.7 us -> 19.3 us
  waiting for transfers between devices: 240 us -> 236 us
    all_to_all x1, waiting for transfers between devices: 13.1 us -> 6.1 us  [segment_sum(): moved = lax.all_to_all(parts, axis, 0, 0, tiled=True)]
    all_to_all x2 -> x1, starting transfers between devices: 14.4 us -> 9.39 us  [head_sum(): moved = lax.all_to_all(parts, axis, 0, 0, tiled=True)]
    all_to_all x2 -> x1, waiting for transfers between devices: 93.8 us -> 97.5 us  [head_sum(): moved = lax.all_to_all(parts, axis, 0, 0, tiled=True)]
  transfers between devices with their start and end apart: 8 -> 7, of which waited for: 6 -> 5; matrix products, arithmetic and copies ran while one was open for 6% -> 7% of each run, Pallas kernels for 0% -> 0%
where the time goes in v5:
time: 320 us; the launch traced here: 319 us
  waiting for transfers between devices  236 us (74%)
  starting transfers between devices  19.3 us (6%)
  local copies, waits for them, and re-layouts  17.9 us (6%)
  between operations  14.3 us (4%)
  blocking collectives  13.3 us (4%)
  matrix products  11.3 us (4%)
  other arithmetic  6.92 us (2%)
    all_to_all x1, waiting for transfers between devices, head_sum(): moved = lax.all_to_all(parts, axis, 0, 0, tiled=True)  97.5 us
    all_gather x1, waiting for transfers between devices, per_device(): gathered = lax.all_gather(gathered, stage, axis=2, tiled=True)  79.7 us
    all_gather x1, waiting for transfers between devices, per_device(): collected = lax.all_gather(encoded, 'segment', axis=0, tiled=True)  40.1 us
    all_gather x1, blocking collectives, per_device(): gathered = lax.all_gather(gathered, stage, axis=2, tiled=True)  13.3 us
    all_to_all x1, waiting for transfers between devices, segment_sum(): return lax.all_to_all(spread, axis, 0, 0, tiled=True).reshape(contrib.shape)  12.6 us
    all_to_all x1, starting transfers between devices, head_sum(): moved = lax.all_to_all(parts, axis, 0, 0, tiled=True)  9.39 us
  transfers between devices with their start and end apart: 7, of which 5 were waited for; matrix products, arithmetic and copies ran while one was open for 7% of the time, Pallas kernels for 0%

profile of v5, /device:TPU:1, one launch (start us, length us, event | category | flops | bytes accessed | tf_op | source)
XLA Modules:
  0.0 319.1 jit_solution(14900120304621219254)
XLA Ops:
  7.2 1.0 pad_maximum_fusion.2
  8.2 13.3 %all_gather.9 = bf16[3,128,1024]{2,1,0:T(8,128)(2,1)} all-gather(bf16[3,128,256]{2,1,0:T(8,128)(2,1)S(1)} %pad_maximum_fusion.2), channel_id=1, replica_groups=mesh['segment'=16,'my'=8,'mx'=4] {'mx'}, dimensions={2}, use_global_device_ids=true | all-gather | bytes 983040 | tf_op jit(solution)/shard_map/all_gather | solution.py:67
  21.6 3.8 %slice_bitcast_fusion.2 = (bf16[8192,128]{1,0:T(8,128)(2,1)}, bf16[8192,128]{1,0:T(8,128)(2,1)S(1)}) fusion(bf16[1,2,8192,128]{3,2,1,0:T(8,128)(2,1)} %param.8), kind=kLoop, calls=%fused_computation.14 | loop fusion | bytes 8388608 | tf_op jit(solution)/shard_map/squeeze | solution.py:73
  25.4 79.7 %all-gather.3.cloned.1.call-done = bf16[3,128,8192]{2,1,0:T(8,128)(2,1)} async-done(((bf16[3,128,1024]{2,1,0:T(8,128)(2,1)}), bf16[3,128,8192]{2,1,0:T(8,128)(2,1)}) %all-gather.3.cloned.1.call-update) | async-done | bytes 6291472 | tf_op jit(solution)/shard_map/all_gather | solution.py:67
  105.1 2.2 slice-done
  107.3 0.7 copy-done
  108.0 1.3 conditional.1
  108.0 1.3 convolution_convert_fusion
  109.3 0.6 copy-done.1
  110.3 2.9 fusion.10
  113.2 40.1 %all-gather.5.cloned.1.call-done = bf16[4096,256]{1,0:T(8,128)(2,1)} async-done(((bf16[256,256]{1,0:T(8,128)(2,1)}), bf16[4096,256]{1,0:T(8,128)(2,1)}) %all-gather.5.cloned.1.call-update) | async-done | bytes 2097168 | tf_op jit(solution)/shard_map/all_gather | solution.py:95
  153.3 1.1 slice.76
  158.5 0.9 copy.19
  159.4 4.4 %all-to-all-start.1 = ((bf16[16,64,256]{2,1,0:T(8,128)(2,1)}), bf16[16,64,256]{2,1,0:T(8,128)(2,1)S(1)}, u32[]{:S(2)}, u32[]{:S(2)}) async-start(bf16[16,64,256]{2,1,0:T(8,128)(2,1)} %bitcast.25), calls=%async_computation.1 | async-start | bytes 1048576 | tf_op jit(solution)/shard_map/all_to_all | solution.py:52
  163.8 2.3 convolution_convert_fusion.3
  166.3 0.6 copy.22
  166.9 1.2 copy.16
  168.6 2.3 convolution_convert_fusion.4
  170.9 0.6 copy.21
  171.5 1.2 copy.15
  172.7 2.4 maximum_bitcast_fusion
  175.1 6.1 %all-to-all-done.1 = bf16[16,64,256]{2,1,0:T(8,128)(2,1)S(1)} async-done(((bf16[16,64,256]{2,1,0:T(8,128)(2,1)}), bf16[16,64,256]{2,1,0:T(8,128)(2,1)S(1)}, u32[]{:S(2)}, u32[]{:S(2)}) %all-to-all-start.1) | async-done | bytes 524320 | tf_op jit(solution)/shard_map/all_to_all | solution.py:52
  181.2 9.4 %all-to-all-start = ((bf16[32,2,256,128]{2,3,1,0:T(8,128)(2,1)}), bf16[32,2,256,128]{2,3,1,0:T(8,128)(2,1)}, u32[]{:S(2)}, u32[]{:S(2)}) async-start(bf16[32,2,256,128]{2,3,1,0:T(8,128)(2,1)} %maximum_bitcast_fusion), calls=%async_computation | async-start | bytes 8388608 | tf_op jit(solution)/shard_map/all_to_all | solution.py:45
  190.6 97.5 %all-to-all-done = bf16[32,2,256,128]{2,3,1,0:T(8,128)(2,1)} async-done(((bf16[32,2,256,128]{2,3,1,0:T(8,128)(2,1)}), bf16[32,2,256,128]{2,3,1,0:T(8,128)(2,1)}, u32[]{:S(2)}, u32[]{:S(2)}) %all-to-all-start) | async-done | bytes 4194336 | tf_op jit(solution)/shard_map/all_to_all | solution.py:45
  288.2 0.8 broadcast_in_dim.5
  289.0 3.7 %all-to-all-start.2 = ((bf16[16,64,256]{2,1,0:T(8,128)(2,1)}), bf16[16,64,256]{2,1,0:T(8,128)(2,1)S(1)}, u32[]{:S(2)}, u32[]{:S(2)}) async-start(bf16[16,64,256]{2,1,0:T(8,128)(2,1)} %broadcast_in_dim.5), calls=%async_computation.2 | async-start | bytes 1048576 | tf_op jit(solution)/shard_map/all_to_all | solution.py:55
  292.7 2.9 convert_reduce_fusion
  295.9 1.5 collective-permute-start
  297.5 12.6 %all-to-all-done.2 = bf16[16,64,256]{2,1,0:T(8,128)(2,1)S(1)} async-done(((bf16[16,64,256]{2,1,0:T(8,128)(2,1)}), bf16[16,64,256]{2,1,0:T(8,128)(2,1)S(1)}, u32[]{:S(2)}, u32[]{:S(2)}) %all-to-all-start.2) | async-done | bytes 524320 | tf_op jit(solution)/shard_map/all_to_all | solution.py:55
  310.1 0.9 reshape_reshape.7
  311.0 0.6 copy.31
  311.6 0.6 copy.32
  (42 shorter events, 5.5 us)
Async XLA Ops:
  7.2 97.9 %all-gather.3.cloned.1.call-start = ((), (), s32[]{:S(2)}) async-start(), calls=%async_computation.3 | async-start | bytes 7077888 | tf_op jit(solution)/shard_map/all_gather | solution.py:67
  21.5 131.8 %all-gather.5.cloned.1.call-start = ((), (), s32[]{:S(2)}) async-start(), calls=%async_computation.4 | async-start | bytes 2228224 | tf_op jit(solution)/shard_map/all_gather | solution.py:95
  105.1 2.2 slice-start
  105.1 2.9 copy-start
  108.0 2.0 copy-start.4
  109.3 0.7 copy-start.1
  159.4 21.7 %all-to-all-start.1 = ((bf16[16,64,256]{2,1,0:T(8,128)(2,1)}), bf16[16,64,256]{2,1,0:T(8,128)(2,1)S(1)}, u32[]{:S(2)}, u32[]{:S(2)}) async-start(bf16[16,64,256]{2,1,0:T(8,128)(2,1)} %bitcast.25), calls=%async_computation.1 | async-start | bytes 1048576 | tf_op jit(solution)/shard_map/all_to_all | solution.py:52
  181.2 107.0 %all-to-all-start = ((bf16[32,2,256,128]{2,3,1,0:T(8,128)(2,1)}), bf16[32,2,256,128]{2,3,1,0:T(8,128)(2,1)}, u32[]{:S(2)}, u32[]{:S(2)}) async-start(bf16[32,2,256,128]{2,3,1,0:T(8,128)(2,1)} %maximum_bitcast_fusion), calls=%async_computation | async-start | bytes 8388608 | tf_op jit(solution)/shard_map/all_to_all | solution.py:45
  289.0 21.0 %all-to-all-start.2 = ((bf16[16,64,256]{2,1,0:T(8,128)(2,1)}), bf16[16,64,256]{2,1,0:T(8,128)(2,1)S(1)}, u32[]{:S(2)}, u32[]{:S(2)}) async-start(bf16[16,64,256]{2,1,0:T(8,128)(2,1)} %broadcast_in_dim.5), calls=%async_computation.2 | async-start | bytes 1048576 | tf_op jit(solution)/shard_map/all_to_all | solution.py:55
  292.7 2.9 copy-start.2
  292.7 2.9 copy-start.3
  295.7 15.3 %collective-permute-start.1 = (bf16[1,128,256]{2,1,0:T(8,128)(2,1)S(1)}, bf16[1,128,256]{2,1,0:T(8,128)(2,1)S(1)}, u32[]{:S(2)}, u32[]{:S(2)}) collective-permute-start(bf16[1,128,256]{2,1,0:T(8,128)(2,1)S(1)} %get-tuple-element.52), channel_id=1, source_target_pairs={{0,480},{32,0},{64,32},{96,64},{128,96},{160,128},{192,160},{224,1... | collective-permute-start | bytes 196616 | tf_op jit(solution)/shard_map/ppermute | solution.py:18
  295.9 15.0 %collective-permute-start = (bf16[1,128,256]{2,1,0:T(8,128)(2,1)S(1)}, bf16[1,128,256]{2,1,0:T(8,128)(2,1)S(1)}, u32[]{:S(2)}, u32[]{:S(2)}) collective-permute-start(bf16[1,128,256]{2,1,0:T(8,128)(2,1)S(1)} %get-tuple-element.53), channel_id=1, source_target_pairs={{0,32},{32,64},{64,96},{96,128},{128,160},{160,192},{192,224},{224... | collective-permute-start | bytes 196616 | tf_op jit(solution)/shard_map/ppermute | solution.py:18
Sparse Core Ops, SparseCore 0:
  21.7 83.3 all-gather.2
  110.1 43.1 all-gather.4

commit v6 on v5

--- a/solution.py
+++ b/solution.py
@@ -56,10 +56,13 @@
 
 
 def per_device(mp, stages, rows, carry, weights, neighbours):
-    segments = lax.axis_size("segment")
-    encoders = segments // 4
+    seg = ("sg", "sr")
+    segments = lax.axis_size(seg)
+    encoders = lax.axis_size("sr")
     first_encoder = segments - encoders
-    is_encoder = lax.axis_index("segment") >= first_encoder
+    last_group = lax.axis_size("sg") - 1
+    group = lax.axis_index("sg")
+    is_encoder = group == last_group
     local_rows = rows[0]
     local_carry = carry[0]
     gathered = jnp.concatenate([local_rows, local_carry[None]], axis=0)
@@ -92,8 +95,11 @@
     encoded, queries = lax.cond(is_encoder, encode, decode)
     per_encoder = 2 * tokens // NBLEN
     pool_blocks = encoders * per_encoder
-    collected = lax.all_gather(encoded, "segment", axis=0, tiled=True)
-    pool = collected[first_encoder * 2 * tokens :].reshape(pool_blocks, NBLEN, 2 * head)
+    piece = encoded
+    for target in range(last_group):
+        arrived = lax.ppermute(encoded, "sg", [(last_group, target)])
+        piece = jnp.where(group == target, arrived, piece)
+    pool = lax.all_gather(piece, "sr", axis=0, tiled=True).reshape(pool_blocks, NBLEN, 2 * head)
     groups = tokens // GROUP
     local_nbr = neighbours[0]
     score_scale = 1.0 / math.sqrt(head)
@@ -129,10 +135,10 @@
     out_sum, grad_input = head_sum(terms, mp)
     forward_rows = (local_rows[0].astype(jnp.float32) + out_sum).astype(jnp.bfloat16)
     forward_rows = jnp.where(is_encoder, local_carry, forward_rows)
-    passed = from_behind(forward_rows[None], "segment", 1)
+    passed = from_behind(forward_rows[None], seg, 1)
     back = local_carry.astype(jnp.float32) + grad_input
     back_rows = jnp.where(is_encoder, local_carry, back.astype(jnp.bfloat16))
-    returned = from_behind(back_rows[None], "segment", -1)
+    returned = from_behind(back_rows[None], seg, -1)
     onehot = (
         local_nbr[1][..., None] == jnp.arange(pool_blocks, dtype=jnp.int32)[None, None, :]
     ).astype(jnp.float32)
@@ -141,45 +147,52 @@
     )
     contrib = jnp.einsum("cbp,cbrf->prf", onehot, grad_keyval)
     contrib = jnp.where(is_encoder, jnp.zeros_like(contrib), contrib)
-    pooled = segment_sum(contrib.astype(jnp.bfloat16).reshape(pool_blocks * NBLEN, 2 * head), "segment")
+    pooled = segment_sum(contrib.astype(jnp.bfloat16).reshape(pool_blocks * NBLEN, 2 * head), seg)
     kv_grad = pooled.reshape(pool_blocks * NBLEN, 2, head)
     return (passed, returned, kv_grad)
 
 
-def split_mp(mesh):
+def split_mesh(mesh):
     devices = mesh.devices
+    segments = devices.shape[0]
+    encoders = segments // 4
+    groups = segments // encoders
     try:
         xs = [d.coords[0] for d in devices[0]]
         ys = [d.coords[1] for d in devices[0]]
-    except (AttributeError, TypeError, IndexError):
-        return None
-    wide = len(set(xs))
-    tall = devices.shape[1] // wide
-    if wide * tall != devices.shape[1] or wide == 1 or tall == 1:
-        return None
-    grid_x = np.array(xs).reshape(tall, wide)
-    grid_y = np.array(ys).reshape(tall, wide)
-    if not ((grid_x == grid_x[:1]).all() and (grid_y == grid_y[:, :1]).all()):
-        return None
-    return Mesh(devices.reshape(devices.shape[0], tall, wide), ("segment", "my", "mx"))
+        wide = len(set(xs))
+        tall = devices.shape[1] // wide
+        grid_x = np.array(xs).reshape(tall, wide)
+        grid_y = np.array(ys).reshape(tall, wide)
+        ok = (
+            wide * tall == devices.shape[1]
+            and wide > 1
+            and tall > 1
+            and (grid_x == grid_x[:1]).all()
+            and (grid_y == grid_y[:, :1]).all()
+        )
+    except (AttributeError, TypeError, IndexError, ValueError):
+        ok = False
+    if ok:
+        view = devices.reshape(groups, encoders, tall, wide)
+        return Mesh(view, ("sg", "sr", "my", "mx")), ("my", "mx"), ("mx", "my")
+    view = devices.reshape(groups, encoders, devices.shape[1])
+    return Mesh(view, ("sg", "sr", "mp")), "mp", ("mp",)
 
 
 def solution(mesh):
-    split = split_mp(mesh)
-    if split is None:
-        inner, mp, stages = mesh, "mp", ("mp",)
-    else:
-        inner, mp, stages = split, ("my", "mx"), ("mx", "my")
+    inner, mp, stages = split_mesh(mesh)
+    seg = ("sg", "sr")
     placed = (
-        P("segment", None, None, mp),
-        P("segment", None, mp),
-        P("segment", None, None, mp),
-        P("segment", None, None, None),
+        P(seg, None, None, mp),
+        P(seg, None, mp),
+        P(seg, None, None, mp),
+        P(seg, None, None, None),
     )
     return jax.shard_map(
         functools.partial(per_device, mp, stages),
         mesh=inner,
         in_specs=placed,
-        out_specs=(P("segment", None, mp), P("segment", None, mp), P(None, None, mp)),
+        out_specs=(P(seg, None, mp), P(seg, None, mp), P(None, None, mp)),
         check_vma=False,
     )

time: 320 us -> 298 us (0.931)
  waiting for transfers between devices: 236 us -> 201 us
  blocking collectives: 13.3 us -> 26.5 us
    all_gather x1 -> x0, waiting for transfers between devices: 40.1 us -> none  [per_device(): collected = lax.all_gather(encoded, 'segment', axis=0, tiled=True)]
    all_gather x0 -> x1, blocking collectives: none -> 13.1 us  [per_device(): lax.all_gather(piece, 'sr', axis=0, tiled=True)]
    ppermute x0 -> x3, waiting for transfers between devices: none -> 5.22 us  [per_device(): arrived = lax.ppermute(encoded, 'sg', [(last_group, target)])]
  transfers between devices with their start and end apart: 7 -> 9, of which waited for: 5 -> 5; matrix products, arithmetic and copies ran while one was open for 7% -> 7% of each run, Pallas kernels for 0% -> 0%
where the time goes in v6:
time: 298 us; the launch traced here: 297 us
  waiting for transfers between devices  201 us (67%)
  blocking collectives  26.5 us (9%)
  starting transfers between devices  21.4 us (7%)
  local copies, waits for them, and re-layouts  16.1 us (5%)
  between operations  14.3 us (5%)
  matrix products  11.3 us (4%)
  other arithmetic  6.95 us (2%)
    all_to_all x1, waiting for transfers between devices, head_sum(): moved = lax.all_to_all(parts, axis, 0, 0, tiled=True)  97.5 us
    all_gather x1, waiting for transfers between devices, per_device(): gathered = lax.all_gather(gathered, stage, axis=2, tiled=True)  79.4 us
    all_gather x1, blocking collectives, per_device(): gathered = lax.all_gather(gathered, stage, axis=2, tiled=True)  13.3 us
    all_gather x1, blocking collectives, per_device(): lax.all_gather(piece, 'sr', axis=0, tiled=True)  13.1 us
    all_to_all x1, waiting for transfers between devices, segment_sum(): return lax.all_to_all(spread, axis, 0, 0, tiled=True).reshape(contrib.shape)  12.6 us
    all_to_all x1, starting transfers between devices, head_sum(): moved = lax.all_to_all(parts, axis, 0, 0, tiled=True)  7.17 us
    all_to_all x1, starting transfers between devices, segment_sum(): moved = lax.all_to_all(parts, axis, 0, 0, tiled=True)  6.16 us
    all_to_all x1, waiting for transfers between devices, segment_sum(): moved = lax.all_to_all(parts, axis, 0, 0, tiled=True)  6.1 us
  transfers between devices with their start and end apart: 9, of which 5 were waited for; matrix products, arithmetic and copies ran while one was open for 7% of the time, Pallas kernels for 0%

profile of v6, /device:TPU:1, one launch (start us, length us, event | category | flops | bytes accessed | tf_op | source)
XLA Modules:
  0.0 297.5 jit_solution(3581924129911619828)
XLA Ops:
  7.2 1.0 pad_maximum_fusion.2
  8.2 13.3 %all_gather.9 = bf16[3,128,1024]{2,1,0:T(8,128)(2,1)} all-gather(bf16[3,128,256]{2,1,0:T(8,128)(2,1)S(1)} %pad_maximum_fusion.2), channel_id=1, replica_groups=mesh['sg'=4,'sr'=4,'my'=8,'mx'=4] {'mx'}, dimensions={2}, use_global_device_ids=true | all-gather | bytes 983040 | tf_op jit(solution)/shard_map/all_gather | solution.py:70
  21.9 3.8 %slice_bitcast_fusion.2 = (bf16[8192,128]{1,0:T(8,128)(2,1)}, bf16[8192,128]{1,0:T(8,128)(2,1)S(1)}) fusion(bf16[1,2,8192,128]{3,2,1,0:T(8,128)(2,1)} %param.8), kind=kLoop, calls=%fused_computation.14 | loop fusion | bytes 8388608 | tf_op jit(solution)/shard_map/squeeze | solution.py:76
  25.7 79.4 %all-gather.2.cloned.1.call-done = bf16[3,128,8192]{2,1,0:T(8,128)(2,1)} async-done(((bf16[3,128,1024]{2,1,0:T(8,128)(2,1)}), bf16[3,128,8192]{2,1,0:T(8,128)(2,1)}) %all-gather.2.cloned.1.call-update) | async-done | bytes 6291472 | tf_op jit(solution)/shard_map/all_gather | solution.py:70
  105.1 2.2 slice-done
  107.3 0.7 copy-done
  108.0 1.3 conditional.1
  108.0 1.3 convolution_convert_fusion
  109.3 1.3 collective-permute-start.2
  110.6 0.7 collective-permute-start.1
  111.3 0.7 collective-permute-start
  112.0 2.9 fusion.10
  114.9 5.2 %collective-permute-done.2 = bf16[256,256]{1,0:T(8,128)(2,1)S(1)} collective-permute-done((bf16[256,256]{1,0:T(8,128)(2,1)S(1)}, bf16[256,256]{1,0:T(8,128)(2,1)S(1)}, u32[]{:S(2)}, u32[]{:S(2)}) %collective-permute-start.2) | collective-permute-done | bytes 131104 | tf_op jit(solution)/shard_map/ppermute | solution.py:100
  120.1 13.1 %all_gather.11 = bf16[1024,256]{1,0:T(8,128)(2,1)S(1)} all-gather(bf16[256,256]{1,0:T(8,128)(2,1)S(1)} %select_select_fusion), channel_id=1, replica_groups=mesh['sg'=4,'sr'=4,'my'=8,'mx'=4] {'sr'}, dimensions={0}, use_global_device_ids=true | all-gather | bytes 655360 | tf_op jit(solution)/shard_map/all_gather | solution.py:102
  137.4 0.9 copy.19
  138.3 6.2 %all-to-all-start.1 = ((bf16[16,64,256]{2,1,0:T(8,128)(2,1)}), bf16[16,64,256]{2,1,0:T(8,128)(2,1)S(1)}, u32[]{:S(2)}, u32[]{:S(2)}) async-start(bf16[16,64,256]{2,1,0:T(8,128)(2,1)} %bitcast.25), calls=%async_computation.1 | async-start | bytes 1048576 | tf_op jit(solution)/shard_map/all_to_all | solution.py:52
  144.4 2.3 convolution_convert_fusion.3
  147.5 1.2 copy.16
  149.2 2.3 convolution_convert_fusion.4
  152.1 1.2 copy.15
  153.3 2.4 maximum_bitcast_fusion
  155.7 6.1 %all-to-all-done.1 = bf16[16,64,256]{2,1,0:T(8,128)(2,1)S(1)} async-done(((bf16[16,64,256]{2,1,0:T(8,128)(2,1)}), bf16[16,64,256]{2,1,0:T(8,128)(2,1)S(1)}, u32[]{:S(2)}, u32[]{:S(2)}) %all-to-all-start.1) | async-done | bytes 524320 | tf_op jit(solution)/shard_map/all_to_all | solution.py:52
  161.8 7.2 %all-to-all-start = ((bf16[32,2,256,128]{2,3,1,0:T(8,128)(2,1)}), bf16[32,2,256,128]{2,3,1,0:T(8,128)(2,1)}, u32[]{:S(2)}, u32[]{:S(2)}) async-start(bf16[32,2,256,128]{2,3,1,0:T(8,128)(2,1)} %maximum_bitcast_fusion), calls=%async_computation | async-start | bytes 8388608 | tf_op jit(solution)/shard_map/all_to_all | solution.py:45
  169.0 97.5 %all-to-all-done = bf16[32,2,256,128]{2,3,1,0:T(8,128)(2,1)} async-done(((bf16[32,2,256,128]{2,3,1,0:T(8,128)(2,1)}), bf16[32,2,256,128]{2,3,1,0:T(8,128)(2,1)}, u32[]{:S(2)}, u32[]{:S(2)}) %all-to-all-start) | async-done | bytes 4194336 | tf_op jit(solution)/shard_map/all_to_all | solution.py:45
  266.6 0.8 broadcast_in_dim.5
  267.4 3.7 %all-to-all-start.2 = ((bf16[16,64,256]{2,1,0:T(8,128)(2,1)}), bf16[16,64,256]{2,1,0:T(8,128)(2,1)S(1)}, u32[]{:S(2)}, u32[]{:S(2)}) async-start(bf16[16,64,256]{2,1,0:T(8,128)(2,1)} %broadcast_in_dim.5), calls=%async_computation.2 | async-start | bytes 1048576 | tf_op jit(solution)/shard_map/all_to_all | solution.py:55
  271.1 2.9 convert_reduce_fusion
  274.3 1.5 collective-permute-start.3
  275.8 12.6 %all-to-all-done.2 = bf16[16,64,256]{2,1,0:T(8,128)(2,1)S(1)} async-done(((bf16[16,64,256]{2,1,0:T(8,128)(2,1)}), bf16[16,64,256]{2,1,0:T(8,128)(2,1)S(1)}, u32[]{:S(2)}, u32[]{:S(2)}) %all-to-all-start.2) | async-done | bytes 524320 | tf_op jit(solution)/shard_map/all_to_all | solution.py:55
  288.4 0.9 reshape_reshape.7
  289.4 0.6 copy.31
  290.0 0.6 copy.32
  (44 shorter events, 6.7 us)
Async XLA Ops:
  7.2 14.4 %copy-start.3 = (s32[1,2,2,2]{3,2,1,0:T(2,128)S(1)}, s32[1,2,2,2]{3,2,1,0:T(2,128)}, u32[]{:S(2)}) copy-start(s32[1,2,2,2]{3,2,1,0:T(2,128)} %param.9) | copy-start | bytes 100
  7.2 97.9 %all-gather.2.cloned.1.call-start = ((), (), s32[]{:S(2)}) async-start(), calls=%async_computation.3 | async-start | bytes 7077888 | tf_op jit(solution)/shard_map/all_gather | solution.py:70
  105.1 2.2 slice-start
  105.1 2.9 copy-start
  109.3 10.8 %collective-permute-start.2 = (bf16[256,256]{1,0:T(8,128)(2,1)S(1)}, bf16[256,256]{1,0:T(8,128)(2,1)S(1)}, u32[]{:S(2)}, u32[]{:S(2)}) collective-permute-start(bf16[256,256]{1,0:T(8,128)(2,1)S(1)} %get-tuple-element.37), channel_id=1, source_target_pairs={{384,0},{385,1},{386,2},{387,3},{388,4},{389,5},{390,6},{391,7},{3... | collective-permute-start | bytes 393224 | tf_op jit(solution)/shard_map/ppermute | solution.py:100
  110.6 9.5 %collective-permute-start.1 = (bf16[256,256]{1,0:T(8,128)(2,1)S(1)}, bf16[256,256]{1,0:T(8,128)(2,1)S(1)}, u32[]{:S(2)}, u32[]{:S(2)}) collective-permute-start(bf16[256,256]{1,0:T(8,128)(2,1)S(1)} %get-tuple-element.37), channel_id=1, source_target_pairs={{384,128},{385,129},{386,130},{387,131},{388,132},{389,133},{390,1... | collective-permute-start | bytes 393224 | tf_op jit(solution)/shard_map/ppermute | solution.py:100
  111.3 8.8 %collective-permute-start = (bf16[256,256]{1,0:T(8,128)(2,1)S(1)}, bf16[256,256]{1,0:T(8,128)(2,1)S(1)}, u32[]{:S(2)}, u32[]{:S(2)}) collective-permute-start(bf16[256,256]{1,0:T(8,128)(2,1)S(1)} %get-tuple-element.37), channel_id=1, source_target_pairs={{384,256},{385,257},{386,258},{387,259},{388,260},{389,261},{390,2... | collective-permute-start | bytes 393224 | tf_op jit(solution)/shard_map/ppermute | solution.py:100
  138.3 23.5 %all-to-all-start.1 = ((bf16[16,64,256]{2,1,0:T(8,128)(2,1)}), bf16[16,64,256]{2,1,0:T(8,128)(2,1)S(1)}, u32[]{:S(2)}, u32[]{:S(2)}) async-start(bf16[16,64,256]{2,1,0:T(8,128)(2,1)} %bitcast.25), calls=%async_computation.1 | async-start | bytes 1048576 | tf_op jit(solution)/shard_map/all_to_all | solution.py:52
  161.8 104.8 %all-to-all-start = ((bf16[32,2,256,128]{2,3,1,0:T(8,128)(2,1)}), bf16[32,2,256,128]{2,3,1,0:T(8,128)(2,1)}, u32[]{:S(2)}, u32[]{:S(2)}) async-start(bf16[32,2,256,128]{2,3,1,0:T(8,128)(2,1)} %maximum_bitcast_fusion), calls=%async_computation | async-start | bytes 8388608 | tf_op jit(solution)/shard_map/all_to_all | solution.py:45
  267.4 21.0 %all-to-all-start.2 = ((bf16[16,64,256]{2,1,0:T(8,128)(2,1)}), bf16[16,64,256]{2,1,0:T(8,128)(2,1)S(1)}, u32[]{:S(2)}, u32[]{:S(2)}) async-start(bf16[16,64,256]{2,1,0:T(8,128)(2,1)} %broadcast_in_dim.5), calls=%async_computation.2 | async-start | bytes 1048576 | tf_op jit(solution)/shard_map/all_to_all | solution.py:55
  271.1 2.9 copy-start.1
  271.1 2.9 copy-start.2
  274.1 15.3 %collective-permute-start.4 = (bf16[1,128,256]{2,1,0:T(8,128)(2,1)S(1)}, bf16[1,128,256]{2,1,0:T(8,128)(2,1)S(1)}, u32[]{:S(2)}, u32[]{:S(2)}) collective-permute-start(bf16[1,128,256]{2,1,0:T(8,128)(2,1)S(1)} %get-tuple-element.52), channel_id=1, source_target_pairs={{0,480},{32,0},{64,32},{96,64},{128,96},{160,128},{192,160},{224,1... | collective-permute-start | bytes 196616 | tf_op jit(solution)/shard_map/ppermute | solution.py:18
  274.3 15.0 %collective-permute-start.3 = (bf16[1,128,256]{2,1,0:T(8,128)(2,1)S(1)}, bf16[1,128,256]{2,1,0:T(8,128)(2,1)S(1)}, u32[]{:S(2)}, u32[]{:S(2)}) collective-permute-start(bf16[1,128,256]{2,1,0:T(8,128)(2,1)S(1)} %get-tuple-element.53), channel_id=1, source_target_pairs={{0,32},{32,64},{64,96},{96,128},{128,160},{160,192},{192,224},{224... | collective-permute-start | bytes 196616 | tf_op jit(solution)/shard_map/ppermute | solution.py:18
Sparse Core Ops, SparseCore 0:
  21.7 83.3 all-gather.1

commit v7 on v6

--- a/solution.py
+++ b/solution.py
@@ -38,12 +38,39 @@
     return (grad_queries, grad_keys, grad_values)
 
 
+def ring_sum(chunks, axis):
+    n = chunks.shape[0]
+    me = lax.axis_index(axis)
+    half = chunks.shape[-1] // 2
+    ahead, behind = chunks[..., :half], chunks[..., half:]
+
+    def take(part, offset):
+        return lax.dynamic_index_in_dim(part, (me + offset) % n, 0, keepdims=False)
+
+    up, down = take(ahead, n - 1), take(behind, 1)
+    for step in range(n - 1):
+        up = lax.ppermute(up, axis, [(i, (i + 1) % n) for i in range(n)])
+        down = lax.ppermute(down, axis, [(i, (i - 1) % n) for i in range(n)])
+        up = up + take(ahead, 2 * n - 2 - step)
+        down = down + take(behind, 2 + step)
+    return jnp.concatenate([up, down], axis=-1)
+
+
 def head_sum(terms, axis):
-    devices = lax.axis_size(axis)
     count, width, tokens = terms.shape
-    parts = terms.astype(jnp.bfloat16).reshape(count, devices, width // devices, tokens).transpose(1, 0, 2, 3)
-    moved = lax.all_to_all(parts, axis, 0, 0, tiled=True)
-    return jnp.sum(moved.astype(jnp.float32), axis=0).transpose(0, 2, 1)
+    rounded = terms.astype(jnp.bfloat16)
+    if isinstance(axis, tuple):
+        tall, wide = lax.axis_size(axis[0]), lax.axis_size(axis[1])
+        parts = rounded.reshape(count, tall, wide, width // (tall * wide), tokens).transpose(2, 1, 0, 3, 4)
+        moved = lax.all_to_all(parts, axis[1], 0, 0, tiled=True)
+        partial = jnp.sum(moved.astype(jnp.float32), axis=0)
+        summed = ring_sum(partial, axis[0])
+    else:
+        devices = lax.axis_size(axis)
+        parts = rounded.reshape(count, devices, width // devices, tokens).transpose(1, 0, 2, 3)
+        moved = lax.all_to_all(parts, axis, 0, 0, tiled=True)
+        summed = jnp.sum(moved.astype(jnp.float32), axis=0)
+    return summed.transpose(0, 2, 1)
 
 
 def segment_sum(contrib, axis):

time: 298 us -> 305 us (1.023)
  waiting for transfers between devices: 201 us -> 147 us
  starting transfers between devices: 21.4 us -> 71.2 us
  local copies, waits for them, and re-layouts: 16.1 us -> 25.9 us
    all_to_all x1, waiting for transfers between devices: 97.5 us -> 46 us  [head_sum(): moved = lax.all_to_all(parts, axis[1], 0, 0, tiled=True)]
    ppermute x0 -> x14, starting transfers between devices: none -> 45.6 us  [the longest x7 31.8 us: ring_sum(): down = lax.ppermute(down, axis, [(i, (i - 1) % n) for i in range(n)])]
    all_to_all x1, waiting for transfers between devices: 12.6 us -> 0.01 us  [segment_sum(): return lax.all_to_all(spread, axis, 0, 0, tiled=True).reshape(contrib.shape)]
    another operation x2 -> x4, local copies, waits for them, and re-layouts: 2.37 us -> 10.9 us  [per_device(): jnp.stack([lax.dot_general(w_out, mixed_flat, (((1,), (1,)), ((), ())), p...]
    ppermute x2, starting transfers between devices: 1.76 us -> 7.6 us  [from_behind(): lax.ppermute(x, axis, [(i, (i + by) % devices) for i in range(devices)])]
    ppermute x0 -> x14, waiting for transfers between devices: none -> 5.02 us  [the longest x7 4.32 us: ring_sum(): down = lax.ppermute(down, axis, [(i, (i - 1) % n) for i in range(n)])]
    all_to_all x1, waiting for transfers between devices: 6.1 us -> 10.1 us  [segment_sum(): moved = lax.all_to_all(parts, axis, 0, 0, tiled=True)]
  transfers between devices with their start and end apart: 9 -> 23, of which waited for: 5 -> 12; matrix products, arithmetic and copies ran while one was open for 7% -> 6% of each run, Pallas kernels for 0% -> 0%
where the time goes in v7:
time: 305 us; the launch traced here: 302 us
  waiting for transfers between devices  147 us (48%)
  starting transfers between devices  71.2 us (23%)
  blocking collectives  26.5 us (9%)
  local copies, waits for them, and re-layouts  25.9 us (8%)
  between operations  14.6 us (5%)
  matrix products  9.71 us (3%)
  other arithmetic  7.39 us (2%)
    all_gather x1, waiting for transfers between devices, per_device(): gathered = lax.all_gather(gathered, stage, axis=2, tiled=True)  79.5 us
    all_to_all x1, waiting for transfers between devices, head_sum(): moved = lax.all_to_all(parts, axis[1], 0, 0, tiled=True)  46 us
    ppermute x7, starting transfers between devices, ring_sum(): down = lax.ppermute(down, axis, [(i, (i - 1) % n) for i in range(n)])  31.8 us
    ppermute x7, starting transfers between devices, ring_sum(): up = lax.ppermute(up, axis, [(i, (i + 1) % n) for i in range(n)])  13.9 us
    all_gather x1, blocking collectives, per_device(): gathered = lax.all_gather(gathered, stage, axis=2, tiled=True)  13.3 us
    all_gather x1, blocking collectives, per_device(): lax.all_gather(piece, 'sr', axis=0, tiled=True)  13.1 us
    another operation x4, local copies, waits for them, and re-layouts, per_device(): jnp.stack([lax.dot_general(w_out, mixed_flat, (((1,), (1,)), ((), ())), p...  10.9 us
    all_to_all x1, waiting for transfers between devices, segment_sum(): moved = lax.all_to_all(parts, axis, 0, 0, tiled=True)  10.1 us
  transfers between devices with their start and end apart: 23, of which 12 were waited for; matrix products, arithmetic and copies ran while one was open for 6% of the time, Pallas kernels for 0%

profile of v7, /device:TPU:1, one launch (start us, length us, event | category | flops | bytes accessed | tf_op | source)
XLA Modules:
  0.0 302.1 jit_solution(13011069141721737453)
XLA Ops:
  8.2 13.3 %all_gather.9 = bf16[3,128,1024]{2,1,0:T(8,128)(2,1)} all-gather(bf16[3,128,256]{2,1,0:T(8,128)(2,1)S(1)} %pad_maximum_fusion.2), channel_id=1, replica_groups=mesh['sg'=4,'sr'=4,'my'=8,'mx'=4] {'mx'}, dimensions={2}, use_global_device_ids=true | all-gather | bytes 983040 | tf_op jit(solution)/shard_map/all_gather | solution.py:97
  21.8 3.8 %slice_bitcast_fusion.2 = (bf16[8192,128]{1,0:T(8,128)(2,1)}, bf16[8192,128]{1,0:T(8,128)(2,1)S(1)}) fusion(bf16[1,2,8192,128]{3,2,1,0:T(8,128)(2,1)} %param.8), kind=kLoop, calls=%fused_computation.16 | loop fusion | bytes 8388608 | tf_op jit(solution)/shard_map/squeeze | solution.py:103
  25.6 79.5 %all-gather.2.cloned.1.call-done = bf16[3,128,8192]{2,1,0:T(8,128)(2,1)} async-done(((bf16[3,128,1024]{2,1,0:T(8,128)(2,1)}), bf16[3,128,8192]{2,1,0:T(8,128)(2,1)}) %all-gather.2.cloned.1.call-update) | async-done | bytes 6291472 | tf_op jit(solution)/shard_map/all_gather | solution.py:97
  105.1 2.2 slice-done
  112.0 2.9 fusion.12
  114.9 5.2 %collective-permute-done.2 = bf16[256,256]{1,0:T(8,128)(2,1)S(1)} collective-permute-done((bf16[256,256]{1,0:T(8,128)(2,1)S(1)}, bf16[256,256]{1,0:T(8,128)(2,1)S(1)}, u32[]{:S(2)}, u32[]{:S(2)}) %collective-permute-start.2) | collective-permute-done | bytes 131104 | tf_op jit(solution)/shard_map/ppermute | solution.py:127
  120.1 13.1 %all_gather.11 = bf16[1024,256]{1,0:T(8,128)(2,1)S(1)} all-gather(bf16[256,256]{1,0:T(8,128)(2,1)S(1)} %select_select_fusion), channel_id=1, replica_groups=mesh['sg'=4,'sr'=4,'my'=8,'mx'=4] {'sr'}, dimensions={0}, use_global_device_ids=true | all-gather | bytes 655360 | tf_op jit(solution)/shard_map/all_gather | solution.py:129
  136.2 2.3 fusion.3
  138.5 2.8 stack.10
  141.3 3.4 %copy.16 = bf16[1,8,4,256,128]{3,1,4,0,2:T(8,128)(2,1)} copy(bf16[1,8,4,256,128]{3,2,1,4,0:T(4,128)(2,1)} %stack.10) | data formatting | bytes 4194304 | tf_op jit(solution)/shard_map/stack | solution.py:156
  145.4 2.8 stack.9
  148.1 2.0 copy.15
  150.3 2.3 maximum_bitcast_fusion
  152.7 4.8 %all-to-all-start = ((bf16[4,8,2,256,128]{3,1,4,2,0:T(8,128)(2,1)}), bf16[4,8,2,256,128]{3,1,4,2,0:T(8,128)(2,1)}, u32[]{:S(2)}, u32[]{:S(2)}) async-start(bf16[4,8,2,256,128]{3,1,4,2,0:T(8,128)(2,1)} %maximum_bitcast_fusion), calls=%async_computation | async-start | bytes 8388608 | tf_op jit(solution)/shard_map/all_to_all | solution.py:65
  160.4 46.0 %all-to-all-done = bf16[4,8,2,256,128]{3,1,4,2,0:T(8,128)(2,1)} async-done(((bf16[4,8,2,256,128]{3,1,4,2,0:T(8,128)(2,1)}), bf16[4,8,2,256,128]{3,1,4,2,0:T(8,128)(2,1)}, u32[]{:S(2)}, u32[]{:S(2)}) %all-to-all-start) | async-done | bytes 4194336 | tf_op jit(solution)/shard_map/all_to_all | solution.py:65
  206.4 7.0 %all-to-all-start.1 = ((bf16[16,64,256]{2,1,0:T(8,128)(2,1)}), bf16[16,64,256]{2,1,0:T(8,128)(2,1)S(1)}, u32[]{:S(2)}, u32[]{:S(2)}) async-start(bf16[16,64,256]{2,1,0:T(8,128)(2,1)} %bitcast.25), calls=%async_computation.1 | async-start | bytes 1048576 | tf_op jit(solution)/shard_map/all_to_all | solution.py:79
  213.4 3.1 %convert_reduce_fusion = f32[8,2,256,128]{2,0,3,1:T(8,128)S(1)} fusion(bf16[4,8,2,256,128]{3,1,4,2,0:T(8,128)(2,1)} %all-to-all-done), kind=kLoop, calls=%fused_computation.12 | loop fusion | flops 3670016 | bytes 6291456 | tf_op jit(solution)/shard_map/reduce_sum | solution.py:66
  216.6 2.1 constant_dynamic-slice_fusion
  220.6 10.1 %all-to-all-done.1 = bf16[16,64,256]{2,1,0:T(8,128)(2,1)S(1)} async-done(((bf16[16,64,256]{2,1,0:T(8,128)(2,1)}), bf16[16,64,256]{2,1,0:T(8,128)(2,1)S(1)}, u32[]{:S(2)}, u32[]{:S(2)}) %all-to-all-start.1) | async-done | bytes 524320 | tf_op jit(solution)/shard_map/all_to_all | solution.py:79
  231.6 3.5 %all-to-all-start.2 = ((bf16[16,64,256]{2,1,0:T(8,128)(2,1)}), bf16[16,64,256]{2,1,0:T(8,128)(2,1)S(1)}, u32[]{:S(2)}, u32[]{:S(2)}) async-start(bf16[16,64,256]{2,1,0:T(8,128)(2,1)} %broadcast_in_dim.5), calls=%async_computation.2 | async-start | bytes 1048576 | tf_op jit(solution)/shard_map/all_to_all | solution.py:82
  235.1 3.1 %collective-permute-start.10 = (f32[2,256,64]{1,2,0:T(8,128)S(1)}, f32[2,256,64]{1,2,0:T(8,128)S(1)}, u32[]{:S(2)}, u32[]{:S(2)}) collective-permute-start(f32[2,256,64]{1,2,0:T(8,128)S(1)} %bitcast.127), channel_id=1, source_target_pairs={{0,28},{4,0},{8,4},{12,8},{16,12},{20,16},{24,20},{28,24},{1,29},{... | collective-permute-start | bytes 393224 | tf_op jit(solution)/shard_map/ppermute | solution.py:53
  238.2 2.2 collective-permute-start.4
  240.4 2.1 collective-permute-done.10
  242.5 4.3 %collective-permute-start.11 = (f32[2,256,64]{1,2,0:T(8,128)S(1)}, f32[2,256,64]{1,2,0:T(8,128)S(1)}, u32[]{:S(2)}, u32[]{:S(2)}) collective-permute-start(f32[2,256,64]{1,2,0:T(8,128)S(1)} %bitcast_add_fusion.6), channel_id=1, source_target_pairs={{0,28},{4,0},{8,4},{12,8},{16,12},{20,16},{24,20},{28,24},{1,29},{... | collective-permute-start | bytes 393224 | tf_op jit(solution)/shard_map/ppermute | solution.py:53
  246.8 1.9 collective-permute-start.5
  249.3 5.3 %collective-permute-start.12 = (f32[2,256,64]{1,2,0:T(8,128)S(1)}, f32[2,256,64]{1,2,0:T(8,128)S(1)}, u32[]{:S(2)}, u32[]{:S(2)}) collective-permute-start(f32[2,256,64]{1,2,0:T(8,128)S(1)} %bitcast_add_fusion.5), channel_id=1, source_target_pairs={{0,28},{4,0},{8,4},{12,8},{16,12},{20,16},{24,20},{28,24},{1,29},{... | collective-permute-start | bytes 393224 | tf_op jit(solution)/shard_map/ppermute | solution.py:53
  254.7 2.1 collective-permute-start.6
  256.8 4.8 %collective-permute-start.13 = (f32[2,256,64]{1,2,0:T(8,128)S(1)}, f32[2,256,64]{1,2,0:T(8,128)S(1)}, u32[]{:S(2)}, u32[]{:S(2)}) collective-permute-start(f32[2,256,64]{1,2,0:T(8,128)S(1)} %bitcast_add_fusion.4), channel_id=1, source_target_pairs={{0,28},{4,0},{8,4},{12,8},{16,12},{20,16},{24,20},{28,24},{1,29},{... | collective-permute-start | bytes 393224 | tf_op jit(solution)/shard_map/ppermute | solution.py:53
  263.7 4.8 %collective-permute-start.14 = (f32[2,256,64]{1,2,0:T(8,128)S(1)}, f32[2,256,64]{1,2,0:T(8,128)S(1)}, u32[]{:S(2)}, u32[]{:S(2)}) collective-permute-start(f32[2,256,64]{1,2,0:T(8,128)S(1)} %bitcast_add_fusion.3), channel_id=1, source_target_pairs={{0,28},{4,0},{8,4},{12,8},{16,12},{20,16},{24,20},{28,24},{1,29},{... | collective-permute-start | bytes 393224 | tf_op jit(solution)/shard_map/ppermute | solution.py:53
  270.7 4.8 %collective-permute-start.15 = (f32[2,256,64]{1,2,0:T(8,128)S(1)}, f32[2,256,64]{1,2,0:T(8,128)S(1)}, u32[]{:S(2)}, u32[]{:S(2)}) collective-permute-start(f32[2,256,64]{1,2,0:T(8,128)S(1)} %bitcast_add_fusion.2), channel_id=1, source_target_pairs={{0,28},{4,0},{8,4},{12,8},{16,12},{20,16},{24,20},{28,24},{1,29},{... | collective-permute-start | bytes 393224 | tf_op jit(solution)/shard_map/ppermute | solution.py:53
  277.6 4.8 %collective-permute-start.16 = (f32[2,256,64]{1,2,0:T(8,128)S(1)}, f32[2,256,64]{1,2,0:T(8,128)S(1)}, u32[]{:S(2)}, u32[]{:S(2)}) collective-permute-start(f32[2,256,64]{1,2,0:T(8,128)S(1)} %bitcast_add_fusion.1), channel_id=1, source_target_pairs={{0,28},{4,0},{8,4},{12,8},{16,12},{20,16},{24,20},{28,24},{1,29},{... | collective-permute-start | bytes 393224 | tf_op jit(solution)/shard_map/ppermute | solution.py:53
  284.4 6.7 %collective-permute-start.18 = (bf16[1,128,256]{2,1,0:T(8,128)(2,1)S(1)}, bf16[1,128,256]{2,1,0:T(8,128)(2,1)S(1)}, u32[]{:S(2)}, u32[]{:S(2)}) collective-permute-start(bf16[1,128,256]{2,1,0:T(8,128)(2,1)S(1)} %get-tuple-element.70), channel_id=1, source_target_pairs={{0,480},{32,0},{64,32},{96,64},{128,96},{160,128},{192,160},{224,1... | collective-permute-start | bytes 196616 | tf_op jit(solution)/shard_map/ppermute | solution.py:18
  (95 shorter events, 30.0 us)
Async XLA Ops:
  7.2 14.4 %copy-start.5 = (s32[1,2,2,2]{3,2,1,0:T(2,128)S(1)}, s32[1,2,2,2]{3,2,1,0:T(2,128)}, u32[]{:S(2)}) copy-start(s32[1,2,2,2]{3,2,1,0:T(2,128)} %param.9) | copy-start | bytes 100
  7.2 97.9 %all-gather.2.cloned.1.call-start = ((), (), s32[]{:S(2)}) async-start(), calls=%async_computation.3 | async-start | bytes 7077888 | tf_op jit(solution)/shard_map/all_gather | solution.py:97
  105.1 2.2 slice-start
  105.1 2.9 copy-start.1
  109.3 10.8 %collective-permute-start.2 = (bf16[256,256]{1,0:T(8,128)(2,1)S(1)}, bf16[256,256]{1,0:T(8,128)(2,1)S(1)}, u32[]{:S(2)}, u32[]{:S(2)}) collective-permute-start(bf16[256,256]{1,0:T(8,128)(2,1)S(1)} %get-tuple-element.37), channel_id=1, source_target_pairs={{384,0},{385,1},{386,2},{387,3},{388,4},{389,5},{390,6},{391,7},{3... | collective-permute-start | bytes 393224 | tf_op jit(solution)/shard_map/ppermute | solution.py:127
  110.6 9.5 %collective-permute-start.1 = (bf16[256,256]{1,0:T(8,128)(2,1)S(1)}, bf16[256,256]{1,0:T(8,128)(2,1)S(1)}, u32[]{:S(2)}, u32[]{:S(2)}) collective-permute-start(bf16[256,256]{1,0:T(8,128)(2,1)S(1)} %get-tuple-element.37), channel_id=1, source_target_pairs={{384,128},{385,129},{386,130},{387,131},{388,132},{389,133},{390,1... | collective-permute-start | bytes 393224 | tf_op jit(solution)/shard_map/ppermute | solution.py:127
  111.3 8.8 %collective-permute-start = (bf16[256,256]{1,0:T(8,128)(2,1)S(1)}, bf16[256,256]{1,0:T(8,128)(2,1)S(1)}, u32[]{:S(2)}, u32[]{:S(2)}) collective-permute-start(bf16[256,256]{1,0:T(8,128)(2,1)S(1)} %get-tuple-element.37), channel_id=1, source_target_pairs={{384,256},{385,257},{386,258},{387,259},{388,260},{389,261},{390,2... | collective-permute-start | bytes 393224 | tf_op jit(solution)/shard_map/ppermute | solution.py:127
  141.3 3.4 %copy-start = (bf16[1,2,8192,128]{3,2,1,0:T(8,128)(2,1)S(1)}, bf16[1,2,8192,128]{3,2,1,0:T(8,128)(2,1)}, u32[]{:S(2)}) copy-start(bf16[1,2,8192,128]{3,2,1,0:T(8,128)(2,1)} %param.8) | copy-start | bytes 12582916
  148.1 2.2 copy-start.2
  152.7 53.7 %all-to-all-start = ((bf16[4,8,2,256,128]{3,1,4,2,0:T(8,128)(2,1)}), bf16[4,8,2,256,128]{3,1,4,2,0:T(8,128)(2,1)}, u32[]{:S(2)}, u32[]{:S(2)}) async-start(bf16[4,8,2,256,128]{3,1,4,2,0:T(8,128)(2,1)} %maximum_bitcast_fusion), calls=%async_computation | async-start | bytes 8388608 | tf_op jit(solution)/shard_map/all_to_all | solution.py:65
  206.4 24.3 %all-to-all-start.1 = ((bf16[16,64,256]{2,1,0:T(8,128)(2,1)}), bf16[16,64,256]{2,1,0:T(8,128)(2,1)S(1)}, u32[]{:S(2)}, u32[]{:S(2)}) async-start(bf16[16,64,256]{2,1,0:T(8,128)(2,1)} %bitcast.25), calls=%async_computation.1 | async-start | bytes 1048576 | tf_op jit(solution)/shard_map/all_to_all | solution.py:79
  218.7 19.5 %collective-permute-start.3 = (f32[2,256,64]{1,2,0:T(8,128)S(1)}, f32[2,256,64]{1,2,0:T(8,128)S(1)}, u32[]{:S(2)}, u32[]{:S(2)}) collective-permute-start(f32[2,256,64]{1,2,0:T(8,128)S(1)} %bitcast.126), channel_id=1, source_target_pairs={{0,4},{4,8},{8,12},{12,16},{16,20},{20,24},{24,28},{28,0},{1,5},{5... | collective-permute-start | bytes 393224 | tf_op jit(solution)/shard_map/ppermute | solution.py:52
  231.6 60.4 %all-to-all-start.2 = ((bf16[16,64,256]{2,1,0:T(8,128)(2,1)}), bf16[16,64,256]{2,1,0:T(8,128)(2,1)S(1)}, u32[]{:S(2)}, u32[]{:S(2)}) async-start(bf16[16,64,256]{2,1,0:T(8,128)(2,1)} %broadcast_in_dim.5), calls=%async_computation.2 | async-start | bytes 1048576 | tf_op jit(solution)/shard_map/all_to_all | solution.py:82
  235.1 7.4 %collective-permute-start.10 = (f32[2,256,64]{1,2,0:T(8,128)S(1)}, f32[2,256,64]{1,2,0:T(8,128)S(1)}, u32[]{:S(2)}, u32[]{:S(2)}) collective-permute-start(f32[2,256,64]{1,2,0:T(8,128)S(1)} %bitcast.127), channel_id=1, source_target_pairs={{0,28},{4,0},{8,4},{12,8},{16,12},{20,16},{24,20},{28,24},{1,29},{... | collective-permute-start | bytes 393224 | tf_op jit(solution)/shard_map/ppermute | solution.py:53
  238.2 8.6 %collective-permute-start.4 = (f32[2,256,64]{1,2,0:T(8,128)S(1)}, f32[2,256,64]{1,2,0:T(8,128)S(1)}, u32[]{:S(2)}, u32[]{:S(2)}) collective-permute-start(f32[2,256,64]{1,2,0:T(8,128)S(1)} %bitcast_add_fusion.13), channel_id=1, source_target_pairs={{0,4},{4,8},{8,12},{12,16},{16,20},{20,24},{24,28},{28,0},{1,5},{5... | collective-permute-start | bytes 393224 | tf_op jit(solution)/shard_map/ppermute | solution.py:52
  242.5 6.8 %collective-permute-start.11 = (f32[2,256,64]{1,2,0:T(8,128)S(1)}, f32[2,256,64]{1,2,0:T(8,128)S(1)}, u32[]{:S(2)}, u32[]{:S(2)}) collective-permute-start(f32[2,256,64]{1,2,0:T(8,128)S(1)} %bitcast_add_fusion.6), channel_id=1, source_target_pairs={{0,28},{4,0},{8,4},{12,8},{16,12},{20,16},{24,20},{28,24},{1,29},{... | collective-permute-start | bytes 393224 | tf_op jit(solution)/shard_map/ppermute | solution.py:53
  246.8 7.8 %collective-permute-start.5 = (f32[2,256,64]{1,2,0:T(8,128)S(1)}, f32[2,256,64]{1,2,0:T(8,128)S(1)}, u32[]{:S(2)}, u32[]{:S(2)}) collective-permute-start(f32[2,256,64]{1,2,0:T(8,128)S(1)} %bitcast_add_fusion.12), channel_id=1, source_target_pairs={{0,4},{4,8},{8,12},{12,16},{16,20},{20,24},{24,28},{28,0},{1,5},{5... | collective-permute-start | bytes 393224 | tf_op jit(solution)/shard_map/ppermute | solution.py:52
  249.3 7.5 %collective-permute-start.12 = (f32[2,256,64]{1,2,0:T(8,128)S(1)}, f32[2,256,64]{1,2,0:T(8,128)S(1)}, u32[]{:S(2)}, u32[]{:S(2)}) collective-permute-start(f32[2,256,64]{1,2,0:T(8,128)S(1)} %bitcast_add_fusion.5), channel_id=1, source_target_pairs={{0,28},{4,0},{8,4},{12,8},{16,12},{20,16},{24,20},{28,24},{1,29},{... | collective-permute-start | bytes 393224 | tf_op jit(solution)/shard_map/ppermute | solution.py:53
  254.7 29.7 %copy-start.3 = (bf16[1,2,128,256]{3,2,1,0:T(8,128)(2,1)S(1)}, bf16[1,2,128,256]{3,2,1,0:T(8,128)(2,1)}, u32[]{:S(2)}) copy-start(bf16[1,2,128,256]{3,2,1,0:T(8,128)(2,1)} %param.6) | copy-start | bytes 393220
  254.7 29.7 %copy-start.4 = (bf16[1,128,256]{2,1,0:T(8,128)(2,1)S(1)}, bf16[1,128,256]{2,1,0:T(8,128)(2,1)}, u32[]{:S(2)}) copy-start(bf16[1,128,256]{2,1,0:T(8,128)(2,1)} %param.7) | copy-start | bytes 196612
  254.7 7.1 %collective-permute-start.6 = (f32[2,256,64]{1,2,0:T(8,128)S(1)}, f32[2,256,64]{1,2,0:T(8,128)S(1)}, u32[]{:S(2)}, u32[]{:S(2)}) collective-permute-start(f32[2,256,64]{1,2,0:T(8,128)S(1)} %bitcast_add_fusion.11), channel_id=1, source_target_pairs={{0,4},{4,8},{8,12},{12,16},{16,20},{20,24},{24,28},{28,0},{1,5},{5... | collective-permute-start | bytes 393224 | tf_op jit(solution)/shard_map/ppermute | solution.py:52
  256.8 6.9 %collective-permute-start.13 = (f32[2,256,64]{1,2,0:T(8,128)S(1)}, f32[2,256,64]{1,2,0:T(8,128)S(1)}, u32[]{:S(2)}, u32[]{:S(2)}) collective-permute-start(f32[2,256,64]{1,2,0:T(8,128)S(1)} %bitcast_add_fusion.4), channel_id=1, source_target_pairs={{0,28},{4,0},{8,4},{12,8},{16,12},{20,16},{24,20},{28,24},{1,29},{... | collective-permute-start | bytes 393224 | tf_op jit(solution)/shard_map/ppermute | solution.py:53
  261.8 6.9 %collective-permute-start.7 = (f32[2,256,64]{1,2,0:T(8,128)S(1)}, f32[2,256,64]{1,2,0:T(8,128)S(1)}, u32[]{:S(2)}, u32[]{:S(2)}) collective-permute-start(f32[2,256,64]{1,2,0:T(8,128)S(1)} %bitcast_add_fusion.10), channel_id=1, source_target_pairs={{0,4},{4,8},{8,12},{12,16},{16,20},{20,24},{24,28},{28,0},{1,5},{5... | collective-permute-start | bytes 393224 | tf_op jit(solution)/shard_map/ppermute | solution.py:52
  263.7 6.9 %collective-permute-start.14 = (f32[2,256,64]{1,2,0:T(8,128)S(1)}, f32[2,256,64]{1,2,0:T(8,128)S(1)}, u32[]{:S(2)}, u32[]{:S(2)}) collective-permute-start(f32[2,256,64]{1,2,0:T(8,128)S(1)} %bitcast_add_fusion.3), channel_id=1, source_target_pairs={{0,28},{4,0},{8,4},{12,8},{16,12},{20,16},{24,20},{28,24},{1,29},{... | collective-permute-start | bytes 393224 | tf_op jit(solution)/shard_map/ppermute | solution.py:53
  268.7 6.9 %collective-permute-start.8 = (f32[2,256,64]{1,2,0:T(8,128)S(1)}, f32[2,256,64]{1,2,0:T(8,128)S(1)}, u32[]{:S(2)}, u32[]{:S(2)}) collective-permute-start(f32[2,256,64]{1,2,0:T(8,128)S(1)} %bitcast_add_fusion.9), channel_id=1, source_target_pairs={{0,4},{4,8},{8,12},{12,16},{16,20},{20,24},{24,28},{28,0},{1,5},{5... | collective-permute-start | bytes 393224 | tf_op jit(solution)/shard_map/ppermute | solution.py:52
  270.7 6.9 %collective-permute-start.15 = (f32[2,256,64]{1,2,0:T(8,128)S(1)}, f32[2,256,64]{1,2,0:T(8,128)S(1)}, u32[]{:S(2)}, u32[]{:S(2)}) collective-permute-start(f32[2,256,64]{1,2,0:T(8,128)S(1)} %bitcast_add_fusion.2), channel_id=1, source_target_pairs={{0,28},{4,0},{8,4},{12,8},{16,12},{20,16},{24,20},{28,24},{1,29},{... | collective-permute-start | bytes 393224 | tf_op jit(solution)/shard_map/ppermute | solution.py:53
  275.6 6.9 %collective-permute-start.9 = (f32[2,256,64]{1,2,0:T(8,128)S(1)}, f32[2,256,64]{1,2,0:T(8,128)S(1)}, u32[]{:S(2)}, u32[]{:S(2)}) collective-permute-start(f32[2,256,64]{1,2,0:T(8,128)S(1)} %bitcast_add_fusion.8), channel_id=1, source_target_pairs={{0,4},{4,8},{8,12},{12,16},{16,20},{20,24},{24,28},{28,0},{1,5},{5... | collective-permute-start | bytes 393224 | tf_op jit(solution)/shard_map/ppermute | solution.py:52
  277.6 6.7 %collective-permute-start.16 = (f32[2,256,64]{1,2,0:T(8,128)S(1)}, f32[2,256,64]{1,2,0:T(8,128)S(1)}, u32[]{:S(2)}, u32[]{:S(2)}) collective-permute-start(f32[2,256,64]{1,2,0:T(8,128)S(1)} %bitcast_add_fusion.1), channel_id=1, source_target_pairs={{0,28},{4,0},{8,4},{12,8},{16,12},{20,16},{24,20},{28,24},{1,29},{... | collective-permute-start | bytes 393224 | tf_op jit(solution)/shard_map/ppermute | solution.py:53
  284.4 9.5 %collective-permute-start.18 = (bf16[1,128,256]{2,1,0:T(8,128)(2,1)S(1)}, bf16[1,128,256]{2,1,0:T(8,128)(2,1)S(1)}, u32[]{:S(2)}, u32[]{:S(2)}) collective-permute-start(bf16[1,128,256]{2,1,0:T(8,128)(2,1)S(1)} %get-tuple-element.70), channel_id=1, source_target_pairs={{0,480},{32,0},{64,32},{96,64},{128,96},{160,128},{192,160},{224,1... | collective-permute-start | bytes 196616 | tf_op jit(solution)/shard_map/ppermute | solution.py:18
  291.1 2.9 collective-permute-start.17
Sparse Core Ops, SparseCore 0:
  21.7 83.3 all-gather.1

commit v8 on v7

--- a/solution.py
+++ b/solution.py
@@ -45,14 +45,14 @@
     ahead, behind = chunks[..., :half], chunks[..., half:]
 
     def take(part, offset):
-        return lax.dynamic_index_in_dim(part, (me + offset) % n, 0, keepdims=False)
+        return lax.dynamic_index_in_dim(part, (me + offset) % n, 0, keepdims=False).astype(jnp.float32)
 
     up, down = take(ahead, n - 1), take(behind, 1)
     for step in range(n - 1):
-        up = lax.ppermute(up, axis, [(i, (i + 1) % n) for i in range(n)])
-        down = lax.ppermute(down, axis, [(i, (i - 1) % n) for i in range(n)])
-        up = up + take(ahead, 2 * n - 2 - step)
-        down = down + take(behind, 2 + step)
+        up = lax.ppermute(up.astype(jnp.bfloat16), axis, [(i, (i + 1) % n) for i in range(n)])
+        down = lax.ppermute(down.astype(jnp.bfloat16), axis, [(i, (i - 1) % n) for i in range(n)])
+        up = up.astype(jnp.float32) + take(ahead, 2 * n - 2 - step)
+        down = down.astype(jnp.float32) + take(behind, 2 + step)
     return jnp.concatenate([up, down], axis=-1)
 
 
@@ -61,10 +61,10 @@
     rounded = terms.astype(jnp.bfloat16)
     if isinstance(axis, tuple):
         tall, wide = lax.axis_size(axis[0]), lax.axis_size(axis[1])
-        parts = rounded.reshape(count, tall, wide, width // (tall * wide), tokens).transpose(2, 1, 0, 3, 4)
-        moved = lax.all_to_all(parts, axis[1], 0, 0, tiled=True)
-        partial = jnp.sum(moved.astype(jnp.float32), axis=0)
-        summed = ring_sum(partial, axis[0])
+        parts = rounded.reshape(count, tall, wide, width // (tall * wide), tokens).transpose(1, 2, 0, 3, 4)
+        partial = ring_sum(parts, axis[0])
+        moved = lax.all_to_all(partial, axis[1], 0, 0, tiled=True)
+        summed = jnp.sum(moved, axis=0)
     else:
         devices = lax.axis_size(axis)
         parts = rounded.reshape(count, devices, width // devices, tokens).transpose(1, 0, 2, 3)

time: 305 us -> 298 us (0.977)
  waiting for transfers between devices: 147 us -> 130 us
  other arithmetic: 7.39 us -> 16.2 us
    all_to_all x1, waiting for transfers between devices: 46 us -> 15 us  [head_sum(): moved = lax.all_to_all(partial, axis[1], 0, 0, tiled=True)]
    all_to_all x1, waiting for transfers between devices: 0.01 us -> 15.4 us  [segment_sum(): return lax.all_to_all(spread, axis, 0, 0, tiled=True).reshape(contrib.shape)]
    convert_element_type x0 -> x12, other arithmetic: none -> 10.1 us  [the longest x6 6.09 us: ring_sum(): up.astype(jnp.bfloat16)]
    all_to_all x1, waiting for transfers between devices: 10.1 us -> 1.32 us  [segment_sum(): moved = lax.all_to_all(parts, axis, 0, 0, tiled=True)]
    ppermute x14, waiting for transfers between devices: 5.02 us -> 13.1 us  [the longest x7 12.2 us: ring_sum(): lax.ppermute(up.astype(jnp.bfloat16), axis, [(i, (i + 1) % n) for i in ra...]
    ppermute x2, starting transfers between devices: 7.6 us -> 1.76 us  [from_behind(): lax.ppermute(x, axis, [(i, (i + by) % devices) for i in range(devices)])]
    all_to_all x1, starting transfers between devices: 6.97 us -> 10.5 us  [segment_sum(): moved = lax.all_to_all(parts, axis, 0, 0, tiled=True)]
  transfers between devices with their start and end apart: 23 -> 23, of which waited for: 12 -> 10; matrix products, arithmetic and copies ran while one was open for 6% -> 9% of each run, Pallas kernels for 0% -> 0%
where the time goes in v8:
time: 298 us; the launch traced here: 296 us
  waiting for transfers between devices  130 us (44%)
  starting transfers between devices  70.5 us (24%)
  local copies, waits for them, and re-layouts  27.1 us (9%)
  blocking collectives  26.4 us (9%)
  other arithmetic  16.2 us (5%)
  between operations  14.7 us (5%)
  matrix products  11.8 us (4%)
    all_gather x1, waiting for transfers between devices, per_device(): gathered = lax.all_gather(gathered, stage, axis=2, tiled=True)  79.5 us
    ppermute x7, starting transfers between devices, ring_sum(): lax.ppermute(down.astype(jnp.bfloat16), axis, [(i, (i - 1) % n) for i in...  31.8 us
    all_to_all x1, waiting for transfers between devices, segment_sum(): return lax.all_to_all(spread, axis, 0, 0, tiled=True).reshape(contrib.shape)  15.4 us
    all_to_all x1, waiting for transfers between devices, head_sum(): moved = lax.all_to_all(partial, axis[1], 0, 0, tiled=True)  15 us
    ppermute x7, starting transfers between devices, ring_sum(): lax.ppermute(up.astype(jnp.bfloat16), axis, [(i, (i + 1) % n) for i in ra...  13.6 us
    all_gather x1, blocking collectives, per_device(): gathered = lax.all_gather(gathered, stage, axis=2, tiled=True)  13.3 us
    all_gather x1, blocking collectives, per_device(): lax.all_gather(piece, 'sr', axis=0, tiled=True)  13.1 us
    another operation x4, local copies, waits for them, and re-layouts, per_device(): jnp.stack([lax.dot_general(w_out, mixed_flat, (((1,), (1,)), ((), ())), p...  12.7 us
  transfers between devices with their start and end apart: 23, of which 10 were waited for; matrix products, arithmetic and copies ran while one was open for 9% of the time, Pallas kernels for 0%

profile of v8, /device:TPU:1, one launch (start us, length us, event | category | flops | bytes accessed | tf_op | source)
XLA Modules:
  0.0 296.4 jit_solution(10560024358476198536)
XLA Ops:
  8.2 13.3 %all_gather.9 = bf16[3,128,1024]{2,1,0:T(8,128)(2,1)} all-gather(bf16[3,128,256]{2,1,0:T(8,128)(2,1)S(1)} %pad_maximum_fusion.3), channel_id=1, replica_groups=mesh['sg'=4,'sr'=4,'my'=8,'mx'=4] {'mx'}, dimensions={2}, use_global_device_ids=true | all-gather | bytes 983040 | tf_op jit(solution)/shard_map/all_gather | solution.py:97
  21.8 3.9 %slice_bitcast_fusion.2 = (bf16[8192,128]{1,0:T(8,128)(2,1)}, bf16[8192,128]{1,0:T(8,128)(2,1)S(1)}) fusion(bf16[1,2,8192,128]{3,2,1,0:T(8,128)(2,1)} %param.8), kind=kLoop, calls=%fused_computation.15 | loop fusion | bytes 8388608 | tf_op jit(solution)/shard_map/squeeze | solution.py:103
  25.6 79.5 %all-gather.2.cloned.1.call-done = bf16[3,128,8192]{2,1,0:T(8,128)(2,1)} async-done(((bf16[3,128,1024]{2,1,0:T(8,128)(2,1)}), bf16[3,128,8192]{2,1,0:T(8,128)(2,1)}) %all-gather.2.cloned.1.call-update) | async-done | bytes 6291472 | tf_op jit(solution)/shard_map/all_gather | solution.py:97
  105.1 2.2 slice-done
  112.0 2.9 fusion.12
  114.9 5.2 %collective-permute-done.2 = bf16[256,256]{1,0:T(8,128)(2,1)S(1)} collective-permute-done((bf16[256,256]{1,0:T(8,128)(2,1)S(1)}, bf16[256,256]{1,0:T(8,128)(2,1)S(1)}, u32[]{:S(2)}, u32[]{:S(2)}) %collective-permute-start.2) | collective-permute-done | bytes 131104 | tf_op jit(solution)/shard_map/ppermute | solution.py:127
  120.1 13.1 %all_gather.11 = bf16[1024,256]{1,0:T(8,128)(2,1)S(1)} all-gather(bf16[256,256]{1,0:T(8,128)(2,1)S(1)} %select_select_fusion), channel_id=1, replica_groups=mesh['sg'=4,'sr'=4,'my'=8,'mx'=4] {'sr'}, dimensions={0}, use_global_device_ids=true | all-gather | bytes 655360 | tf_op jit(solution)/shard_map/all_gather | solution.py:129
  136.2 2.3 fusion.3
  138.5 2.8 stack.10
  141.3 4.2 %copy.30 = bf16[1,8,4,256,128]{3,4,0,2,1:T(8,128)(2,1)} copy(bf16[1,8,4,256,128]{3,2,1,4,0:T(4,128)(2,1)} %stack.10) | data formatting | bytes 4194304 | tf_op jit(solution)/shard_map/stack | solution.py:156
  146.3 2.8 stack.9
  149.1 2.9 copy.29
  154.2 1.9 collective-permute-start.3
  156.2 4.6 %collective-permute-start.10 = (bf16[4,2,256,64]{2,3,1,0:T(8,128)(2,1)S(1)}, bf16[4,2,256,64]{2,3,1,0:T(8,128)(2,1)S(1)}, u32[]{:S(2)}, u32[]{:S(2)}) collective-permute-start(bf16[4,2,256,64]{2,3,1,0:T(8,128)(2,1)S(1)} %dynamic-slice_bitcast_fusion), channel_id=1, source_target_pairs={{0,28},{4,0},{8,4},{12,8},{16,12},{20,16},{24,20},{28,24},{1,29},{... | collective-permute-start | bytes 786440 | tf_op jit(solution)/shard_map/ppermute | solution.py:53
  160.8 4.3 %collective-permute-done.3 = bf16[4,2,256,64]{2,3,1,0:T(8,128)(2,1)S(1)} collective-permute-done((bf16[4,2,256,64]{2,3,1,0:T(8,128)(2,1)S(1)}, bf16[4,2,256,64]{2,3,1,0:T(8,128)(2,1)S(1)}, u32[]{:S(2)}, u32[]{:S(2)}) %collective-permute-start.3) | collective-permute-done | bytes 262176 | tf_op jit(solution)/shard_map/ppermute | solution.py:52
  166.0 2.1 collective-permute-start.4
  168.2 4.4 %collective-permute-start.11 = (bf16[4,2,256,64]{2,3,1,0:T(8,128)(2,1)S(1)}, bf16[4,2,256,64]{2,3,1,0:T(8,128)(2,1)S(1)}, u32[]{:S(2)}, u32[]{:S(2)}) collective-permute-start(bf16[4,2,256,64]{2,3,1,0:T(8,128)(2,1)S(1)} %fusion.18), channel_id=1, source_target_pairs={{0,28},{4,0},{8,4},{12,8},{16,12},{20,16},{24,20},{28,24},{1,29},{... | collective-permute-start | bytes 786440 | tf_op jit(solution)/shard_map/ppermute | solution.py:53
  172.9 3.1 %collective-permute-done.4 = bf16[4,2,256,64]{2,3,1,0:T(8,128)(2,1)S(1)} collective-permute-done((bf16[4,2,256,64]{2,3,1,0:T(8,128)(2,1)S(1)}, bf16[4,2,256,64]{2,3,1,0:T(8,128)(2,1)S(1)}, u32[]{:S(2)}, u32[]{:S(2)}) %collective-permute-start.4) | collective-permute-done | bytes 262176 | tf_op jit(solution)/shard_map/ppermute | solution.py:52
  177.0 1.9 collective-permute-start.5
  179.0 4.6 %collective-permute-start.12 = (bf16[4,2,256,64]{2,3,1,0:T(8,128)(2,1)S(1)}, bf16[4,2,256,64]{2,3,1,0:T(8,128)(2,1)S(1)}, u32[]{:S(2)}, u32[]{:S(2)}) collective-permute-start(bf16[4,2,256,64]{2,3,1,0:T(8,128)(2,1)S(1)} %fusion.17), channel_id=1, source_target_pairs={{0,28},{4,0},{8,4},{12,8},{16,12},{20,16},{24,20},{28,24},{1,29},{... | collective-permute-start | bytes 786440 | tf_op jit(solution)/shard_map/ppermute | solution.py:53
  187.0 1.9 collective-permute-start.6
  189.8 4.6 %collective-permute-start.13 = (bf16[4,2,256,64]{2,3,1,0:T(8,128)(2,1)}, bf16[4,2,256,64]{2,3,1,0:T(8,128)(2,1)}, u32[]{:S(2)}, u32[]{:S(2)}) collective-permute-start(bf16[4,2,256,64]{2,3,1,0:T(8,128)(2,1)} %fusion.16), channel_id=1, source_target_pairs={{0,28},{4,0},{8,4},{12,8},{16,12},{20,16},{24,20},{28,24},{1,29},{... | collective-permute-start | bytes 786440 | tf_op jit(solution)/shard_map/ppermute | solution.py:53
  197.1 1.9 collective-permute-start.7
  200.1 4.6 %collective-permute-start.14 = (bf16[4,2,256,64]{2,3,1,0:T(8,128)(2,1)S(1)}, bf16[4,2,256,64]{2,3,1,0:T(8,128)(2,1)}, u32[]{:S(2)}, u32[]{:S(2)}) collective-permute-start(bf16[4,2,256,64]{2,3,1,0:T(8,128)(2,1)S(1)} %fusion.15), channel_id=1, source_target_pairs={{0,28},{4,0},{8,4},{12,8},{16,12},{20,16},{24,20},{28,24},{1,29},{... | collective-permute-start | bytes 786440 | tf_op jit(solution)/shard_map/ppermute | solution.py:53
  210.1 4.6 %collective-permute-start.15 = (bf16[4,2,256,64]{2,3,1,0:T(8,128)(2,1)S(1)}, bf16[4,2,256,64]{2,3,1,0:T(8,128)(2,1)}, u32[]{:S(2)}, u32[]{:S(2)}) collective-permute-start(bf16[4,2,256,64]{2,3,1,0:T(8,128)(2,1)S(1)} %fusion.14), channel_id=1, source_target_pairs={{0,28},{4,0},{8,4},{12,8},{16,12},{20,16},{24,20},{28,24},{1,29},{... | collective-permute-start | bytes 786440 | tf_op jit(solution)/shard_map/ppermute | solution.py:53
  216.1 10.5 %all-to-all-start.1 = ((bf16[16,64,256]{2,1,0:T(8,128)(2,1)}), bf16[16,64,256]{2,1,0:T(8,128)(2,1)S(1)}, u32[]{:S(2)}, u32[]{:S(2)}) async-start(bf16[16,64,256]{2,1,0:T(8,128)(2,1)} %bitcast.41), calls=%async_computation.1 | async-start | bytes 1048576 | tf_op jit(solution)/shard_map/all_to_all | solution.py:79
  230.6 4.6 %collective-permute-start.16 = (bf16[4,2,256,64]{2,3,1,0:T(8,128)(2,1)S(1)}, bf16[4,2,256,64]{2,3,1,0:T(8,128)(2,1)}, u32[]{:S(2)}, u32[]{:S(2)}) collective-permute-start(bf16[4,2,256,64]{2,3,1,0:T(8,128)(2,1)S(1)} %fusion.13), channel_id=1, source_target_pairs={{0,28},{4,0},{8,4},{12,8},{16,12},{20,16},{24,20},{28,24},{1,29},{... | collective-permute-start | bytes 786440 | tf_op jit(solution)/shard_map/ppermute | solution.py:53
  235.3 3.4 %collective-permute-done.9 = bf16[4,2,256,64]{2,3,1,0:T(8,128)(2,1)S(1)} collective-permute-done((bf16[4,2,256,64]{2,3,1,0:T(8,128)(2,1)S(1)}, bf16[4,2,256,64]{2,3,1,0:T(8,128)(2,1)S(1)}, u32[]{:S(2)}, u32[]{:S(2)}) %collective-permute-start.9) | collective-permute-done | bytes 262176 | tf_op jit(solution)/shard_map/ppermute | solution.py:52
  244.0 4.0 %all-to-all-start = ((f32[4,2,256,128]{2,3,1,0:T(8,128)}), f32[4,2,256,128]{2,3,1,0:T(8,128)S(1)}, u32[]{:S(2)}, u32[]{:S(2)}) async-start(f32[4,2,256,128]{2,3,1,0:T(8,128)} %pad_maximum_fusion.1), calls=%async_computation | async-start | bytes 2097152 | tf_op jit(solution)/shard_map/all_to_all | solution.py:66
  248.0 15.0 %all-to-all-done = f32[4,2,256,128]{2,3,1,0:T(8,128)S(1)} async-done(((f32[4,2,256,128]{2,3,1,0:T(8,128)}), f32[4,2,256,128]{2,3,1,0:T(8,128)S(1)}, u32[]{:S(2)}, u32[]{:S(2)}) %all-to-all-start) | async-done | bytes 1048608 | tf_op jit(solution)/shard_map/all_to_all | solution.py:66
  263.9 6.2 %all-to-all-start.2 = ((bf16[16,64,256]{2,1,0:T(8,128)(2,1)}), bf16[16,64,256]{2,1,0:T(8,128)(2,1)S(1)}, u32[]{:S(2)}, u32[]{:S(2)}) async-start(bf16[16,64,256]{2,1,0:T(8,128)(2,1)} %broadcast_in_dim.5), calls=%async_computation.2 | async-start | bytes 1048576 | tf_op jit(solution)/shard_map/all_to_all | solution.py:82
  271.9 15.4 %all-to-all-done.2 = bf16[16,64,256]{2,1,0:T(8,128)(2,1)S(1)} async-done(((bf16[16,64,256]{2,1,0:T(8,128)(2,1)}), bf16[16,64,256]{2,1,0:T(8,128)(2,1)S(1)}, u32[]{:S(2)}, u32[]{:S(2)}) %all-to-all-start.2) | async-done | bytes 524320 | tf_op jit(solution)/shard_map/all_to_all | solution.py:82
  (100 shorter events, 44.4 us)
Async XLA Ops:
  7.2 14.4 %copy-start.7 = (s32[1,2,2,2]{3,2,1,0:T(2,128)S(1)}, s32[1,2,2,2]{3,2,1,0:T(2,128)}, u32[]{:S(2)}) copy-start(s32[1,2,2,2]{3,2,1,0:T(2,128)} %param.9) | copy-start | bytes 100
  7.2 97.9 %all-gather.2.cloned.1.call-start = ((), (), s32[]{:S(2)}) async-start(), calls=%async_computation.3 | async-start | bytes 7077888 | tf_op jit(solution)/shard_map/all_gather | solution.py:97
  105.1 2.2 slice-start
  105.1 2.9 copy-start.2
  109.3 10.8 %collective-permute-start.2 = (bf16[256,256]{1,0:T(8,128)(2,1)S(1)}, bf16[256,256]{1,0:T(8,128)(2,1)S(1)}, u32[]{:S(2)}, u32[]{:S(2)}) collective-permute-start(bf16[256,256]{1,0:T(8,128)(2,1)S(1)} %get-tuple-element.37), channel_id=1, source_target_pairs={{384,0},{385,1},{386,2},{387,3},{388,4},{389,5},{390,6},{391,7},{3... | collective-permute-start | bytes 393224 | tf_op jit(solution)/shard_map/ppermute | solution.py:127
  110.6 9.5 %collective-permute-start.1 = (bf16[256,256]{1,0:T(8,128)(2,1)S(1)}, bf16[256,256]{1,0:T(8,128)(2,1)S(1)}, u32[]{:S(2)}, u32[]{:S(2)}) collective-permute-start(bf16[256,256]{1,0:T(8,128)(2,1)S(1)} %get-tuple-element.37), channel_id=1, source_target_pairs={{384,128},{385,129},{386,130},{387,131},{388,132},{389,133},{390,1... | collective-permute-start | bytes 393224 | tf_op jit(solution)/shard_map/ppermute | solution.py:127
  111.3 8.8 %collective-permute-start = (bf16[256,256]{1,0:T(8,128)(2,1)S(1)}, bf16[256,256]{1,0:T(8,128)(2,1)S(1)}, u32[]{:S(2)}, u32[]{:S(2)}) collective-permute-start(bf16[256,256]{1,0:T(8,128)(2,1)S(1)} %get-tuple-element.37), channel_id=1, source_target_pairs={{384,256},{385,257},{386,258},{387,259},{388,260},{389,261},{390,2... | collective-permute-start | bytes 393224 | tf_op jit(solution)/shard_map/ppermute | solution.py:127
  114.9 21.0 %copy-start.8 = (bf16[128,128]{1,0:T(8,128)(2,1)}, bf16[128,128]{1,0:T(8,128)(2,1)S(1)}, u32[]{:S(2)}) copy-start(bf16[128,128]{1,0:T(8,128)(2,1)S(1)} %fusion.12) | copy-start | bytes 98308
  141.3 4.2 %copy-start = (bf16[1,2,8192,128]{3,2,1,0:T(8,128)(2,1)S(1)}, bf16[1,2,8192,128]{3,2,1,0:T(8,128)(2,1)}, u32[]{:S(2)}) copy-start(bf16[1,2,8192,128]{3,2,1,0:T(8,128)(2,1)} %param.8) | copy-start | bytes 12582916
  149.1 2.9 copy-start.3
  154.2 10.9 %collective-permute-start.3 = (bf16[4,2,256,64]{2,3,1,0:T(8,128)(2,1)S(1)}, bf16[4,2,256,64]{2,3,1,0:T(8,128)(2,1)S(1)}, u32[]{:S(2)}, u32[]{:S(2)}) collective-permute-start(bf16[4,2,256,64]{2,3,1,0:T(8,128)(2,1)S(1)} %dynamic-slice_bitcast_fusion.1), channel_id=1, source_target_pairs={{0,4},{4,8},{8,12},{12,16},{16,20},{20,24},{24,28},{28,0},{1,5},{5... | collective-permute-start | bytes 786440 | tf_op jit(solution)/shard_map/ppermute | solution.py:52
  156.2 12.0 %collective-permute-start.10 = (bf16[4,2,256,64]{2,3,1,0:T(8,128)(2,1)S(1)}, bf16[4,2,256,64]{2,3,1,0:T(8,128)(2,1)S(1)}, u32[]{:S(2)}, u32[]{:S(2)}) collective-permute-start(bf16[4,2,256,64]{2,3,1,0:T(8,128)(2,1)S(1)} %dynamic-slice_bitcast_fusion), channel_id=1, source_target_pairs={{0,28},{4,0},{8,4},{12,8},{16,12},{20,16},{24,20},{28,24},{1,29},{... | collective-permute-start | bytes 786440 | tf_op jit(solution)/shard_map/ppermute | solution.py:53
  166.0 9.9 %collective-permute-start.4 = (bf16[4,2,256,64]{2,3,1,0:T(8,128)(2,1)S(1)}, bf16[4,2,256,64]{2,3,1,0:T(8,128)(2,1)S(1)}, u32[]{:S(2)}, u32[]{:S(2)}) collective-permute-start(bf16[4,2,256,64]{2,3,1,0:T(8,128)(2,1)S(1)} %fusion.24), channel_id=1, source_target_pairs={{0,4},{4,8},{8,12},{12,16},{16,20},{20,24},{24,28},{28,0},{1,5},{5... | collective-permute-start | bytes 786440 | tf_op jit(solution)/shard_map/ppermute | solution.py:52
  168.2 10.7 %collective-permute-start.11 = (bf16[4,2,256,64]{2,3,1,0:T(8,128)(2,1)S(1)}, bf16[4,2,256,64]{2,3,1,0:T(8,128)(2,1)S(1)}, u32[]{:S(2)}, u32[]{:S(2)}) collective-permute-start(bf16[4,2,256,64]{2,3,1,0:T(8,128)(2,1)S(1)} %fusion.18), channel_id=1, source_target_pairs={{0,28},{4,0},{8,4},{12,8},{16,12},{20,16},{24,20},{28,24},{1,29},{... | collective-permute-start | bytes 786440 | tf_op jit(solution)/shard_map/ppermute | solution.py:53
  177.0 9.0 %collective-permute-start.5 = (bf16[4,2,256,64]{2,3,1,0:T(8,128)(2,1)S(1)}, bf16[4,2,256,64]{2,3,1,0:T(8,128)(2,1)S(1)}, u32[]{:S(2)}, u32[]{:S(2)}) collective-permute-start(bf16[4,2,256,64]{2,3,1,0:T(8,128)(2,1)S(1)} %fusion.23), channel_id=1, source_target_pairs={{0,4},{4,8},{8,12},{12,16},{16,20},{20,24},{24,28},{28,0},{1,5},{5... | collective-permute-start | bytes 786440 | tf_op jit(solution)/shard_map/ppermute | solution.py:52
  179.0 9.9 %collective-permute-start.12 = (bf16[4,2,256,64]{2,3,1,0:T(8,128)(2,1)S(1)}, bf16[4,2,256,64]{2,3,1,0:T(8,128)(2,1)S(1)}, u32[]{:S(2)}, u32[]{:S(2)}) collective-permute-start(bf16[4,2,256,64]{2,3,1,0:T(8,128)(2,1)S(1)} %fusion.17), channel_id=1, source_target_pairs={{0,28},{4,0},{8,4},{12,8},{16,12},{20,16},{24,20},{28,24},{1,29},{... | collective-permute-start | bytes 786440 | tf_op jit(solution)/shard_map/ppermute | solution.py:53
  187.0 9.0 %collective-permute-start.6 = (bf16[4,2,256,64]{2,3,1,0:T(8,128)(2,1)S(1)}, bf16[4,2,256,64]{2,3,1,0:T(8,128)(2,1)S(1)}, u32[]{:S(2)}, u32[]{:S(2)}) collective-permute-start(bf16[4,2,256,64]{2,3,1,0:T(8,128)(2,1)S(1)} %fusion.22), channel_id=1, source_target_pairs={{0,4},{4,8},{8,12},{12,16},{16,20},{20,24},{24,28},{28,0},{1,5},{5... | collective-permute-start | bytes 786440 | tf_op jit(solution)/shard_map/ppermute | solution.py:52
  189.0 15.7 %copy-start.6 = (bf16[2,256,128]{1,2,0:T(8,128)(2,1)S(1)}, bf16[2,256,128]{1,2,0:T(8,128)(2,1)}, u32[]{:S(2)}) copy-start(bf16[2,256,128]{1,2,0:T(8,128)(2,1)} %convolution_multiply_fusion) | copy-start | bytes 393220
  189.8 9.3 %collective-permute-start.13 = (bf16[4,2,256,64]{2,3,1,0:T(8,128)(2,1)}, bf16[4,2,256,64]{2,3,1,0:T(8,128)(2,1)}, u32[]{:S(2)}, u32[]{:S(2)}) collective-permute-start(bf16[4,2,256,64]{2,3,1,0:T(8,128)(2,1)} %fusion.16), channel_id=1, source_target_pairs={{0,28},{4,0},{8,4},{12,8},{16,12},{20,16},{24,20},{28,24},{1,29},{... | collective-permute-start | bytes 786440 | tf_op jit(solution)/shard_map/ppermute | solution.py:53
  197.1 9.0 %collective-permute-start.7 = (bf16[4,2,256,64]{2,3,1,0:T(8,128)(2,1)S(1)}, bf16[4,2,256,64]{2,3,1,0:T(8,128)(2,1)S(1)}, u32[]{:S(2)}, u32[]{:S(2)}) collective-permute-start(bf16[4,2,256,64]{2,3,1,0:T(8,128)(2,1)S(1)} %fusion.21), channel_id=1, source_target_pairs={{0,4},{4,8},{8,12},{12,16},{16,20},{20,24},{24,28},{28,0},{1,5},{5... | collective-permute-start | bytes 786440 | tf_op jit(solution)/shard_map/ppermute | solution.py:52
  200.1 9.0 %collective-permute-start.14 = (bf16[4,2,256,64]{2,3,1,0:T(8,128)(2,1)S(1)}, bf16[4,2,256,64]{2,3,1,0:T(8,128)(2,1)}, u32[]{:S(2)}, u32[]{:S(2)}) collective-permute-start(bf16[4,2,256,64]{2,3,1,0:T(8,128)(2,1)S(1)} %fusion.15), channel_id=1, source_target_pairs={{0,28},{4,0},{8,4},{12,8},{16,12},{20,16},{24,20},{28,24},{1,29},{... | collective-permute-start | bytes 786440 | tf_op jit(solution)/shard_map/ppermute | solution.py:53
  207.2 19.5 %collective-permute-start.8 = (bf16[4,2,256,64]{2,3,1,0:T(8,128)(2,1)S(1)}, bf16[4,2,256,64]{2,3,1,0:T(8,128)(2,1)S(1)}, u32[]{:S(2)}, u32[]{:S(2)}) collective-permute-start(bf16[4,2,256,64]{2,3,1,0:T(8,128)(2,1)S(1)} %fusion.20), channel_id=1, source_target_pairs={{0,4},{4,8},{8,12},{12,16},{16,20},{20,24},{24,28},{28,0},{1,5},{5... | collective-permute-start | bytes 786440 | tf_op jit(solution)/shard_map/ppermute | solution.py:52
  210.1 19.5 %collective-permute-start.15 = (bf16[4,2,256,64]{2,3,1,0:T(8,128)(2,1)S(1)}, bf16[4,2,256,64]{2,3,1,0:T(8,128)(2,1)}, u32[]{:S(2)}, u32[]{:S(2)}) collective-permute-start(bf16[4,2,256,64]{2,3,1,0:T(8,128)(2,1)S(1)} %fusion.14), channel_id=1, source_target_pairs={{0,28},{4,0},{8,4},{12,8},{16,12},{20,16},{24,20},{28,24},{1,29},{... | collective-permute-start | bytes 786440 | tf_op jit(solution)/shard_map/ppermute | solution.py:53
  216.1 27.8 %all-to-all-start.1 = ((bf16[16,64,256]{2,1,0:T(8,128)(2,1)}), bf16[16,64,256]{2,1,0:T(8,128)(2,1)S(1)}, u32[]{:S(2)}, u32[]{:S(2)}) async-start(bf16[16,64,256]{2,1,0:T(8,128)(2,1)} %bitcast.41), calls=%async_computation.1 | async-start | bytes 1048576 | tf_op jit(solution)/shard_map/all_to_all | solution.py:79
  227.7 11.0 %collective-permute-start.9 = (bf16[4,2,256,64]{2,3,1,0:T(8,128)(2,1)S(1)}, bf16[4,2,256,64]{2,3,1,0:T(8,128)(2,1)S(1)}, u32[]{:S(2)}, u32[]{:S(2)}) collective-permute-start(bf16[4,2,256,64]{2,3,1,0:T(8,128)(2,1)S(1)} %fusion.19), channel_id=1, source_target_pairs={{0,4},{4,8},{8,12},{12,16},{16,20},{20,24},{24,28},{28,0},{1,5},{5... | collective-permute-start | bytes 786440 | tf_op jit(solution)/shard_map/ppermute | solution.py:52
  230.6 9.9 %collective-permute-start.16 = (bf16[4,2,256,64]{2,3,1,0:T(8,128)(2,1)S(1)}, bf16[4,2,256,64]{2,3,1,0:T(8,128)(2,1)}, u32[]{:S(2)}, u32[]{:S(2)}) collective-permute-start(bf16[4,2,256,64]{2,3,1,0:T(8,128)(2,1)S(1)} %fusion.13), channel_id=1, source_target_pairs={{0,28},{4,0},{8,4},{12,8},{16,12},{20,16},{24,20},{28,24},{1,29},{... | collective-permute-start | bytes 786440 | tf_op jit(solution)/shard_map/ppermute | solution.py:53
  244.0 19.1 %all-to-all-start = ((f32[4,2,256,128]{2,3,1,0:T(8,128)}), f32[4,2,256,128]{2,3,1,0:T(8,128)S(1)}, u32[]{:S(2)}, u32[]{:S(2)}) async-start(f32[4,2,256,128]{2,3,1,0:T(8,128)} %pad_maximum_fusion.1), calls=%async_computation | async-start | bytes 2097152 | tf_op jit(solution)/shard_map/all_to_all | solution.py:66
  247.9 22.2 %copy-start.4 = (bf16[1,2,128,256]{3,2,1,0:T(8,128)(2,1)S(1)}, bf16[1,2,128,256]{3,2,1,0:T(8,128)(2,1)}, u32[]{:S(2)}) copy-start(bf16[1,2,128,256]{3,2,1,0:T(8,128)(2,1)} %param.6) | copy-start | bytes 393220
  247.9 22.2 %copy-start.5 = (bf16[1,128,256]{2,1,0:T(8,128)(2,1)S(1)}, bf16[1,128,256]{2,1,0:T(8,128)(2,1)}, u32[]{:S(2)}) copy-start(bf16[1,128,256]{2,1,0:T(8,128)(2,1)} %param.7) | copy-start | bytes 196612
  263.9 23.5 %all-to-all-start.2 = ((bf16[16,64,256]{2,1,0:T(8,128)(2,1)}), bf16[16,64,256]{2,1,0:T(8,128)(2,1)S(1)}, u32[]{:S(2)}, u32[]{:S(2)}) async-start(bf16[16,64,256]{2,1,0:T(8,128)(2,1)} %broadcast_in_dim.5), calls=%async_computation.2 | async-start | bytes 1048576 | tf_op jit(solution)/shard_map/all_to_all | solution.py:82
  270.2 18.1 %collective-permute-start.18 = (bf16[1,128,256]{2,1,0:T(8,128)(2,1)S(1)}, bf16[1,128,256]{2,1,0:T(8,128)(2,1)S(1)}, u32[]{:S(2)}, u32[]{:S(2)}) collective-permute-start(bf16[1,128,256]{2,1,0:T(8,128)(2,1)S(1)} %get-tuple-element.54), channel_id=1, source_target_pairs={{0,480},{32,0},{64,32},{96,64},{128,96},{160,128},{192,160},{224,1... | collective-permute-start | bytes 196616 | tf_op jit(solution)/shard_map/ppermute | solution.py:18
  270.3 18.0 %collective-permute-start.17 = (bf16[1,128,256]{2,1,0:T(8,128)(2,1)S(1)}, bf16[1,128,256]{2,1,0:T(8,128)(2,1)S(1)}, u32[]{:S(2)}, u32[]{:S(2)}) collective-permute-start(bf16[1,128,256]{2,1,0:T(8,128)(2,1)S(1)} %get-tuple-element.55), channel_id=1, source_target_pairs={{0,32},{32,64},{64,96},{96,128},{128,160},{160,192},{192,224},{224... | collective-permute-start | bytes 196616 | tf_op jit(solution)/shard_map/ppermute | solution.py:18
  (1 other events, 1.3 us)
Sparse Core Ops, SparseCore 0:
  21.7 83.3 all-gather.1

commit v9 on v6

--- a/solution.py
+++ b/solution.py
@@ -39,11 +39,20 @@
 
 
 def head_sum(terms, axis):
-    devices = lax.axis_size(axis)
     count, width, tokens = terms.shape
-    parts = terms.astype(jnp.bfloat16).reshape(count, devices, width // devices, tokens).transpose(1, 0, 2, 3)
-    moved = lax.all_to_all(parts, axis, 0, 0, tiled=True)
-    return jnp.sum(moved.astype(jnp.float32), axis=0).transpose(0, 2, 1)
+    rounded = terms.astype(jnp.bfloat16)
+    if isinstance(axis, tuple):
+        tall, wide = lax.axis_size(axis[0]), lax.axis_size(axis[1])
+        parts = rounded.reshape(count, tall, wide, width // (tall * wide), tokens).transpose(1, 2, 0, 3, 4)
+        partial = lax.psum_scatter(parts, axis[0], scatter_dimension=0, tiled=True)[0]
+        moved = lax.all_to_all(partial.astype(jnp.float32), axis[1], 0, 0, tiled=True)
+        summed = jnp.sum(moved, axis=0)
+    else:
+        devices = lax.axis_size(axis)
+        parts = rounded.reshape(count, devices, width // devices, tokens).transpose(1, 0, 2, 3)
+        moved = lax.all_to_all(parts, axis, 0, 0, tiled=True)
+        summed = jnp.sum(moved.astype(jnp.float32), axis=0)
+    return summed.transpose(0, 2, 1)
 
 
 def segment_sum(contrib, axis):

time: 298 us -> 263 us (0.88)
  waiting for transfers between devices: 201 us -> 160 us
    all_to_all x1, waiting for transfers between devices: 97.5 us -> 14.2 us  [head_sum(): lax.all_to_all(partial.astype(jnp.float32), axis[1], 0, 0, tiled=True)]
    reduce_scatter x0 -> x1, waiting for transfers between devices: none -> 46 us  [head_sum(): lax.psum_scatter(parts, axis[0], scatter_dimension=0, tiled=True)[0]]
    all_to_all x1, waiting for transfers between devices: 6.1 us -> 0.01 us  [segment_sum(): moved = lax.all_to_all(parts, axis, 0, 0, tiled=True)]
    all_to_all x1, starting transfers between devices: 3.67 us -> 9.16 us  [segment_sum(): return lax.all_to_all(spread, axis, 0, 0, tiled=True).reshape(contrib.shape)]
    all_to_all x1, starting transfers between devices: 7.17 us -> 3.98 us  [head_sum(): lax.all_to_all(partial.astype(jnp.float32), axis[1], 0, 0, tiled=True)]
  transfers between devices with their start and end apart: 9 -> 10, of which waited for: 5 -> 5; matrix products, arithmetic and copies ran while one was open for 7% -> 5% of each run, Pallas kernels for 0% -> 0%
where the time goes in v9:
time: 263 us; the launch traced here: 262 us
  waiting for transfers between devices  160 us (61%)
  blocking collectives  26.5 us (10%)
  starting transfers between devices  23.8 us (9%)
  local copies, waits for them, and re-layouts  18.8 us (7%)
  between operations  14.3 us (5%)
  matrix products  11.3 us (4%)
  other arithmetic  7.42 us (3%)
    all_gather x1, waiting for transfers between devices, per_device(): gathered = lax.all_gather(gathered, stage, axis=2, tiled=True)  79.5 us
    reduce_scatter x1, waiting for transfers between devices, head_sum(): lax.psum_scatter(parts, axis[0], scatter_dimension=0, tiled=True)[0]  46 us
    all_to_all x1, waiting for transfers between devices, segment_sum(): return lax.all_to_all(spread, axis, 0, 0, tiled=True).reshape(contrib.shape)  15.4 us
    all_to_all x1, waiting for transfers between devices, head_sum(): lax.all_to_all(partial.astype(jnp.float32), axis[1], 0, 0, tiled=True)  14.2 us
    all_gather x1, blocking collectives, per_device(): gathered = lax.all_gather(gathered, stage, axis=2, tiled=True)  13.3 us
    all_gather x1, blocking collectives, per_device(): lax.all_gather(piece, 'sr', axis=0, tiled=True)  13.1 us
    all_to_all x1, starting transfers between devices, segment_sum(): return lax.all_to_all(spread, axis, 0, 0, tiled=True).reshape(contrib.shape)  9.16 us
    all_to_all x1, starting transfers between devices, segment_sum(): moved = lax.all_to_all(parts, axis, 0, 0, tiled=True)  6.17 us
  transfers between devices with their start and end apart: 10, of which 5 were waited for; matrix products, arithmetic and copies ran while one was open for 5% of the time, Pallas kernels for 0%

profile of v9, /device:TPU:1, one launch (start us, length us, event | category | flops | bytes accessed | tf_op | source)
XLA Modules:
  0.0 262.4 jit_solution(3934175423955182575)
XLA Ops:
  7.2 1.0 pad_maximum_fusion.2
  8.2 13.3 %all_gather.9 = bf16[3,128,1024]{2,1,0:T(8,128)(2,1)} all-gather(bf16[3,128,256]{2,1,0:T(8,128)(2,1)S(1)} %pad_maximum_fusion.2), channel_id=1, replica_groups=mesh['sg'=4,'sr'=4,'my'=8,'mx'=4] {'mx'}, dimensions={2}, use_global_device_ids=true | all-gather | bytes 983040 | tf_op jit(solution)/shard_map/all_gather | solution.py:79
  21.8 3.8 %slice_bitcast_fusion.2 = (bf16[8192,128]{1,0:T(8,128)(2,1)}, bf16[8192,128]{1,0:T(8,128)(2,1)S(1)}) fusion(bf16[1,2,8192,128]{3,2,1,0:T(8,128)(2,1)} %param.8), kind=kLoop, calls=%fused_computation.15 | loop fusion | bytes 8388608 | tf_op jit(solution)/shard_map/squeeze | solution.py:85
  25.7 79.5 %all-gather.2.cloned.1.call-done = bf16[3,128,8192]{2,1,0:T(8,128)(2,1)} async-done(((bf16[3,128,1024]{2,1,0:T(8,128)(2,1)}), bf16[3,128,8192]{2,1,0:T(8,128)(2,1)}) %all-gather.2.cloned.1.call-update) | async-done | bytes 6291472 | tf_op jit(solution)/shard_map/all_gather | solution.py:79
  105.1 2.2 slice-done
  107.3 0.7 copy-done
  108.0 1.3 conditional.1
  108.0 1.3 convolution_convert_fusion
  109.3 1.3 collective-permute-start.2
  110.6 0.7 collective-permute-start.1
  111.3 0.7 collective-permute-start
  112.0 2.9 %fusion.12 = bf16[128,128]{1,0:T(8,128)(2,1)S(1)} fusion(bf16[3,128,8192]{2,1,0:T(8,128)(2,1)} %all-gather.2.cloned.1.call-done, bf16[1,2,8192,128]{3,2,1,0:T(8,128)(2,1)} %param.8), kind=kOutput, calls=%fused_computation.29 | convolution fusion | flops 268451840 | bytes 4227072 | tf_op jit(solution)/shard_map/dot_general | solution.py:128
  114.9 5.2 %collective-permute-done.2 = bf16[256,256]{1,0:T(8,128)(2,1)S(1)} collective-permute-done((bf16[256,256]{1,0:T(8,128)(2,1)S(1)}, bf16[256,256]{1,0:T(8,128)(2,1)S(1)}, u32[]{:S(2)}, u32[]{:S(2)}) %collective-permute-start.2) | collective-permute-done | bytes 131104 | tf_op jit(solution)/shard_map/ppermute | solution.py:109
  120.1 13.1 %all_gather.11 = bf16[1024,256]{1,0:T(8,128)(2,1)S(1)} all-gather(bf16[256,256]{1,0:T(8,128)(2,1)S(1)} %select_select_fusion), channel_id=1, replica_groups=mesh['sg'=4,'sr'=4,'my'=8,'mx'=4] {'sr'}, dimensions={0}, use_global_device_ids=true | all-gather | bytes 655360 | tf_op jit(solution)/shard_map/all_gather | solution.py:111
  136.2 2.3 fusion.3
  138.5 2.5 copy.23
  141.0 2.3 fusion.2
  143.3 2.5 copy.22
  145.8 4.5 %maximum_bitcast_fusion = bf16[8,4,2,256,128]{4,3,2,1,0:T(8,128)(2,1)} fusion(bf16[1,8,4,256,128]{4,3,0,2,1:T(8,128)(2,1)} %bitcast.84, bf16[1,8,4,256,128]{4,3,0,2,1:T(8,128)(2,1)} %bitcast.85), kind=kLoop, calls=%fused_computation.12 | loop fusion | flops 2097152 | bytes 8388608 | tf_op jit(solution)/shard_map/transpose | solution.py:46
  152.3 0.9 copy.20
  153.2 6.2 %all-to-all-start.1 = ((bf16[16,64,256]{2,1,0:T(8,128)(2,1)}), bf16[16,64,256]{2,1,0:T(8,128)(2,1)S(1)}, u32[]{:S(2)}, u32[]{:S(2)}) async-start(bf16[16,64,256]{2,1,0:T(8,128)(2,1)} %bitcast.28), calls=%async_computation.2 | async-start | bytes 1048576 | tf_op jit(solution)/shard_map/all_to_all | solution.py:61
  159.3 46.0 %reduce-scatter.2.cloned.1.call-done = bf16[1,4,2,256,128]{4,3,2,1,0:T(8,128)(2,1)} async-done(((bf16[8,4,2,256,128]{4,3,2,1,0:T(8,128)(2,1)}), bf16[1,4,2,256,128]{4,3,2,1,0:T(8,128)(2,1)}) %reduce-scatter.2.cloned.1.call-update) | async-done | bytes 524304 | tf_op jit(solution)/shard_map/reduce_scatter | solution.py:47
  205.4 1.1 bitcast_convert_fusion
  206.5 1.3 copy.17
  207.8 4.0 %all-to-all-start = ((f32[4,2,256,128]{2,3,1,0:T(8,128)}), f32[4,2,256,128]{2,3,1,0:T(8,128)S(1)}, u32[]{:S(2)}, u32[]{:S(2)}) async-start(f32[4,2,256,128]{2,3,1,0:T(8,128)} %copy.17), calls=%async_computation.1 | async-start | bytes 2097152 | tf_op jit(solution)/shard_map/all_to_all | solution.py:48
  211.9 14.2 %all-to-all-done = f32[4,2,256,128]{2,3,1,0:T(8,128)S(1)} async-done(((f32[4,2,256,128]{2,3,1,0:T(8,128)}), f32[4,2,256,128]{2,3,1,0:T(8,128)S(1)}, u32[]{:S(2)}, u32[]{:S(2)}) %all-to-all-start) | async-done | bytes 1048608 | tf_op jit(solution)/shard_map/all_to_all | solution.py:48
  226.0 0.8 broadcast_in_dim.5
  226.9 9.2 %all-to-all-start.2 = ((bf16[16,64,256]{2,1,0:T(8,128)(2,1)}), bf16[16,64,256]{2,1,0:T(8,128)(2,1)S(1)}, u32[]{:S(2)}, u32[]{:S(2)}) async-start(bf16[16,64,256]{2,1,0:T(8,128)(2,1)} %broadcast_in_dim.5), calls=%async_computation.3 | async-start | bytes 1048576 | tf_op jit(solution)/shard_map/all_to_all | solution.py:64
  236.3 1.6 collective-permute-start.3
  238.0 15.4 %all-to-all-done.2 = bf16[16,64,256]{2,1,0:T(8,128)(2,1)S(1)} async-done(((bf16[16,64,256]{2,1,0:T(8,128)(2,1)}), bf16[16,64,256]{2,1,0:T(8,128)(2,1)S(1)}, u32[]{:S(2)}, u32[]{:S(2)}) %all-to-all-start.2) | async-done | bytes 524320 | tf_op jit(solution)/shard_map/all_to_all | solution.py:64
  253.4 0.9 reshape_reshape.7
  254.3 0.6 copy.32
  (47 shorter events, 6.1 us)
Async XLA Ops:
  7.2 14.5 %copy-start.3 = (s32[1,2,2,2]{3,2,1,0:T(2,128)S(1)}, s32[1,2,2,2]{3,2,1,0:T(2,128)}, u32[]{:S(2)}) copy-start(s32[1,2,2,2]{3,2,1,0:T(2,128)} %param.9) | copy-start | bytes 100
  7.2 97.9 %all-gather.2.cloned.1.call-start = ((), (), s32[]{:S(2)}) async-start(), calls=%async_computation.4 | async-start | bytes 7077888 | tf_op jit(solution)/shard_map/all_gather | solution.py:79
  21.6 183.8 %reduce-scatter.2.cloned.1.call-start = ((), (), s32[]{:S(2)}) async-start(), calls=%async_computation.5 | async-start | bytes 4718592 | tf_op jit(solution)/shard_map/reduce_scatter | solution.py:47
  105.1 2.2 slice-start
  105.1 2.9 %copy-start = (bf16[8192,128]{1,0:T(8,128)(2,1)S(1)}, bf16[8192,128]{1,0:T(8,128)(2,1)}, u32[]{:S(2)}) copy-start(bf16[8192,128]{1,0:T(8,128)(2,1)} %get-tuple-element.50) | copy-start | bytes 6291460
  109.3 10.8 %collective-permute-start.2 = (bf16[256,256]{1,0:T(8,128)(2,1)S(1)}, bf16[256,256]{1,0:T(8,128)(2,1)S(1)}, u32[]{:S(2)}, u32[]{:S(2)}) collective-permute-start(bf16[256,256]{1,0:T(8,128)(2,1)S(1)} %get-tuple-element.37), channel_id=1, source_target_pairs={{384,0},{385,1},{386,2},{387,3},{388,4},{389,5},{390,6},{391,7},{3... | collective-permute-start | bytes 393224 | tf_op jit(solution)/shard_map/ppermute | solution.py:109
  110.6 9.5 %collective-permute-start.1 = (bf16[256,256]{1,0:T(8,128)(2,1)S(1)}, bf16[256,256]{1,0:T(8,128)(2,1)S(1)}, u32[]{:S(2)}, u32[]{:S(2)}) collective-permute-start(bf16[256,256]{1,0:T(8,128)(2,1)S(1)} %get-tuple-element.37), channel_id=1, source_target_pairs={{384,128},{385,129},{386,130},{387,131},{388,132},{389,133},{390,1... | collective-permute-start | bytes 393224 | tf_op jit(solution)/shard_map/ppermute | solution.py:109
  111.3 8.8 %collective-permute-start = (bf16[256,256]{1,0:T(8,128)(2,1)S(1)}, bf16[256,256]{1,0:T(8,128)(2,1)S(1)}, u32[]{:S(2)}, u32[]{:S(2)}) collective-permute-start(bf16[256,256]{1,0:T(8,128)(2,1)S(1)} %get-tuple-element.37), channel_id=1, source_target_pairs={{384,256},{385,257},{386,258},{387,259},{388,260},{389,261},{390,2... | collective-permute-start | bytes 393224 | tf_op jit(solution)/shard_map/ppermute | solution.py:109
  153.2 54.6 %all-to-all-start.1 = ((bf16[16,64,256]{2,1,0:T(8,128)(2,1)}), bf16[16,64,256]{2,1,0:T(8,128)(2,1)S(1)}, u32[]{:S(2)}, u32[]{:S(2)}) async-start(bf16[16,64,256]{2,1,0:T(8,128)(2,1)} %bitcast.28), calls=%async_computation.2 | async-start | bytes 1048576 | tf_op jit(solution)/shard_map/all_to_all | solution.py:61
  207.8 18.2 %all-to-all-start = ((f32[4,2,256,128]{2,3,1,0:T(8,128)}), f32[4,2,256,128]{2,3,1,0:T(8,128)S(1)}, u32[]{:S(2)}, u32[]{:S(2)}) async-start(f32[4,2,256,128]{2,3,1,0:T(8,128)} %copy.17), calls=%async_computation.1 | async-start | bytes 2097152 | tf_op jit(solution)/shard_map/all_to_all | solution.py:48
  211.8 24.4 %copy-start.1 = (bf16[1,2,128,256]{3,2,1,0:T(8,128)(2,1)S(1)}, bf16[1,2,128,256]{3,2,1,0:T(8,128)(2,1)}, u32[]{:S(2)}) copy-start(bf16[1,2,128,256]{3,2,1,0:T(8,128)(2,1)} %param.6) | copy-start | bytes 393220
  211.8 24.4 %copy-start.2 = (bf16[1,128,256]{2,1,0:T(8,128)(2,1)S(1)}, bf16[1,128,256]{2,1,0:T(8,128)(2,1)}, u32[]{:S(2)}) copy-start(bf16[1,128,256]{2,1,0:T(8,128)(2,1)} %param.7) | copy-start | bytes 196612
  226.9 26.5 %all-to-all-start.2 = ((bf16[16,64,256]{2,1,0:T(8,128)(2,1)}), bf16[16,64,256]{2,1,0:T(8,128)(2,1)S(1)}, u32[]{:S(2)}, u32[]{:S(2)}) async-start(bf16[16,64,256]{2,1,0:T(8,128)(2,1)} %broadcast_in_dim.5), calls=%async_computation.3 | async-start | bytes 1048576 | tf_op jit(solution)/shard_map/all_to_all | solution.py:64
  236.2 18.1 %collective-permute-start.4 = (bf16[1,128,256]{2,1,0:T(8,128)(2,1)S(1)}, bf16[1,128,256]{2,1,0:T(8,128)(2,1)S(1)}, u32[]{:S(2)}, u32[]{:S(2)}) collective-permute-start(bf16[1,128,256]{2,1,0:T(8,128)(2,1)S(1)} %get-tuple-element.52), channel_id=1, source_target_pairs={{0,480},{32,0},{64,32},{96,64},{128,96},{160,128},{192,160},{224,1... | collective-permute-start | bytes 196616 | tf_op jit(solution)/shard_map/ppermute | solution.py:18
  236.3 18.0 %collective-permute-start.3 = (bf16[1,128,256]{2,1,0:T(8,128)(2,1)S(1)}, bf16[1,128,256]{2,1,0:T(8,128)(2,1)S(1)}, u32[]{:S(2)}, u32[]{:S(2)}) collective-permute-start(bf16[1,128,256]{2,1,0:T(8,128)(2,1)S(1)} %get-tuple-element.53), channel_id=1, source_target_pairs={{0,32},{32,64},{64,96},{96,128},{128,160},{160,192},{192,224},{224... | collective-permute-start | bytes 196616 | tf_op jit(solution)/shard_map/ppermute | solution.py:18
Sparse Core Ops, SparseCore 0:
  21.7 83.3 all-gather.1
  150.4 54.8 reduce-scatter.1

commit v10 on v9

--- a/solution.py
+++ b/solution.py
@@ -38,13 +38,14 @@
     return (grad_queries, grad_keys, grad_values)
 
 
-def head_sum(terms, axis):
+def head_sum(terms, axis, tie):
     count, width, tokens = terms.shape
     rounded = terms.astype(jnp.bfloat16)
     if isinstance(axis, tuple):
         tall, wide = lax.axis_size(axis[0]), lax.axis_size(axis[1])
         parts = rounded.reshape(count, tall, wide, width // (tall * wide), tokens).transpose(1, 2, 0, 3, 4)
         partial = lax.psum_scatter(parts, axis[0], scatter_dimension=0, tiled=True)[0]
+        partial, tie = lax.optimization_barrier((partial, tie))
         moved = lax.all_to_all(partial.astype(jnp.float32), axis[1], 0, 0, tiled=True)
         summed = jnp.sum(moved, axis=0)
     else:
@@ -52,7 +53,7 @@
         parts = rounded.reshape(count, devices, width // devices, tokens).transpose(1, 0, 2, 3)
         moved = lax.all_to_all(parts, axis, 0, 0, tiled=True)
         summed = jnp.sum(moved.astype(jnp.float32), axis=0)
-    return summed.transpose(0, 2, 1)
+    return summed.transpose(0, 2, 1), tie
 
 
 def segment_sum(contrib, axis):
@@ -141,23 +142,24 @@
             lax.dot_general(w_query, grad_flat, (((1,), (1,)), ((), ())), preferred_element_type=jnp.float32),
         ]
     )
-    out_sum, grad_input = head_sum(terms, mp)
+    onehot = (
+        local_nbr[1][..., None] == jnp.arange(pool_blocks, dtype=jnp.int32)[None, None, :]
+    ).astype(jnp.float32)
+    grad_keyval = jnp.concatenate([grad_keys, grad_values], axis=-1).reshape(
+        groups, NEIGH, NBLEN, 2 * head
+    )
+    contrib = jnp.einsum("cbp,cbrf->prf", onehot, grad_keyval)
+    contrib = jnp.where(is_encoder, jnp.zeros_like(contrib), contrib)
+    pooled = segment_sum(contrib.astype(jnp.bfloat16).reshape(pool_blocks * NBLEN, 2 * head), seg)
+    kv_grad = pooled.reshape(pool_blocks * NBLEN, 2, head)
+    summed, kv_grad = head_sum(terms, mp, kv_grad)
+    out_sum, grad_input = summed
     forward_rows = (local_rows[0].astype(jnp.float32) + out_sum).astype(jnp.bfloat16)
     forward_rows = jnp.where(is_encoder, local_carry, forward_rows)
     passed = from_behind(forward_rows[None], seg, 1)
     back = local_carry.astype(jnp.float32) + grad_input
     back_rows = jnp.where(is_encoder, local_carry, back.astype(jnp.bfloat16))
     returned = from_behind(back_rows[None], seg, -1)
-    onehot = (
-        local_nbr[1][..., None] == jnp.arange(pool_blocks, dtype=jnp.int32)[None, None, :]
-    ).astype(jnp.float32)
-    grad_keyval = jnp.concatenate([grad_keys, grad_values], axis=-1).reshape(
-        groups, NEIGH, NBLEN, 2 * head
-    )
-    contrib = jnp.einsum("cbp,cbrf->prf", onehot, grad_keyval)
-    contrib = jnp.where(is_encoder, jnp.zeros_like(contrib), contrib)
-    pooled = segment_sum(contrib.astype(jnp.bfloat16).reshape(pool_blocks * NBLEN, 2 * head), seg)
-    kv_grad = pooled.reshape(pool_blocks * NBLEN, 2, head)
     return (passed, returned, kv_grad)
 
 

time: 263 us -> 241 us (0.916)
  waiting for transfers between devices: 160 us -> 95.3 us
  blocking collectives: 26.5 us -> 87.9 us
  starting transfers between devices: 23.8 us -> 5.81 us
    all_to_all x0 -> x3, blocking collectives: none -> 61.4 us  [the longest x1 23.3 us: segment_sum(): moved = lax.all_to_all(parts, axis, 0, 0, tiled=True)]
    reduce_scatter x1, waiting for transfers between devices: 46 us -> 8.63 us  [head_sum(): lax.psum_scatter(parts, axis[0], scatter_dimension=0, tiled=True)[0]]
    all_to_all x3 -> x0, waiting for transfers between devices: 29.6 us -> none  [the longest x1 15.4 us: segment_sum(): return lax.all_to_all(spread, axis, 0, 0, tiled=True).reshape(contrib.shape)]
    all_to_all x3 -> x0, starting transfers between devices: 19.3 us -> none  [the longest x1 9.16 us: segment_sum(): return lax.all_to_all(spread, axis, 0, 0, tiled=True).reshape(contrib.shape)]
  transfers between devices with their start and end apart: 10 -> 7, of which waited for: 5 -> 4; matrix products, arithmetic and copies ran while one was open for 5% -> 4% of each run, Pallas kernels for 0% -> 0%
where the time goes in v10:
time: 241 us; the launch traced here: 238 us
  waiting for transfers between devices  95.3 us (40%)
  blocking collectives  87.9 us (36%)
  local copies, waits for them, and re-layouts  17.2 us (7%)
  between operations  14.3 us (6%)
  matrix products  11.3 us (5%)
  other arithmetic  6.31 us (3%)
  starting transfers between devices  5.81 us (2%)
    all_gather x1, waiting for transfers between devices, per_device(): gathered = lax.all_gather(gathered, stage, axis=2, tiled=True)  79.5 us
    all_to_all x1, blocking collectives, segment_sum(): moved = lax.all_to_all(parts, axis, 0, 0, tiled=True)  23.3 us
    all_to_all x1, blocking collectives, segment_sum(): return lax.all_to_all(spread, axis, 0, 0, tiled=True).reshape(contrib.shape)  20 us
    all_to_all x1, blocking collectives, head_sum(): lax.all_to_all(partial.astype(jnp.float32), axis[1], 0, 0, tiled=True)  18.1 us
    all_gather x1, blocking collectives, per_device(): gathered = lax.all_gather(gathered, stage, axis=2, tiled=True)  13.3 us
    all_gather x1, blocking collectives, per_device(): lax.all_gather(piece, 'sr', axis=0, tiled=True)  13.1 us
    reduce_scatter x1, waiting for transfers between devices, head_sum(): lax.psum_scatter(parts, axis[0], scatter_dimension=0, tiled=True)[0]  8.63 us
    ppermute x3, waiting for transfers between devices, per_device(): arrived = lax.ppermute(encoded, 'sg', [(last_group, target)])  5.22 us
  transfers between devices with their start and end apart: 7, of which 4 were waited for; matrix products, arithmetic and copies ran while one was open for 4% of the time, Pallas kernels for 0%

profile of v10, /device:TPU:1, one launch (start us, length us, event | category | flops | bytes accessed | tf_op | source)
XLA Modules:
  0.0 238.0 jit_solution(9152944023082938235)
XLA Ops:
  7.2 1.0 pad_maximum_fusion.2
  8.2 13.3 %all_gather.9 = bf16[3,128,1024]{2,1,0:T(8,128)(2,1)} all-gather(bf16[3,128,256]{2,1,0:T(8,128)(2,1)S(1)} %pad_maximum_fusion.2), channel_id=1, replica_groups=mesh['sg'=4,'sr'=4,'my'=8,'mx'=4] {'mx'}, dimensions={2}, use_global_device_ids=true | all-gather | bytes 983040 | tf_op jit(solution)/shard_map/all_gather | solution.py:80
  21.8 3.8 %slice_bitcast_fusion.2 = (bf16[8192,128]{1,0:T(8,128)(2,1)}, bf16[8192,128]{1,0:T(8,128)(2,1)S(1)}) fusion(bf16[1,2,8192,128]{3,2,1,0:T(8,128)(2,1)} %param.8), kind=kLoop, calls=%fused_computation.15 | loop fusion | bytes 8388608 | tf_op jit(solution)/shard_map/squeeze | solution.py:86
  25.7 79.5 %all-gather.2.cloned.1.call-done = bf16[3,128,8192]{2,1,0:T(8,128)(2,1)} async-done(((bf16[3,128,1024]{2,1,0:T(8,128)(2,1)}), bf16[3,128,8192]{2,1,0:T(8,128)(2,1)}) %all-gather.2.cloned.1.call-update) | async-done | bytes 6291472 | tf_op jit(solution)/shard_map/all_gather | solution.py:80
  105.1 2.2 slice-done
  107.3 0.7 copy-done
  108.0 1.3 conditional.1
  108.0 1.3 convolution_convert_fusion
  109.3 1.3 collective-permute-start.2
  110.6 0.7 collective-permute-start.1
  111.3 0.7 collective-permute-start
  112.0 2.9 %fusion.12 = bf16[128,128]{1,0:T(8,128)(2,1)S(1)} fusion(bf16[3,128,8192]{2,1,0:T(8,128)(2,1)} %all-gather.2.cloned.1.call-done, bf16[1,2,8192,128]{3,2,1,0:T(8,128)(2,1)} %param.8), kind=kOutput, calls=%fused_computation.29 | convolution fusion | flops 268451840 | bytes 4227072 | tf_op jit(solution)/shard_map/dot_general | solution.py:129
  114.9 5.2 %collective-permute-done.2 = bf16[256,256]{1,0:T(8,128)(2,1)S(1)} collective-permute-done((bf16[256,256]{1,0:T(8,128)(2,1)S(1)}, bf16[256,256]{1,0:T(8,128)(2,1)S(1)}, u32[]{:S(2)}, u32[]{:S(2)}) %collective-permute-start.2) | collective-permute-done | bytes 131104 | tf_op jit(solution)/shard_map/ppermute | solution.py:110
  120.1 13.1 %all_gather.11 = bf16[1024,256]{1,0:T(8,128)(2,1)S(1)} all-gather(bf16[256,256]{1,0:T(8,128)(2,1)S(1)} %select_select_fusion), channel_id=1, replica_groups=mesh['sg'=4,'sr'=4,'my'=8,'mx'=4] {'sr'}, dimensions={0}, use_global_device_ids=true | all-gather | bytes 655360 | tf_op jit(solution)/shard_map/all_gather | solution.py:112
  133.3 0.6 gather_fusion.1
  133.8 0.6 gather_fusion
  136.2 2.3 fusion.3
  138.5 2.5 %copy.23 = bf16[8192,128]{1,0:T(8,128)(2,1)} copy(bf16[8192,128]{0,1:T(8,128)(2,1)S(1)} %fusion.3) | data formatting | bytes 4194304 | tf_op jit(solution)/shard_map/stack | solution.py:139
  141.0 2.3 fusion.2
  143.3 2.5 %copy.22 = bf16[8192,128]{1,0:T(8,128)(2,1)} copy(bf16[8192,128]{0,1:T(8,128)(2,1)S(1)} %fusion.2) | data formatting | bytes 4194304 | tf_op jit(solution)/shard_map/stack | solution.py:139
  145.8 4.5 %maximum_bitcast_fusion = bf16[8,4,2,256,128]{4,3,2,1,0:T(8,128)(2,1)} fusion(bf16[1,8,4,256,128]{4,3,0,2,1:T(8,128)(2,1)} %bitcast.82, bf16[1,8,4,256,128]{4,3,0,2,1:T(8,128)(2,1)} %bitcast.83), kind=kLoop, calls=%fused_computation.12 | loop fusion | flops 2097152 | bytes 8388608 | tf_op jit(solution)/shard_map/transpose | solution.py:46
  152.4 23.3 %all_to_all.15 = bf16[16,64,256]{2,1,0:T(8,128)(2,1)S(1)} all-to-all(bf16[16,64,256]{2,1,0:T(8,128)(2,1)S(1)} %bitcast.86), channel_id=1, replica_groups=mesh['sg'=4,'sr'=4,'my'=8,'mx'=4] {'sg','sr'}, dimensions={0} | all-to-all | bytes 1048576 | tf_op jit(solution)/shard_map/all_to_all | solution.py:62
  175.8 20.0 %all_to_all.16 = bf16[16,64,256]{2,1,0:T(8,128)(2,1)S(1)} all-to-all(bf16[16,64,256]{2,1,0:T(8,128)(2,1)S(1)} %broadcast_in_dim.5), channel_id=1, replica_groups=mesh['sg'=4,'sr'=4,'my'=8,'mx'=4] {'sg','sr'}, dimensions={0} | all-to-all | bytes 1048576 | tf_op jit(solution)/shard_map/all_to_all | solution.py:65
  195.8 0.9 reshape_reshape.7
  196.7 8.6 %reduce-scatter.2.cloned.1.call-done = bf16[1,4,2,256,128]{4,3,2,1,0:T(8,128)(2,1)} async-done(((bf16[8,4,2,256,128]{4,3,2,1,0:T(8,128)(2,1)}), bf16[1,4,2,256,128]{4,3,2,1,0:T(8,128)(2,1)}) %reduce-scatter.2.cloned.1.call-update) | async-done | bytes 524304 | tf_op jit(solution)/shard_map/reduce_scatter | solution.py:47
  205.4 1.2 copy.20
  206.6 18.1 %all_to_all.17 = f32[4,2,256,128]{2,3,1,0:T(8,128)S(1)} all-to-all(f32[4,2,256,128]{2,3,1,0:T(8,128)S(1)} %copy.20), channel_id=1, replica_groups=mesh['sg'=4,'sr'=4,'my'=8,'mx'=4] {'mx'}, dimensions={0} | all-to-all | bytes 2097152 | tf_op jit(solution)/shard_map/all_to_all | solution.py:49
  224.9 1.8 collective-permute-start.4
  226.8 1.3 collective-permute-start.3
  228.0 1.9 collective-permute-done.4
  229.9 0.6 copy.32
  230.6 0.6 copy.33
  (43 shorter events, 4.4 us)
Async XLA Ops:
  7.2 14.5 %copy-start.3 = (s32[1,2,2,2]{3,2,1,0:T(2,128)S(1)}, s32[1,2,2,2]{3,2,1,0:T(2,128)}, u32[]{:S(2)}) copy-start(s32[1,2,2,2]{3,2,1,0:T(2,128)} %param.9) | copy-start | bytes 100
  7.2 97.9 %all-gather.2.cloned.1.call-start = ((), (), s32[]{:S(2)}) async-start(), calls=%async_computation.4 | async-start | bytes 7077888 | tf_op jit(solution)/shard_map/all_gather | solution.py:80
  21.6 183.8 %reduce-scatter.2.cloned.1.call-start = ((), (), s32[]{:S(2)}) async-start(), calls=%async_computation.5 | async-start | bytes 4718592 | tf_op jit(solution)/shard_map/reduce_scatter | solution.py:47
  105.1 2.2 slice-start
  105.1 2.9 %copy-start = (bf16[8192,128]{1,0:T(8,128)(2,1)S(1)}, bf16[8192,128]{1,0:T(8,128)(2,1)}, u32[]{:S(2)}) copy-start(bf16[8192,128]{1,0:T(8,128)(2,1)} %get-tuple-element.54) | copy-start | bytes 6291460
  109.3 10.8 %collective-permute-start.2 = (bf16[256,256]{1,0:T(8,128)(2,1)S(1)}, bf16[256,256]{1,0:T(8,128)(2,1)S(1)}, u32[]{:S(2)}, u32[]{:S(2)}) collective-permute-start(bf16[256,256]{1,0:T(8,128)(2,1)S(1)} %get-tuple-element.39), channel_id=1, source_target_pairs={{384,0},{385,1},{386,2},{387,3},{388,4},{389,5},{390,6},{391,7},{3... | collective-permute-start | bytes 393224 | tf_op jit(solution)/shard_map/ppermute | solution.py:110
  110.6 9.5 %collective-permute-start.1 = (bf16[256,256]{1,0:T(8,128)(2,1)S(1)}, bf16[256,256]{1,0:T(8,128)(2,1)S(1)}, u32[]{:S(2)}, u32[]{:S(2)}) collective-permute-start(bf16[256,256]{1,0:T(8,128)(2,1)S(1)} %get-tuple-element.39), channel_id=1, source_target_pairs={{384,128},{385,129},{386,130},{387,131},{388,132},{389,133},{390,1... | collective-permute-start | bytes 393224 | tf_op jit(solution)/shard_map/ppermute | solution.py:110
  111.3 8.8 %collective-permute-start = (bf16[256,256]{1,0:T(8,128)(2,1)S(1)}, bf16[256,256]{1,0:T(8,128)(2,1)S(1)}, u32[]{:S(2)}, u32[]{:S(2)}) collective-permute-start(bf16[256,256]{1,0:T(8,128)(2,1)S(1)} %get-tuple-element.39), channel_id=1, source_target_pairs={{384,256},{385,257},{386,258},{387,259},{388,260},{389,261},{390,2... | collective-permute-start | bytes 393224 | tf_op jit(solution)/shard_map/ppermute | solution.py:110
  206.6 18.2 %copy-start.1 = (bf16[1,2,128,256]{3,2,1,0:T(8,128)(2,1)S(1)}, bf16[1,2,128,256]{3,2,1,0:T(8,128)(2,1)}, u32[]{:S(2)}) copy-start(bf16[1,2,128,256]{3,2,1,0:T(8,128)(2,1)} %param.6) | copy-start | bytes 393220
  206.6 18.2 %copy-start.2 = (bf16[1,128,256]{2,1,0:T(8,128)(2,1)S(1)}, bf16[1,128,256]{2,1,0:T(8,128)(2,1)}, u32[]{:S(2)}) copy-start(bf16[1,128,256]{2,1,0:T(8,128)(2,1)} %param.7) | copy-start | bytes 196612
  224.9 5.0 %collective-permute-start.4 = (bf16[1,128,256]{2,1,0:T(8,128)(2,1)S(1)}, bf16[1,128,256]{2,1,0:T(8,128)(2,1)S(1)}, u32[]{:S(2)}, u32[]{:S(2)}) collective-permute-start(bf16[1,128,256]{2,1,0:T(8,128)(2,1)S(1)} %get-tuple-element.56), channel_id=1, source_target_pairs={{0,480},{32,0},{64,32},{96,64},{128,96},{160,128},{192,160},{224,1... | collective-permute-start | bytes 196616 | tf_op jit(solution)/shard_map/ppermute | solution.py:18
  226.8 3.2 %collective-permute-start.3 = (bf16[1,128,256]{2,1,0:T(8,128)(2,1)S(1)}, bf16[1,128,256]{2,1,0:T(8,128)(2,1)S(1)}, u32[]{:S(2)}, u32[]{:S(2)}) collective-permute-start(bf16[1,128,256]{2,1,0:T(8,128)(2,1)S(1)} %get-tuple-element.57), channel_id=1, source_target_pairs={{0,32},{32,64},{64,96},{96,128},{128,160},{160,192},{192,224},{224... | collective-permute-start | bytes 196616 | tf_op jit(solution)/shard_map/ppermute | solution.py:18
Sparse Core Ops, SparseCore 0:
  21.7 83.3 all-gather.1
  150.4 54.8 reduce-scatter.1

commit v11 on v10

--- a/solution.py
+++ b/solution.py
@@ -46,8 +46,8 @@
         parts = rounded.reshape(count, tall, wide, width // (tall * wide), tokens).transpose(1, 2, 0, 3, 4)
         partial = lax.psum_scatter(parts, axis[0], scatter_dimension=0, tiled=True)[0]
         partial, tie = lax.optimization_barrier((partial, tie))
-        moved = lax.all_to_all(partial.astype(jnp.float32), axis[1], 0, 0, tiled=True)
-        summed = jnp.sum(moved, axis=0)
+        moved = lax.all_to_all(partial, axis[1], 0, 0, tiled=True)
+        summed = jnp.sum(moved.astype(jnp.float32), axis=0)
     else:
         devices = lax.axis_size(axis)
         parts = rounded.reshape(count, devices, width // devices, tokens).transpose(1, 0, 2, 3)

time: 241 us -> 235 us (0.975)
  blocking collectives: 87.9 us -> 82.1 us
    all_to_all x1, blocking collectives: 18.1 us -> 12.4 us  [head_sum(): moved = lax.all_to_all(partial, axis[1], 0, 0, tiled=True)]
where the time goes in v11:
time: 235 us; the launch traced here: 232 us
  waiting for transfers between devices  95.3 us (41%)
  blocking collectives  82.1 us (35%)
  local copies, waits for them, and re-layouts  17.2 us (7%)
  between operations  14.3 us (6%)
  matrix products  11.3 us (5%)
  other arithmetic  6.31 us (3%)
  starting transfers between devices  5.81 us (2%)
    all_gather x1, waiting for transfers between devices, per_device(): gathered = lax.all_gather(gathered, stage, axis=2, tiled=True)  79.5 us
    all_to_all x1, blocking collectives, segment_sum(): moved = lax.all_to_all(parts, axis, 0, 0, tiled=True)  23.3 us
    all_to_all x1, blocking collectives, segment_sum(): return lax.all_to_all(spread, axis, 0, 0, tiled=True).reshape(contrib.shape)  20 us
    all_gather x1, blocking collectives, per_device(): gathered = lax.all_gather(gathered, stage, axis=2, tiled=True)  13.3 us
    all_gather x1, blocking collectives, per_device(): lax.all_gather(piece, 'sr', axis=0, tiled=True)  13.1 us
    all_to_all x1, blocking collectives, head_sum(): moved = lax.all_to_all(partial, axis[1], 0, 0, tiled=True)  12.4 us
    reduce_scatter x1, waiting for transfers between devices, head_sum(): lax.psum_scatter(parts, axis[0], scatter_dimension=0, tiled=True)[0]  8.63 us
    ppermute x3, waiting for transfers between devices, per_device(): arrived = lax.ppermute(encoded, 'sg', [(last_group, target)])  5.22 us
  transfers between devices with their start and end apart: 7, of which 4 were waited for; matrix products, arithmetic and copies ran while one was open for 4% of the time, Pallas kernels for 0%

profile of v11, /device:TPU:1, one launch (start us, length us, event | category | flops | bytes accessed | tf_op | source)
XLA Modules:
  0.0 232.3 jit_solution(7432874130987226434)
XLA Ops:
  7.2 1.0 pad_maximum_fusion.2
  8.2 13.3 %all_gather.9 = bf16[3,128,1024]{2,1,0:T(8,128)(2,1)} all-gather(bf16[3,128,256]{2,1,0:T(8,128)(2,1)S(1)} %pad_maximum_fusion.2), channel_id=1, replica_groups=mesh['sg'=4,'sr'=4,'my'=8,'mx'=4] {'mx'}, dimensions={2}, use_global_device_ids=true | all-gather | bytes 983040 | tf_op jit(solution)/shard_map/all_gather | solution.py:80
  21.8 3.8 %slice_bitcast_fusion.2 = (bf16[8192,128]{1,0:T(8,128)(2,1)}, bf16[8192,128]{1,0:T(8,128)(2,1)S(1)}) fusion(bf16[1,2,8192,128]{3,2,1,0:T(8,128)(2,1)} %param.8), kind=kLoop, calls=%fused_computation.15 | loop fusion | bytes 8388608 | tf_op jit(solution)/shard_map/squeeze | solution.py:86
  25.7 79.5 %all-gather.2.cloned.1.call-done = bf16[3,128,8192]{2,1,0:T(8,128)(2,1)} async-done(((bf16[3,128,1024]{2,1,0:T(8,128)(2,1)}), bf16[3,128,8192]{2,1,0:T(8,128)(2,1)}) %all-gather.2.cloned.1.call-update) | async-done | bytes 6291472 | tf_op jit(solution)/shard_map/all_gather | solution.py:80
  105.1 2.2 slice-done
  107.3 0.7 copy-done
  108.0 1.3 conditional.1
  108.0 1.3 convolution_convert_fusion
  109.3 1.3 collective-permute-start.2
  110.6 0.7 collective-permute-start.1
  111.3 0.7 collective-permute-start
  112.0 2.9 %fusion.12 = bf16[128,128]{1,0:T(8,128)(2,1)S(1)} fusion(bf16[3,128,8192]{2,1,0:T(8,128)(2,1)} %all-gather.2.cloned.1.call-done, bf16[1,2,8192,128]{3,2,1,0:T(8,128)(2,1)} %param.8), kind=kOutput, calls=%fused_computation.29 | convolution fusion | flops 268451840 | bytes 4227072 | tf_op jit(solution)/shard_map/dot_general | solution.py:129
  114.9 5.2 %collective-permute-done.2 = bf16[256,256]{1,0:T(8,128)(2,1)S(1)} collective-permute-done((bf16[256,256]{1,0:T(8,128)(2,1)S(1)}, bf16[256,256]{1,0:T(8,128)(2,1)S(1)}, u32[]{:S(2)}, u32[]{:S(2)}) %collective-permute-start.2) | collective-permute-done | bytes 131104 | tf_op jit(solution)/shard_map/ppermute | solution.py:110
  120.1 13.1 %all_gather.11 = bf16[1024,256]{1,0:T(8,128)(2,1)S(1)} all-gather(bf16[256,256]{1,0:T(8,128)(2,1)S(1)} %select_select_fusion), channel_id=1, replica_groups=mesh['sg'=4,'sr'=4,'my'=8,'mx'=4] {'sr'}, dimensions={0}, use_global_device_ids=true | all-gather | bytes 655360 | tf_op jit(solution)/shard_map/all_gather | solution.py:112
  133.3 0.6 gather_fusion.1
  133.8 0.6 gather_fusion
  136.2 2.3 fusion.3
  138.5 2.5 %copy.23 = bf16[8192,128]{1,0:T(8,128)(2,1)} copy(bf16[8192,128]{0,1:T(8,128)(2,1)S(1)} %fusion.3) | data formatting | bytes 4194304 | tf_op jit(solution)/shard_map/stack | solution.py:139
  141.0 2.3 fusion.2
  143.3 2.5 %copy.22 = bf16[8192,128]{1,0:T(8,128)(2,1)} copy(bf16[8192,128]{0,1:T(8,128)(2,1)S(1)} %fusion.2) | data formatting | bytes 4194304 | tf_op jit(solution)/shard_map/stack | solution.py:139
  145.8 4.5 %maximum_bitcast_fusion = bf16[8,4,2,256,128]{4,3,2,1,0:T(8,128)(2,1)} fusion(bf16[1,8,4,256,128]{4,3,0,2,1:T(8,128)(2,1)} %bitcast.82, bf16[1,8,4,256,128]{4,3,0,2,1:T(8,128)(2,1)} %bitcast.83), kind=kLoop, calls=%fused_computation.12 | loop fusion | flops 2097152 | bytes 8388608 | tf_op jit(solution)/shard_map/transpose | solution.py:46
  152.4 23.3 %all_to_all.15 = bf16[16,64,256]{2,1,0:T(8,128)(2,1)S(1)} all-to-all(bf16[16,64,256]{2,1,0:T(8,128)(2,1)S(1)} %bitcast.86), channel_id=1, replica_groups=mesh['sg'=4,'sr'=4,'my'=8,'mx'=4] {'sg','sr'}, dimensions={0} | all-to-all | bytes 1048576 | tf_op jit(solution)/shard_map/all_to_all | solution.py:62
  175.8 20.0 %all_to_all.16 = bf16[16,64,256]{2,1,0:T(8,128)(2,1)S(1)} all-to-all(bf16[16,64,256]{2,1,0:T(8,128)(2,1)S(1)} %broadcast_in_dim.5), channel_id=1, replica_groups=mesh['sg'=4,'sr'=4,'my'=8,'mx'=4] {'sg','sr'}, dimensions={0} | all-to-all | bytes 1048576 | tf_op jit(solution)/shard_map/all_to_all | solution.py:65
  195.8 0.9 reshape_reshape.7
  196.7 8.6 %reduce-scatter.2.cloned.1.call-done = bf16[1,4,2,256,128]{4,3,2,1,0:T(8,128)(2,1)} async-done(((bf16[8,4,2,256,128]{4,3,2,1,0:T(8,128)(2,1)}), bf16[1,4,2,256,128]{4,3,2,1,0:T(8,128)(2,1)}) %reduce-scatter.2.cloned.1.call-update) | async-done | bytes 524304 | tf_op jit(solution)/shard_map/reduce_scatter | solution.py:47
  205.4 1.2 copy.20
  206.6 12.4 %all_to_all.17 = bf16[4,2,256,128]{2,3,1,0:T(8,128)(2,1)S(1)} all-to-all(bf16[4,2,256,128]{2,3,1,0:T(8,128)(2,1)S(1)} %copy.20), channel_id=1, replica_groups=mesh['sg'=4,'sr'=4,'my'=8,'mx'=4] {'mx'}, dimensions={0} | all-to-all | bytes 1048576 | tf_op jit(solution)/shard_map/all_to_all | solution.py:49
  219.1 1.8 collective-permute-start.4
  221.0 1.3 collective-permute-start.3
  222.2 1.9 collective-permute-done.4
  224.2 0.6 copy.32
  224.8 0.6 copy.33
  (43 shorter events, 4.4 us)
Async XLA Ops:
  7.2 14.5 %copy-start.3 = (s32[1,2,2,2]{3,2,1,0:T(2,128)S(1)}, s32[1,2,2,2]{3,2,1,0:T(2,128)}, u32[]{:S(2)}) copy-start(s32[1,2,2,2]{3,2,1,0:T(2,128)} %param.9) | copy-start | bytes 100
  7.2 97.9 %all-gather.2.cloned.1.call-start = ((), (), s32[]{:S(2)}) async-start(), calls=%async_computation.4 | async-start | bytes 7077888 | tf_op jit(solution)/shard_map/all_gather | solution.py:80
  21.6 183.8 %reduce-scatter.2.cloned.1.call-start = ((), (), s32[]{:S(2)}) async-start(), calls=%async_computation.5 | async-start | bytes 4718592 | tf_op jit(solution)/shard_map/reduce_scatter | solution.py:47
  105.1 2.2 slice-start
  105.1 2.9 %copy-start = (bf16[8192,128]{1,0:T(8,128)(2,1)S(1)}, bf16[8192,128]{1,0:T(8,128)(2,1)}, u32[]{:S(2)}) copy-start(bf16[8192,128]{1,0:T(8,128)(2,1)} %get-tuple-element.54) | copy-start | bytes 6291460
  109.3 10.8 %collective-permute-start.2 = (bf16[256,256]{1,0:T(8,128)(2,1)S(1)}, bf16[256,256]{1,0:T(8,128)(2,1)S(1)}, u32[]{:S(2)}, u32[]{:S(2)}) collective-permute-start(bf16[256,256]{1,0:T(8,128)(2,1)S(1)} %get-tuple-element.39), channel_id=1, source_target_pairs={{384,0},{385,1},{386,2},{387,3},{388,4},{389,5},{390,6},{391,7},{3... | collective-permute-start | bytes 393224 | tf_op jit(solution)/shard_map/ppermute | solution.py:110
  110.6 9.5 %collective-permute-start.1 = (bf16[256,256]{1,0:T(8,128)(2,1)S(1)}, bf16[256,256]{1,0:T(8,128)(2,1)S(1)}, u32[]{:S(2)}, u32[]{:S(2)}) collective-permute-start(bf16[256,256]{1,0:T(8,128)(2,1)S(1)} %get-tuple-element.39), channel_id=1, source_target_pairs={{384,128},{385,129},{386,130},{387,131},{388,132},{389,133},{390,1... | collective-permute-start | bytes 393224 | tf_op jit(solution)/shard_map/ppermute | solution.py:110
  111.3 8.8 %collective-permute-start = (bf16[256,256]{1,0:T(8,128)(2,1)S(1)}, bf16[256,256]{1,0:T(8,128)(2,1)S(1)}, u32[]{:S(2)}, u32[]{:S(2)}) collective-permute-start(bf16[256,256]{1,0:T(8,128)(2,1)S(1)} %get-tuple-element.39), channel_id=1, source_target_pairs={{384,256},{385,257},{386,258},{387,259},{388,260},{389,261},{390,2... | collective-permute-start | bytes 393224 | tf_op jit(solution)/shard_map/ppermute | solution.py:110
  195.8 23.3 %copy-start.1 = (bf16[1,2,128,256]{3,2,1,0:T(8,128)(2,1)S(1)}, bf16[1,2,128,256]{3,2,1,0:T(8,128)(2,1)}, u32[]{:S(2)}) copy-start(bf16[1,2,128,256]{3,2,1,0:T(8,128)(2,1)} %param.6) | copy-start | bytes 393220
  195.8 23.3 %copy-start.2 = (bf16[1,128,256]{2,1,0:T(8,128)(2,1)S(1)}, bf16[1,128,256]{2,1,0:T(8,128)(2,1)}, u32[]{:S(2)}) copy-start(bf16[1,128,256]{2,1,0:T(8,128)(2,1)} %param.7) | copy-start | bytes 196612
  219.1 5.0 %collective-permute-start.4 = (bf16[1,128,256]{2,1,0:T(8,128)(2,1)S(1)}, bf16[1,128,256]{2,1,0:T(8,128)(2,1)S(1)}, u32[]{:S(2)}, u32[]{:S(2)}) collective-permute-start(bf16[1,128,256]{2,1,0:T(8,128)(2,1)S(1)} %get-tuple-element.56), channel_id=1, source_target_pairs={{0,480},{32,0},{64,32},{96,64},{128,96},{160,128},{192,160},{224,1... | collective-permute-start | bytes 196616 | tf_op jit(solution)/shard_map/ppermute | solution.py:18
  221.0 3.2 %collective-permute-start.3 = (bf16[1,128,256]{2,1,0:T(8,128)(2,1)S(1)}, bf16[1,128,256]{2,1,0:T(8,128)(2,1)S(1)}, u32[]{:S(2)}, u32[]{:S(2)}) collective-permute-start(bf16[1,128,256]{2,1,0:T(8,128)(2,1)S(1)} %get-tuple-element.57), channel_id=1, source_target_pairs={{0,32},{32,64},{64,96},{96,128},{128,160},{160,192},{192,224},{224... | collective-permute-start | bytes 196616 | tf_op jit(solution)/shard_map/ppermute | solution.py:18
Sparse Core Ops, SparseCore 0:
  21.7 83.3 all-gather.1
  150.4 54.8 reduce-scatter.1

commit v12 on v11

--- a/solution.py
+++ b/solution.py
@@ -75,10 +75,11 @@
     is_encoder = group == last_group
     local_rows = rows[0]
     local_carry = carry[0]
-    gathered = jnp.concatenate([local_rows, local_carry[None]], axis=0)
+    full_rows, full_carry = local_rows, local_carry
     for stage in stages:
-        gathered = lax.all_gather(gathered, stage, axis=2, tiled=True)
-    full_rows, full_carry = gathered[:2], gathered[2]
+        full_rows = lax.all_gather(full_rows, stage, axis=2, tiled=True)
+    for stage in stages:
+        full_carry = lax.all_gather(full_carry, stage, axis=1, tiled=True)
     tokens = local_rows.shape[1]
     width = full_rows.shape[2]
     head = weights.shape[3]

time: 235 us -> 241 us (1.026)
  blocking collectives: 82.1 us -> 91.6 us
    all_gather x1 -> x2, blocking collectives: 13.3 us -> 23.9 us  [the longest x1 13.3 us: per_device(): full_rows = lax.all_gather(full_rows, stage, axis=2, tiled=True)]
    ppermute x3, waiting for transfers between devices: 5.22 us -> 0.01 us  [per_device(): arrived = lax.ppermute(encoded, 'sg', [(last_group, target)])]
    all_gather x1 -> x2, waiting for transfers between devices: 79.5 us -> 82.4 us  [the longest x1 47.5 us: per_device(): full_rows = lax.all_gather(full_rows, stage, axis=2, tiled=True)]
  transfers between devices with their start and end apart: 7 -> 8, of which waited for: 4 -> 5; matrix products, arithmetic and copies ran while one was open for 4% -> 6% of each run, Pallas kernels for 0% -> 0%
where the time goes in v12:
time: 241 us; the launch traced here: 240 us
  waiting for transfers between devices  94.3 us (39%)
  blocking collectives  91.6 us (38%)
  local copies, waits for them, and re-layouts  14.9 us (6%)
  between operations  14 us (6%)
  matrix products  13.4 us (6%)
  other arithmetic  6.03 us (3%)
  starting transfers between devices  5.83 us (2%)
    all_gather x1, waiting for transfers between devices, per_device(): full_rows = lax.all_gather(full_rows, stage, axis=2, tiled=True)  47.5 us
    all_gather x1, waiting for transfers between devices, per_device(): full_carry = lax.all_gather(full_carry, stage, axis=1, tiled=True)  35 us
    all_to_all x1, blocking collectives, segment_sum(): moved = lax.all_to_all(parts, axis, 0, 0, tiled=True)  23.6 us
    all_to_all x1, blocking collectives, segment_sum(): return lax.all_to_all(spread, axis, 0, 0, tiled=True).reshape(contrib.shape)  20 us
    all_gather x1, blocking collectives, per_device(): full_rows = lax.all_gather(full_rows, stage, axis=2, tiled=True)  13.3 us
    all_to_all x1, blocking collectives, head_sum(): moved = lax.all_to_all(partial, axis[1], 0, 0, tiled=True)  12.4 us
    all_gather x1, blocking collectives, per_device(): lax.all_gather(piece, 'sr', axis=0, tiled=True)  11.7 us
    all_gather x1, blocking collectives, per_device(): full_carry = lax.all_gather(full_carry, stage, axis=1, tiled=True)  10.6 us
  transfers between devices with their start and end apart: 8, of which 5 were waited for; matrix products, arithmetic and copies ran while one was open for 6% of the time, Pallas kernels for 0%

profile of v12, /device:TPU:1, one launch (start us, length us, event | category | flops | bytes accessed | tf_op | source)
XLA Modules:
  0.0 240.1 jit_solution(17684323944178127631)
XLA Ops:
  7.2 13.3 %all-gather = bf16[1,2,128,1024]{3,2,1,0:T(8,128)(2,1)} all-gather(bf16[1,2,128,256]{3,2,1,0:T(8,128)(2,1)} %param.6), channel_id=2, replica_groups=mesh['sg'=4,'sr'=4,'my'=8,'mx'=4] {'mx'}, dimensions={3}, use_global_device_ids=true | all-gather | bytes 655360 | tf_op jit(solution)/shard_map/all_gather | solution.py:80
  20.6 10.6 %all-gather.2 = bf16[1,128,1024]{2,1,0:T(8,128)(2,1)} all-gather(bf16[1,128,256]{2,1,0:T(8,128)(2,1)} %param.7), channel_id=4, replica_groups=mesh['sg'=4,'sr'=4,'my'=8,'mx'=4] {'mx'}, dimensions={2}, use_global_device_ids=true | all-gather | bytes 327680 | tf_op jit(solution)/shard_map/all_gather | solution.py:82
  31.3 0.7 compare_select_fusion.1
  32.1 3.8 %slice_bitcast_fusion = (bf16[8192,128]{1,0:T(8,128)(2,1)}, bf16[8192,128]{1,0:T(8,128)(2,1)S(1)}) fusion(bf16[1,2,8192,128]{3,2,1,0:T(8,128)(2,1)} %param.8), kind=kLoop, calls=%fused_computation.15 | loop fusion | bytes 8388608 | tf_op jit(solution)/shard_map/squeeze | solution.py:87
  36.0 47.5 %all-gather.7.cloned.1.call-done = bf16[1,2,128,8192]{3,2,1,0:T(8,128)(2,1)} async-done(((bf16[1,2,128,1024]{3,2,1,0:T(8,128)(2,1)}), bf16[1,2,128,8192]{3,2,1,0:T(8,128)(2,1)}) %all-gather.7.cloned.1.call-update) | async-done | bytes 4194320 | tf_op jit(solution)/shard_map/all_gather | solution.py:80
  83.5 3.5 %conditional.1 = (bf16[256,256]{1,0:T(8,128)(2,1)S(1)}, bf16[2,64,128]{2,1,0:T(8,128)(2,1)S(1)}, bf16[2,64,128]{2,1,0:T(8,128)(2,1)S(1)}) conditional(s32[]{:T(128)} %convert_element_type.64, (bf16[2,128,8192]{2,1,0:T(8,128)(2,1)}, bf16[8192,128]{1,0:T(8,128)(2,1)S(1)}) %tuple.46, (bf16[2,128,8192]{2,1,0:T(8,128)(2,1)}, ...), branch_computations={%region_0.0_spmd, %region_1.0_spmd} | conditional | flops 1074069504 | bytes 30081080 | solution.py:106
  83.5 3.4 %convolution_convert_fusion = bf16[256,128]{1,0:T(8,128)(2,1)S(1)} fusion(bf16[256,8192]{1,0:T(8,128)(2,1)} %bitcast.81, bf16[8192,128]{1,0:T(8,128)(2,1)S(1)} %get-tuple-element.26), kind=kOutput, calls=%fused_computation.2 | convolution fusion | flops 536903680 | bytes 6356992 | tf_op jit(solution)/shard_map/cond/branch_0_fun/dot_general | solution.py:101
  87.0 0.7 collective-permute-start
  87.6 0.7 collective-permute-start.1
  88.3 1.3 collective-permute-start.2
  89.6 35.0 %all-gather.9.cloned.1.call-done = bf16[1,128,8192]{2,1,0:T(8,128)(2,1)} async-done(((bf16[1,128,1024]{2,1,0:T(8,128)(2,1)}), bf16[1,128,8192]{2,1,0:T(8,128)(2,1)}) %all-gather.9.cloned.1.call-update) | async-done | bytes 2097168 | tf_op jit(solution)/shard_map/all_gather | solution.py:82
  124.6 2.9 %fusion.13 = bf16[128,128]{1,0:T(8,128)(2,1)S(1)} fusion(bf16[1,128,8192]{2,1,0:T(8,128)(2,1)} %all-gather.9.cloned.1.call-done, bf16[1,2,8192,128]{3,2,1,0:T(8,128)(2,1)} %param.8), kind=kOutput, calls=%fused_computation.29 | convolution fusion | flops 268451840 | bytes 4227072 | tf_op jit(solution)/shard_map/dot_general | solution.py:130
  127.6 11.7 %all_gather.17 = bf16[1024,256]{1,0:T(8,128)(2,1)S(1)} all-gather(bf16[256,256]{1,0:T(8,128)(2,1)S(1)} %select_select_fusion), channel_id=1, replica_groups=mesh['sg'=4,'sr'=4,'my'=8,'mx'=4] {'sr'}, dimensions={0}, use_global_device_ids=true | all-gather | bytes 655360 | tf_op jit(solution)/shard_map/all_gather | solution.py:113
  139.3 0.6 gather_fusion.1
  141.0 2.3 fusion.3
  143.3 2.5 %copy.23 = bf16[8192,128]{1,0:T(8,128)(2,1)} copy(bf16[8192,128]{0,1:T(8,128)(2,1)S(1)} %fusion.3) | data formatting | bytes 4194304 | tf_op jit(solution)/shard_map/stack | solution.py:140
  145.8 0.6 gather_fusion
  147.0 2.3 fusion.2
  149.3 2.5 %copy.22 = bf16[8192,128]{1,0:T(8,128)(2,1)} copy(bf16[8192,128]{0,1:T(8,128)(2,1)S(1)} %fusion.2) | data formatting | bytes 4194304 | tf_op jit(solution)/shard_map/stack | solution.py:140
  151.8 4.5 %maximum_bitcast_fusion = bf16[8,4,2,256,128]{4,3,2,1,0:T(8,128)(2,1)} fusion(bf16[1,8,4,256,128]{4,3,0,2,1:T(8,128)(2,1)} %bitcast.84, bf16[1,8,4,256,128]{4,3,0,2,1:T(8,128)(2,1)} %bitcast.85), kind=kLoop, calls=%fused_computation.12 | loop fusion | flops 2097152 | bytes 8388608 | tf_op jit(solution)/shard_map/transpose | solution.py:46
  156.4 0.7 copy-done.3
  159.1 23.6 %all_to_all.15 = bf16[16,64,256]{2,1,0:T(8,128)(2,1)S(1)} all-to-all(bf16[16,64,256]{2,1,0:T(8,128)(2,1)S(1)} %bitcast.88), channel_id=1, replica_groups=mesh['sg'=4,'sr'=4,'my'=8,'mx'=4] {'sg','sr'}, dimensions={0} | all-to-all | bytes 1048576 | tf_op jit(solution)/shard_map/all_to_all | solution.py:62
  182.8 20.0 %all_to_all.16 = bf16[16,64,256]{2,1,0:T(8,128)(2,1)S(1)} all-to-all(bf16[16,64,256]{2,1,0:T(8,128)(2,1)S(1)} %broadcast_in_dim.5), channel_id=1, replica_groups=mesh['sg'=4,'sr'=4,'my'=8,'mx'=4] {'sg','sr'}, dimensions={0} | all-to-all | bytes 1048576 | tf_op jit(solution)/shard_map/all_to_all | solution.py:65
  202.8 0.9 reshape_reshape.7
  203.8 8.1 %reduce-scatter.2.cloned.1.call-done = bf16[1,4,2,256,128]{4,3,2,1,0:T(8,128)(2,1)} async-done(((bf16[8,4,2,256,128]{4,3,2,1,0:T(8,128)(2,1)}), bf16[1,4,2,256,128]{4,3,2,1,0:T(8,128)(2,1)}) %reduce-scatter.2.cloned.1.call-update) | async-done | bytes 524304 | tf_op jit(solution)/shard_map/reduce_scatter | solution.py:47
  211.8 1.2 copy.20
  213.1 12.4 %all_to_all.17 = bf16[4,2,256,128]{2,3,1,0:T(8,128)(2,1)S(1)} all-to-all(bf16[4,2,256,128]{2,3,1,0:T(8,128)(2,1)S(1)} %copy.20), channel_id=1, replica_groups=mesh['sg'=4,'sr'=4,'my'=8,'mx'=4] {'mx'}, dimensions={0} | all-to-all | bytes 1048576 | tf_op jit(solution)/shard_map/all_to_all | solution.py:49
  225.6 3.1 %collective-permute-start.3 = (bf16[1,128,256]{2,1,0:T(8,128)(2,1)S(1)}, bf16[1,128,256]{2,1,0:T(8,128)(2,1)S(1)}, u32[]{:S(2)}, u32[]{:S(2)}) collective-permute-start(bf16[1,128,256]{2,1,0:T(8,128)(2,1)S(1)} %get-tuple-element.57), channel_id=1, source_target_pairs={{0,32},{32,64},{64,96},{96,128},{128,160},{160,192},{192,224},{224... | collective-permute-start | bytes 196616 | tf_op jit(solution)/shard_map/ppermute | solution.py:18
  228.7 1.3 collective-permute-done.3
  230.0 2.4 collective-permute-done.4
  232.4 0.6 copy.32
  233.0 0.6 copy.33
  (42 shorter events, 4.5 us)
Async XLA Ops:
  7.2 76.3 %all-gather.7.cloned.1.call-start = ((), (), s32[]{:S(2)}) async-start(), calls=%async_computation.5 | async-start | bytes 4718592 | tf_op jit(solution)/shard_map/all_gather | solution.py:80
  20.6 104.0 %all-gather.9.cloned.1.call-start = ((), (), s32[]{:S(2)}) async-start(), calls=%async_computation.6 | async-start | bytes 2359296 | tf_op jit(solution)/shard_map/all_gather | solution.py:82
  31.2 180.6 %reduce-scatter.2.cloned.1.call-start = ((), (), s32[]{:S(2)}) async-start(), calls=%async_computation.4 | async-start | bytes 4718592 | tf_op jit(solution)/shard_map/reduce_scatter | solution.py:47
  87.0 40.5 %collective-permute-start = (bf16[256,256]{1,0:T(8,128)(2,1)S(1)}, bf16[256,256]{1,0:T(8,128)(2,1)S(1)}, u32[]{:S(2)}, u32[]{:S(2)}) collective-permute-start(bf16[256,256]{1,0:T(8,128)(2,1)S(1)} %get-tuple-element.39), channel_id=1, source_target_pairs={{384,256},{385,257},{386,258},{387,259},{388,260},{389,261},{390,2... | collective-permute-start | bytes 393224 | tf_op jit(solution)/shard_map/ppermute | solution.py:111
  87.6 39.9 %collective-permute-start.1 = (bf16[256,256]{1,0:T(8,128)(2,1)S(1)}, bf16[256,256]{1,0:T(8,128)(2,1)S(1)}, u32[]{:S(2)}, u32[]{:S(2)}) collective-permute-start(bf16[256,256]{1,0:T(8,128)(2,1)S(1)} %get-tuple-element.39), channel_id=1, source_target_pairs={{384,128},{385,129},{386,130},{387,131},{388,132},{389,133},{390,1... | collective-permute-start | bytes 393224 | tf_op jit(solution)/shard_map/ppermute | solution.py:111
  88.3 39.2 %collective-permute-start.2 = (bf16[256,256]{1,0:T(8,128)(2,1)S(1)}, bf16[256,256]{1,0:T(8,128)(2,1)S(1)}, u32[]{:S(2)}, u32[]{:S(2)}) collective-permute-start(bf16[256,256]{1,0:T(8,128)(2,1)S(1)} %get-tuple-element.39), channel_id=1, source_target_pairs={{384,0},{385,1},{386,2},{387,3},{388,4},{389,5},{390,6},{391,7},{3... | collective-permute-start | bytes 393224 | tf_op jit(solution)/shard_map/ppermute | solution.py:111
  156.3 0.7 copy-start.3
  202.8 22.7 %copy-start.1 = (bf16[1,2,128,256]{3,2,1,0:T(8,128)(2,1)S(1)}, bf16[1,2,128,256]{3,2,1,0:T(8,128)(2,1)}, u32[]{:S(2)}) copy-start(bf16[1,2,128,256]{3,2,1,0:T(8,128)(2,1)} %param.6) | copy-start | bytes 393220
  202.8 22.7 %copy-start.2 = (bf16[1,128,256]{2,1,0:T(8,128)(2,1)S(1)}, bf16[1,128,256]{2,1,0:T(8,128)(2,1)}, u32[]{:S(2)}) copy-start(bf16[1,128,256]{2,1,0:T(8,128)(2,1)} %param.7) | copy-start | bytes 196612
  225.6 4.4 %collective-permute-start.3 = (bf16[1,128,256]{2,1,0:T(8,128)(2,1)S(1)}, bf16[1,128,256]{2,1,0:T(8,128)(2,1)S(1)}, u32[]{:S(2)}, u32[]{:S(2)}) collective-permute-start(bf16[1,128,256]{2,1,0:T(8,128)(2,1)S(1)} %get-tuple-element.57), channel_id=1, source_target_pairs={{0,32},{32,64},{64,96},{96,128},{128,160},{160,192},{192,224},{224... | collective-permute-start | bytes 196616 | tf_op jit(solution)/shard_map/ppermute | solution.py:18
  228.7 3.7 %collective-permute-start.4 = (bf16[1,128,256]{2,1,0:T(8,128)(2,1)S(1)}, bf16[1,128,256]{2,1,0:T(8,128)(2,1)S(1)}, u32[]{:S(2)}, u32[]{:S(2)}) collective-permute-start(bf16[1,128,256]{2,1,0:T(8,128)(2,1)S(1)} %get-tuple-element.56), channel_id=1, source_target_pairs={{0,480},{32,0},{64,32},{96,64},{128,96},{160,128},{192,160},{224,1... | collective-permute-start | bytes 196616 | tf_op jit(solution)/shard_map/ppermute | solution.py:18
Sparse Core Ops, SparseCore 0:
  20.7 62.7 all-gather.6
  85.6 38.9 all-gather.8
  156.5 55.2 reduce-scatter.1

commit v13 on v11

--- a/solution.py
+++ b/solution.py
@@ -109,7 +109,14 @@
     for target in range(last_group):
         arrived = lax.ppermute(encoded, "sg", [(last_group, target)])
         piece = jnp.where(group == target, arrived, piece)
-    pool = lax.all_gather(piece, "sr", axis=0, tiled=True).reshape(pool_blocks, NBLEN, 2 * head)
+    places = lax.axis_size("sr")
+    spot = lax.axis_index("sr")
+    held = [piece] + [
+        lax.ppermute(piece, "sr", [(i, (i + shift) % places) for i in range(places)])
+        for shift in range(1, places)
+    ]
+    ordered = jnp.roll(jnp.stack(held[::-1]), spot + 1, axis=0)
+    pool = ordered.reshape(pool_blocks, NBLEN, 2 * head)
     groups = tokens // GROUP
     local_nbr = neighbours[0]
     score_scale = 1.0 / math.sqrt(head)

time: 235 us -> 243 us (1.034)
  starting transfers between devices: 5.81 us -> 19.4 us
  blocking collectives: 82.1 us -> 69.5 us
  waiting for transfers between devices: 95.3 us -> 103 us
    ppermute x0 -> x3, starting transfers between devices: none -> 13.6 us  [per_device(): lax.ppermute(piece, 'sr', [(i, (i + shift) % places) for i in range(place...]
    all_gather x1 -> x0, blocking collectives: 13.1 us -> none  [per_device(): lax.all_gather(piece, 'sr', axis=0, tiled=True)]
    ppermute x0 -> x3, waiting for transfers between devices: none -> 4.36 us  [per_device(): lax.ppermute(piece, 'sr', [(i, (i + shift) % places) for i in range(place...]
    ppermute x3, waiting for transfers between devices: 5.22 us -> 7.92 us  [per_device(): arrived = lax.ppermute(encoded, 'sg', [(last_group, target)])]
  transfers between devices with their start and end apart: 7 -> 10, of which waited for: 4 -> 5; matrix products, arithmetic and copies ran while one was open for 4% -> 4% of each run, Pallas kernels for 0% -> 0%
where the time goes in v13:
time: 243 us; the launch traced here: 241 us
  waiting for transfers between devices  103 us (42%)
  blocking collectives  69.5 us (29%)
  starting transfers between devices  19.4 us (8%)
  local copies, waits for them, and re-layouts  17.3 us (7%)
  between operations  14.4 us (6%)
  matrix products  11.3 us (5%)
  other arithmetic  6.3 us (3%)
    all_gather x1, waiting for transfers between devices, per_device(): gathered = lax.all_gather(gathered, stage, axis=2, tiled=True)  79.7 us
    all_to_all x1, blocking collectives, segment_sum(): moved = lax.all_to_all(parts, axis, 0, 0, tiled=True)  23.7 us
    all_to_all x1, blocking collectives, segment_sum(): return lax.all_to_all(spread, axis, 0, 0, tiled=True).reshape(contrib.shape)  20 us
    ppermute x3, starting transfers between devices, per_device(): lax.ppermute(piece, 'sr', [(i, (i + shift) % places) for i in range(place...  13.6 us
    all_gather x1, blocking collectives, per_device(): gathered = lax.all_gather(gathered, stage, axis=2, tiled=True)  13.3 us
    all_to_all x1, blocking collectives, head_sum(): moved = lax.all_to_all(partial, axis[1], 0, 0, tiled=True)  12.4 us
    reduce_scatter x1, waiting for transfers between devices, head_sum(): lax.psum_scatter(parts, axis[0], scatter_dimension=0, tiled=True)[0]  8.6 us
    ppermute x3, waiting for transfers between devices, per_device(): arrived = lax.ppermute(encoded, 'sg', [(last_group, target)])  7.92 us
  transfers between devices with their start and end apart: 10, of which 5 were waited for; matrix products, arithmetic and copies ran while one was open for 4% of the time, Pallas kernels for 0%

profile of v13, /device:TPU:1, one launch (start us, length us, event | category | flops | bytes accessed | tf_op | source)
XLA Modules:
  0.0 240.7 jit_solution(14813527661428295488)
XLA Ops:
  7.2 1.0 pad_maximum_fusion.2
  8.2 13.3 %all_gather.6 = bf16[3,128,1024]{2,1,0:T(8,128)(2,1)} all-gather(bf16[3,128,256]{2,1,0:T(8,128)(2,1)S(1)} %pad_maximum_fusion.2), channel_id=1, replica_groups=mesh['sg'=4,'sr'=4,'my'=8,'mx'=4] {'mx'}, dimensions={2}, use_global_device_ids=true | all-gather | bytes 983040 | tf_op jit(solution)/shard_map/all_gather | solution.py:80
  21.6 3.8 %slice_bitcast_fusion.2 = (bf16[8192,128]{1,0:T(8,128)(2,1)}, bf16[8192,128]{1,0:T(8,128)(2,1)S(1)}) fusion(bf16[1,2,8192,128]{3,2,1,0:T(8,128)(2,1)} %param.8), kind=kLoop, calls=%fused_computation.15 | loop fusion | bytes 8388608 | tf_op jit(solution)/shard_map/squeeze | solution.py:86
  25.4 79.7 %all-gather.2.cloned.1.call-done = bf16[3,128,8192]{2,1,0:T(8,128)(2,1)} async-done(((bf16[3,128,1024]{2,1,0:T(8,128)(2,1)}), bf16[3,128,8192]{2,1,0:T(8,128)(2,1)}) %all-gather.2.cloned.1.call-update) | async-done | bytes 6291472 | tf_op jit(solution)/shard_map/all_gather | solution.py:80
  105.1 2.2 slice-done
  107.3 0.7 copy-done
  108.0 1.3 conditional.1
  108.0 1.3 convolution_convert_fusion
  109.3 1.3 collective-permute-start.2
  110.6 0.7 collective-permute-start.1
  111.3 0.7 collective-permute-start
  112.2 7.9 %collective-permute-done.2 = bf16[256,256]{1,0:T(8,128)(2,1)S(1)} collective-permute-done((bf16[256,256]{1,0:T(8,128)(2,1)S(1)}, bf16[256,256]{1,0:T(8,128)(2,1)S(1)}, u32[]{:S(2)}, u32[]{:S(2)}) %collective-permute-start.2) | collective-permute-done | bytes 131104 | tf_op jit(solution)/shard_map/ppermute | solution.py:110
  120.1 4.1 %collective-permute-start.3 = (bf16[256,256]{1,0:T(8,128)(2,1)S(1)}, bf16[256,256]{1,0:T(8,128)(2,1)S(1)}, u32[]{:S(2)}, u32[]{:S(2)}) collective-permute-start(bf16[256,256]{1,0:T(8,128)(2,1)S(1)} %select_select_fusion), channel_id=1, source_target_pairs={{0,96},{32,0},{64,32},{96,64},{1,97},{33,1},{65,33},{97,65},{2,98}... | collective-permute-start | bytes 393224 | tf_op jit(solution)/shard_map/ppermute | solution.py:115
  124.3 2.9 %fusion.12 = bf16[128,128]{1,0:T(8,128)(2,1)S(1)} fusion(bf16[3,128,8192]{2,1,0:T(8,128)(2,1)} %all-gather.2.cloned.1.call-done, bf16[1,2,8192,128]{3,2,1,0:T(8,128)(2,1)} %param.8), kind=kOutput, calls=%fused_computation.29 | convolution fusion | flops 268451840 | bytes 4227072 | tf_op jit(solution)/shard_map/dot_general | solution.py:136
  127.2 6.9 %collective-permute-start.5 = (bf16[256,256]{1,0:T(8,128)(2,1)S(1)}, bf16[256,256]{1,0:T(8,128)(2,1)S(1)}, u32[]{:S(2)}, u32[]{:S(2)}) collective-permute-start(bf16[256,256]{1,0:T(8,128)(2,1)S(1)} %select_select_fusion), channel_id=1, source_target_pairs={{0,32},{32,64},{64,96},{96,0},{1,33},{33,65},{65,97},{97,1},{2,34}... | collective-permute-start | bytes 393224 | tf_op jit(solution)/shard_map/ppermute | solution.py:115
  134.1 2.6 %collective-permute-start.4 = (bf16[256,256]{1,0:T(8,128)(2,1)S(1)}, bf16[256,256]{1,0:T(8,128)(2,1)S(1)}, u32[]{:S(2)}, u32[]{:S(2)}) collective-permute-start(bf16[256,256]{1,0:T(8,128)(2,1)S(1)} %select_select_fusion), channel_id=1, source_target_pairs={{0,64},{32,96},{64,0},{96,32},{1,65},{33,97},{65,1},{97,33},{2,66}... | collective-permute-start | bytes 393224 | tf_op jit(solution)/shard_map/ppermute | solution.py:115
  136.7 4.4 %collective-permute-done.4 = bf16[256,256]{1,0:T(8,128)(2,1)S(1)} collective-permute-done((bf16[256,256]{1,0:T(8,128)(2,1)S(1)}, bf16[256,256]{1,0:T(8,128)(2,1)S(1)}, u32[]{:S(2)}, u32[]{:S(2)}) %collective-permute-start.4) | collective-permute-done | bytes 131104 | tf_op jit(solution)/shard_map/ppermute | solution.py:115
  144.2 2.3 fusion.3
  146.5 2.5 %copy.23 = bf16[8192,128]{1,0:T(8,128)(2,1)} copy(bf16[8192,128]{0,1:T(8,128)(2,1)S(1)} %fusion.3) | data formatting | bytes 4194304 | tf_op jit(solution)/shard_map/stack | solution.py:146
  149.0 2.3 fusion.2
  151.3 2.5 %copy.22 = bf16[8192,128]{1,0:T(8,128)(2,1)} copy(bf16[8192,128]{0,1:T(8,128)(2,1)S(1)} %fusion.2) | data formatting | bytes 4194304 | tf_op jit(solution)/shard_map/stack | solution.py:146
  153.8 4.5 %maximum_bitcast_fusion = bf16[8,4,2,256,128]{4,3,2,1,0:T(8,128)(2,1)} fusion(bf16[1,8,4,256,128]{4,3,0,2,1:T(8,128)(2,1)} %bitcast.94, bf16[1,8,4,256,128]{4,3,0,2,1:T(8,128)(2,1)} %bitcast.95), kind=kLoop, calls=%fused_computation.12 | loop fusion | flops 2097152 | bytes 8388608 | tf_op jit(solution)/shard_map/transpose | solution.py:46
  160.4 23.7 %all_to_all.15 = bf16[16,64,256]{2,1,0:T(8,128)(2,1)S(1)} all-to-all(bf16[16,64,256]{2,1,0:T(8,128)(2,1)S(1)} %bitcast.98), channel_id=1, replica_groups=mesh['sg'=4,'sr'=4,'my'=8,'mx'=4] {'sg','sr'}, dimensions={0} | all-to-all | bytes 1048576 | tf_op jit(solution)/shard_map/all_to_all | solution.py:62
  184.2 20.0 %all_to_all.16 = bf16[16,64,256]{2,1,0:T(8,128)(2,1)S(1)} all-to-all(bf16[16,64,256]{2,1,0:T(8,128)(2,1)S(1)} %broadcast_in_dim.5), channel_id=1, replica_groups=mesh['sg'=4,'sr'=4,'my'=8,'mx'=4] {'sg','sr'}, dimensions={0} | all-to-all | bytes 1048576 | tf_op jit(solution)/shard_map/all_to_all | solution.py:65
  204.3 0.9 reshape_reshape.7
  205.2 8.6 %reduce-scatter.2.cloned.1.call-done = bf16[1,4,2,256,128]{4,3,2,1,0:T(8,128)(2,1)} async-done(((bf16[8,4,2,256,128]{4,3,2,1,0:T(8,128)(2,1)}), bf16[1,4,2,256,128]{4,3,2,1,0:T(8,128)(2,1)}) %reduce-scatter.2.cloned.1.call-update) | async-done | bytes 524304 | tf_op jit(solution)/shard_map/reduce_scatter | solution.py:47
  213.8 1.2 copy.20
  215.0 12.4 %all_to_all.17 = bf16[4,2,256,128]{2,3,1,0:T(8,128)(2,1)S(1)} all-to-all(bf16[4,2,256,128]{2,3,1,0:T(8,128)(2,1)S(1)} %copy.20), channel_id=1, replica_groups=mesh['sg'=4,'sr'=4,'my'=8,'mx'=4] {'mx'}, dimensions={0} | all-to-all | bytes 1048576 | tf_op jit(solution)/shard_map/all_to_all | solution.py:49
  227.5 1.8 collective-permute-start.7
  229.4 1.3 collective-permute-start.6
  230.7 1.9 collective-permute-done.7
  232.6 0.6 copy.39
  (56 shorter events, 6.3 us)
Async XLA Ops:
  7.2 97.9 %all-gather.2.cloned.1.call-start = ((), (), s32[]{:S(2)}) async-start(), calls=%async_computation.4 | async-start | bytes 7077888 | tf_op jit(solution)/shard_map/all_gather | solution.py:80
  21.5 192.2 %reduce-scatter.2.cloned.1.call-start = ((), (), s32[]{:S(2)}) async-start(), calls=%async_computation.5 | async-start | bytes 4718592 | tf_op jit(solution)/shard_map/reduce_scatter | solution.py:47
  105.1 2.2 slice-start
  105.1 2.9 %copy-start = (bf16[8192,128]{1,0:T(8,128)(2,1)S(1)}, bf16[8192,128]{1,0:T(8,128)(2,1)}, u32[]{:S(2)}) copy-start(bf16[8192,128]{1,0:T(8,128)(2,1)} %get-tuple-element.54) | copy-start | bytes 6291460
  108.0 4.0 %copy-start.3 = (s32[1,2,2,2]{3,2,1,0:T(2,128)S(1)}, s32[1,2,2,2]{3,2,1,0:T(2,128)}, u32[]{:S(2)}) copy-start(s32[1,2,2,2]{3,2,1,0:T(2,128)} %param.9) | copy-start | bytes 100
  109.3 10.8 %collective-permute-start.2 = (bf16[256,256]{1,0:T(8,128)(2,1)S(1)}, bf16[256,256]{1,0:T(8,128)(2,1)S(1)}, u32[]{:S(2)}, u32[]{:S(2)}) collective-permute-start(bf16[256,256]{1,0:T(8,128)(2,1)S(1)} %get-tuple-element.39), channel_id=1, source_target_pairs={{384,0},{385,1},{386,2},{387,3},{388,4},{389,5},{390,6},{391,7},{3... | collective-permute-start | bytes 393224 | tf_op jit(solution)/shard_map/ppermute | solution.py:110
  110.6 9.5 %collective-permute-start.1 = (bf16[256,256]{1,0:T(8,128)(2,1)S(1)}, bf16[256,256]{1,0:T(8,128)(2,1)S(1)}, u32[]{:S(2)}, u32[]{:S(2)}) collective-permute-start(bf16[256,256]{1,0:T(8,128)(2,1)S(1)} %get-tuple-element.39), channel_id=1, source_target_pairs={{384,128},{385,129},{386,130},{387,131},{388,132},{389,133},{390,1... | collective-permute-start | bytes 393224 | tf_op jit(solution)/shard_map/ppermute | solution.py:110
  111.3 8.8 %collective-permute-start = (bf16[256,256]{1,0:T(8,128)(2,1)S(1)}, bf16[256,256]{1,0:T(8,128)(2,1)S(1)}, u32[]{:S(2)}, u32[]{:S(2)}) collective-permute-start(bf16[256,256]{1,0:T(8,128)(2,1)S(1)} %get-tuple-element.39), channel_id=1, source_target_pairs={{384,256},{385,257},{386,258},{387,259},{388,260},{389,261},{390,2... | collective-permute-start | bytes 393224 | tf_op jit(solution)/shard_map/ppermute | solution.py:110
  120.1 16.5 %collective-permute-start.3 = (bf16[256,256]{1,0:T(8,128)(2,1)S(1)}, bf16[256,256]{1,0:T(8,128)(2,1)S(1)}, u32[]{:S(2)}, u32[]{:S(2)}) collective-permute-start(bf16[256,256]{1,0:T(8,128)(2,1)S(1)} %select_select_fusion), channel_id=1, source_target_pairs={{0,96},{32,0},{64,32},{96,64},{1,97},{33,1},{65,33},{97,65},{2,98}... | collective-permute-start | bytes 393224 | tf_op jit(solution)/shard_map/ppermute | solution.py:115
  127.2 13.9 %collective-permute-start.5 = (bf16[256,256]{1,0:T(8,128)(2,1)S(1)}, bf16[256,256]{1,0:T(8,128)(2,1)S(1)}, u32[]{:S(2)}, u32[]{:S(2)}) collective-permute-start(bf16[256,256]{1,0:T(8,128)(2,1)S(1)} %select_select_fusion), channel_id=1, source_target_pairs={{0,32},{32,64},{64,96},{96,0},{1,33},{33,65},{65,97},{97,1},{2,34}... | collective-permute-start | bytes 393224 | tf_op jit(solution)/shard_map/ppermute | solution.py:115
  134.1 7.0 %collective-permute-start.4 = (bf16[256,256]{1,0:T(8,128)(2,1)S(1)}, bf16[256,256]{1,0:T(8,128)(2,1)S(1)}, u32[]{:S(2)}, u32[]{:S(2)}) collective-permute-start(bf16[256,256]{1,0:T(8,128)(2,1)S(1)} %select_select_fusion), channel_id=1, source_target_pairs={{0,64},{32,96},{64,0},{96,32},{1,65},{33,97},{65,1},{97,33},{2,66}... | collective-permute-start | bytes 393224 | tf_op jit(solution)/shard_map/ppermute | solution.py:115
  204.3 23.2 %copy-start.1 = (bf16[1,2,128,256]{3,2,1,0:T(8,128)(2,1)S(1)}, bf16[1,2,128,256]{3,2,1,0:T(8,128)(2,1)}, u32[]{:S(2)}) copy-start(bf16[1,2,128,256]{3,2,1,0:T(8,128)(2,1)} %param.6) | copy-start | bytes 393220
  204.3 23.2 %copy-start.2 = (bf16[1,128,256]{2,1,0:T(8,128)(2,1)S(1)}, bf16[1,128,256]{2,1,0:T(8,128)(2,1)}, u32[]{:S(2)}) copy-start(bf16[1,128,256]{2,1,0:T(8,128)(2,1)} %param.7) | copy-start | bytes 196612
  227.5 5.0 %collective-permute-start.7 = (bf16[1,128,256]{2,1,0:T(8,128)(2,1)S(1)}, bf16[1,128,256]{2,1,0:T(8,128)(2,1)S(1)}, u32[]{:S(2)}, u32[]{:S(2)}) collective-permute-start(bf16[1,128,256]{2,1,0:T(8,128)(2,1)S(1)} %get-tuple-element.56), channel_id=1, source_target_pairs={{0,480},{32,0},{64,32},{96,64},{128,96},{160,128},{192,160},{224,1... | collective-permute-start | bytes 196616 | tf_op jit(solution)/shard_map/ppermute | solution.py:18
  229.4 3.2 %collective-permute-start.6 = (bf16[1,128,256]{2,1,0:T(8,128)(2,1)S(1)}, bf16[1,128,256]{2,1,0:T(8,128)(2,1)S(1)}, u32[]{:S(2)}, u32[]{:S(2)}) collective-permute-start(bf16[1,128,256]{2,1,0:T(8,128)(2,1)S(1)} %get-tuple-element.57), channel_id=1, source_target_pairs={{0,32},{32,64},{64,96},{96,128},{128,160},{160,192},{192,224},{224... | collective-permute-start | bytes 196616 | tf_op jit(solution)/shard_map/ppermute | solution.py:18
Sparse Core Ops, SparseCore 0:
  21.7 83.3 all-gather.1
  158.4 55.2 reduce-scatter.1

commit v14 on v11

--- a/solution.py
+++ b/solution.py
@@ -43,8 +43,9 @@
     rounded = terms.astype(jnp.bfloat16)
     if isinstance(axis, tuple):
         tall, wide = lax.axis_size(axis[0]), lax.axis_size(axis[1])
-        parts = rounded.reshape(count, tall, wide, width // (tall * wide), tokens).transpose(1, 2, 0, 3, 4)
-        partial = lax.psum_scatter(parts, axis[0], scatter_dimension=0, tiled=True)[0]
+        parts = tuple(r.reshape(tall, wide, width // (tall * wide), tokens) for r in rounded)
+        scattered = lax.psum_scatter(parts, axis[0], scatter_dimension=0, tiled=True)
+        partial = jnp.stack([p[0] for p in scattered], axis=1)
         partial, tie = lax.optimization_barrier((partial, tie))
         moved = lax.all_to_all(partial, axis[1], 0, 0, tiled=True)
         summed = jnp.sum(moved.astype(jnp.float32), axis=0)

time: 235 us -> 255 us (1.085)
  waiting for transfers between devices: 95.3 us -> 119 us
  starting transfers between devices: 5.81 us -> 10.2 us
  other arithmetic: 6.31 us -> 2.85 us
    reduce_scatter x1 -> x2, waiting for transfers between devices: 8.63 us -> 31.9 us  [head_sum(): lax.psum_scatter(parts, axis[0], scatter_dimension=0, tiled=True)]
    transpose x1 -> x0, other arithmetic: 4.54 us -> none  [head_sum(): rounded.reshape(count, tall, wide, width // (tall * wide), tokens)]
    ppermute x2, starting transfers between devices: 3.1 us -> 7.45 us  [from_behind(): lax.ppermute(x, axis, [(i, (i + by) % devices) for i in range(devices)])]
  transfers between devices with their start and end apart: 7 -> 8, of which waited for: 4 -> 4; matrix products, arithmetic and copies ran while one was open for 4% -> 6% of each run, Pallas kernels for 0% -> 0%
where the time goes in v14:
time: 255 us; the launch traced here: 253 us
  waiting for transfers between devices  119 us (47%)
  blocking collectives  80.3 us (31%)
  local copies, waits for them, and re-layouts  16.1 us (6%)
  between operations  14 us (5%)
  matrix products  11.3 us (4%)
  starting transfers between devices  10.2 us (4%)
  other arithmetic  2.85 us (1%)
    all_gather x1, waiting for transfers between devices, per_device(): gathered = lax.all_gather(gathered, stage, axis=2, tiled=True)  79.5 us
    reduce_scatter x2, waiting for transfers between devices, head_sum(): lax.psum_scatter(parts, axis[0], scatter_dimension=0, tiled=True)  31.9 us
    all_to_all x1, blocking collectives, segment_sum(): moved = lax.all_to_all(parts, axis, 0, 0, tiled=True)  23.3 us
    all_to_all x1, blocking collectives, segment_sum(): return lax.all_to_all(spread, axis, 0, 0, tiled=True).reshape(contrib.shape)  20 us
    all_gather x1, blocking collectives, per_device(): gathered = lax.all_gather(gathered, stage, axis=2, tiled=True)  13.3 us
    all_gather x1, blocking collectives, per_device(): lax.all_gather(piece, 'sr', axis=0, tiled=True)  13.1 us
    all_to_all x1, blocking collectives, head_sum(): moved = lax.all_to_all(partial, axis[1], 0, 0, tiled=True)  10.6 us
    ppermute x2, starting transfers between devices, from_behind(): lax.ppermute(x, axis, [(i, (i + by) % devices) for i in range(devices)])  7.45 us
  transfers between devices with their start and end apart: 8, of which 4 were waited for; matrix products, arithmetic and copies ran while one was open for 6% of the time, Pallas kernels for 0%

profile of v14, /device:TPU:1, one launch (start us, length us, event | category | flops | bytes accessed | tf_op | source)
XLA Modules:
  0.0 253.5 jit_solution(4701688512123943433)
XLA Ops:
  7.2 1.0 pad_maximum_fusion.3
  8.2 13.3 %all_gather.9 = bf16[3,128,1024]{2,1,0:T(8,128)(2,1)} all-gather(bf16[3,128,256]{2,1,0:T(8,128)(2,1)S(1)} %pad_maximum_fusion.3), channel_id=1, replica_groups=mesh['sg'=4,'sr'=4,'my'=8,'mx'=4] {'mx'}, dimensions={2}, use_global_device_ids=true | all-gather | bytes 983040 | tf_op jit(solution)/shard_map/all_gather | solution.py:81
  21.7 3.8 %slice_bitcast_fusion.2 = (bf16[8192,128]{1,0:T(8,128)(2,1)}, bf16[8192,128]{1,0:T(8,128)(2,1)S(1)}) fusion(bf16[1,2,8192,128]{3,2,1,0:T(8,128)(2,1)} %param.8), kind=kLoop, calls=%fused_computation.14 | loop fusion | bytes 8388608 | tf_op jit(solution)/shard_map/squeeze | solution.py:87
  25.6 79.5 %all-gather.2.cloned.1.call-done = bf16[3,128,8192]{2,1,0:T(8,128)(2,1)} async-done(((bf16[3,128,1024]{2,1,0:T(8,128)(2,1)}), bf16[3,128,8192]{2,1,0:T(8,128)(2,1)}) %all-gather.2.cloned.1.call-update) | async-done | bytes 6291472 | tf_op jit(solution)/shard_map/all_gather | solution.py:81
  105.1 2.2 slice-done
  107.3 0.7 copy-done
  108.0 1.3 conditional.1
  108.0 1.3 convolution_convert_fusion
  109.3 1.3 collective-permute-start.2
  110.6 0.7 collective-permute-start.1
  111.3 0.7 collective-permute-start
  112.0 2.9 %fusion.12 = bf16[128,128]{1,0:T(8,128)(2,1)S(1)} fusion(bf16[3,128,8192]{2,1,0:T(8,128)(2,1)} %all-gather.2.cloned.1.call-done, bf16[1,2,8192,128]{3,2,1,0:T(8,128)(2,1)} %param.8), kind=kOutput, calls=%fused_computation.28 | convolution fusion | flops 268451840 | bytes 4227072 | tf_op jit(solution)/shard_map/dot_general | solution.py:130
  114.9 5.2 %collective-permute-done.2 = bf16[256,256]{1,0:T(8,128)(2,1)S(1)} collective-permute-done((bf16[256,256]{1,0:T(8,128)(2,1)S(1)}, bf16[256,256]{1,0:T(8,128)(2,1)S(1)}, u32[]{:S(2)}, u32[]{:S(2)}) %collective-permute-start.2) | collective-permute-done | bytes 131104 | tf_op jit(solution)/shard_map/ppermute | solution.py:111
  120.1 13.1 %all_gather.11 = bf16[1024,256]{1,0:T(8,128)(2,1)S(1)} all-gather(bf16[256,256]{1,0:T(8,128)(2,1)S(1)} %select_select_fusion), channel_id=1, replica_groups=mesh['sg'=4,'sr'=4,'my'=8,'mx'=4] {'sr'}, dimensions={0}, use_global_device_ids=true | all-gather | bytes 655360 | tf_op jit(solution)/shard_map/all_gather | solution.py:113
  133.3 0.6 gather_fusion.1
  135.0 2.3 fusion.3
  137.3 2.5 copy.25
  139.9 0.6 gather_fusion
  141.2 2.3 fusion.2
  143.5 2.5 copy.24
  147.4 0.5 fusion.6
  148.0 23.3 %all_to_all.15 = bf16[16,64,256]{2,1,0:T(8,128)(2,1)S(1)} all-to-all(bf16[16,64,256]{2,1,0:T(8,128)(2,1)S(1)} %bitcast.85), channel_id=1, replica_groups=mesh['sg'=4,'sr'=4,'my'=8,'mx'=4] {'sg','sr'}, dimensions={0} | all-to-all | bytes 1048576 | tf_op jit(solution)/shard_map/all_to_all | solution.py:63
  171.4 20.0 %all_to_all.16 = bf16[16,64,256]{2,1,0:T(8,128)(2,1)S(1)} all-to-all(bf16[16,64,256]{2,1,0:T(8,128)(2,1)S(1)} %broadcast_in_dim.5), channel_id=1, replica_groups=mesh['sg'=4,'sr'=4,'my'=8,'mx'=4] {'sg','sr'}, dimensions={0} | all-to-all | bytes 1048576 | tf_op jit(solution)/shard_map/all_to_all | solution.py:66
  191.4 0.9 reshape_reshape.7
  192.4 31.9 %reduce-scatter.3.cloned.1.call-done = bf16[1,4,256,128]{3,2,1,0:T(8,128)(2,1)} async-done(((bf16[8,4,256,128]{3,2,1,0:T(8,128)(2,1)}), bf16[1,4,256,128]{3,2,1,0:T(8,128)(2,1)}) %reduce-scatter.3.cloned.1.call-update) | async-done | bytes 262160 | tf_op jit(solution)/shard_map/reduce_scatter | solution.py:47
  224.3 1.1 pad_maximum_fusion.1
  225.6 10.6 %all_to_all.17 = bf16[4,2,256,128]{2,3,1,0:T(8,128)(2,1)S(1)} all-to-all(bf16[4,2,256,128]{2,3,1,0:T(8,128)(2,1)S(1)} %copy.22), channel_id=1, replica_groups=mesh['sg'=4,'sr'=4,'my'=8,'mx'=4] {'mx'}, dimensions={0} | all-to-all | bytes 1048576 | tf_op jit(solution)/shard_map/all_to_all | solution.py:50
  236.3 5.9 %collective-permute-start.4 = (bf16[1,128,256]{2,1,0:T(8,128)(2,1)S(1)}, bf16[1,128,256]{2,1,0:T(8,128)(2,1)S(1)}, u32[]{:S(2)}, u32[]{:S(2)}) collective-permute-start(bf16[1,128,256]{2,1,0:T(8,128)(2,1)S(1)} %get-tuple-element.56), channel_id=1, source_target_pairs={{0,480},{32,0},{64,32},{96,64},{128,96},{160,128},{192,160},{224,1... | collective-permute-start | bytes 196616 | tf_op jit(solution)/shard_map/ppermute | solution.py:18
  242.2 1.6 collective-permute-start.3
  243.8 1.9 collective-permute-done.4
  245.7 0.6 copy.34
  246.3 0.6 copy.35
  (46 shorter events, 4.2 us)
Async XLA Ops:
  7.2 14.5 %copy-start.3 = (s32[1,2,2,2]{3,2,1,0:T(2,128)S(1)}, s32[1,2,2,2]{3,2,1,0:T(2,128)}, u32[]{:S(2)}) copy-start(s32[1,2,2,2]{3,2,1,0:T(2,128)} %param.9) | copy-start | bytes 100
  7.2 97.9 %all-gather.2.cloned.1.call-start = ((), (), s32[]{:S(2)}) async-start(), calls=%async_computation.5 | async-start | bytes 7077888 | tf_op jit(solution)/shard_map/all_gather | solution.py:81
  21.6 170.8 %reduce-scatter.5.cloned.1.call-start = ((), (), s32[]{:S(2)}) async-start(), calls=%async_computation.7 | async-start | bytes 2359296 | tf_op jit(solution)/shard_map/reduce_scatter | solution.py:47
  105.1 2.2 slice-start
  105.1 2.9 %copy-start = (bf16[8192,128]{1,0:T(8,128)(2,1)S(1)}, bf16[8192,128]{1,0:T(8,128)(2,1)}, u32[]{:S(2)}) copy-start(bf16[8192,128]{1,0:T(8,128)(2,1)} %get-tuple-element.54) | copy-start | bytes 6291460
  109.3 10.8 %collective-permute-start.2 = (bf16[256,256]{1,0:T(8,128)(2,1)S(1)}, bf16[256,256]{1,0:T(8,128)(2,1)S(1)}, u32[]{:S(2)}, u32[]{:S(2)}) collective-permute-start(bf16[256,256]{1,0:T(8,128)(2,1)S(1)} %get-tuple-element.39), channel_id=1, source_target_pairs={{384,0},{385,1},{386,2},{387,3},{388,4},{389,5},{390,6},{391,7},{3... | collective-permute-start | bytes 393224 | tf_op jit(solution)/shard_map/ppermute | solution.py:111
  110.6 9.5 %collective-permute-start.1 = (bf16[256,256]{1,0:T(8,128)(2,1)S(1)}, bf16[256,256]{1,0:T(8,128)(2,1)S(1)}, u32[]{:S(2)}, u32[]{:S(2)}) collective-permute-start(bf16[256,256]{1,0:T(8,128)(2,1)S(1)} %get-tuple-element.39), channel_id=1, source_target_pairs={{384,128},{385,129},{386,130},{387,131},{388,132},{389,133},{390,1... | collective-permute-start | bytes 393224 | tf_op jit(solution)/shard_map/ppermute | solution.py:111
  111.3 8.8 %collective-permute-start = (bf16[256,256]{1,0:T(8,128)(2,1)S(1)}, bf16[256,256]{1,0:T(8,128)(2,1)S(1)}, u32[]{:S(2)}, u32[]{:S(2)}) collective-permute-start(bf16[256,256]{1,0:T(8,128)(2,1)S(1)} %get-tuple-element.39), channel_id=1, source_target_pairs={{384,256},{385,257},{386,258},{387,259},{388,260},{389,261},{390,2... | collective-permute-start | bytes 393224 | tf_op jit(solution)/shard_map/ppermute | solution.py:111
  139.8 84.5 %reduce-scatter.3.cloned.1.call-start = ((), (), s32[]{:S(2)}) async-start(), calls=%async_computation.6 | async-start | bytes 2359296 | tf_op jit(solution)/shard_map/reduce_scatter | solution.py:47
  192.4 43.9 %copy-start.1 = (bf16[1,2,128,256]{3,2,1,0:T(8,128)(2,1)S(1)}, bf16[1,2,128,256]{3,2,1,0:T(8,128)(2,1)}, u32[]{:S(2)}) copy-start(bf16[1,2,128,256]{3,2,1,0:T(8,128)(2,1)} %param.6) | copy-start | bytes 393220
  192.4 43.9 %copy-start.2 = (bf16[1,128,256]{2,1,0:T(8,128)(2,1)S(1)}, bf16[1,128,256]{2,1,0:T(8,128)(2,1)}, u32[]{:S(2)}) copy-start(bf16[1,128,256]{2,1,0:T(8,128)(2,1)} %param.7) | copy-start | bytes 196612
  236.3 9.4 %collective-permute-start.4 = (bf16[1,128,256]{2,1,0:T(8,128)(2,1)S(1)}, bf16[1,128,256]{2,1,0:T(8,128)(2,1)S(1)}, u32[]{:S(2)}, u32[]{:S(2)}) collective-permute-start(bf16[1,128,256]{2,1,0:T(8,128)(2,1)S(1)} %get-tuple-element.56), channel_id=1, source_target_pairs={{0,480},{32,0},{64,32},{96,64},{128,96},{160,128},{192,160},{224,1... | collective-permute-start | bytes 196616 | tf_op jit(solution)/shard_map/ppermute | solution.py:18
  242.2 3.5 %collective-permute-start.3 = (bf16[1,128,256]{2,1,0:T(8,128)(2,1)S(1)}, bf16[1,128,256]{2,1,0:T(8,128)(2,1)S(1)}, u32[]{:S(2)}, u32[]{:S(2)}) collective-permute-start(bf16[1,128,256]{2,1,0:T(8,128)(2,1)S(1)} %get-tuple-element.57), channel_id=1, source_target_pairs={{0,32},{32,64},{64,96},{96,128},{128,160},{160,192},{192,224},{224... | collective-permute-start | bytes 196616 | tf_op jit(solution)/shard_map/ppermute | solution.py:18
Sparse Core Ops, SparseCore 0:
  21.7 83.3 all-gather.1
  139.9 37.6 reduce-scatter.4
  180.5 43.7 reduce-scatter.2

commit v15 on v11

--- a/solution.py
+++ b/solution.py
@@ -136,11 +136,11 @@
         query_blocks[1], keys_back, values_back, soft_back, rounded_back, upstream, score_scale
     )
     grad_flat = grad_queries.reshape(tokens, head)
-    terms = jnp.stack(
-        [
-            lax.dot_general(w_out, mixed_flat, (((1,), (1,)), ((), ())), preferred_element_type=jnp.float32),
-            lax.dot_general(w_query, grad_flat, (((1,), (1,)), ((), ())), preferred_element_type=jnp.float32),
-        ]
+    terms = jnp.einsum(
+        "kfd,ktd->kft",
+        weights[0][::-1],
+        jnp.stack([mixed_flat, grad_flat]),
+        preferred_element_type=jnp.float32,
     )
     onehot = (
         local_nbr[1][..., None] == jnp.arange(pool_blocks, dtype=jnp.int32)[None, None, :]

time: 235 us -> 242 us (1.030)
  local copies, waits for them, and re-layouts: 17.2 us -> 28.2 us
  other arithmetic: 6.31 us -> 2.47 us
    reshape x0 -> x2, local copies, waits for them, and re-layouts: none -> 15.3 us  [head_sum(): rounded.reshape(count, tall, wide, width // (tall * wide), tokens)]
    another operation x3 -> x1, local copies, waits for them, and re-layouts: 4.94 us -> 0.01 us  [the longest x2 4.93 us: per_device(): jnp.stack([lax.dot_general(w_out, mixed_flat, (((1,), (1,)), ((), ())), p...]
    transpose x1 -> x0, other arithmetic: 4.54 us -> none  [head_sum(): rounded.reshape(count, tall, wide, width // (tall * wide), tokens)]
    dot_general x2 -> x1, matrix products: 4.59 us -> 5.42 us  [per_device(): jnp.einsum('kfd,ktd->kft', weights[0][::-1], jnp.stack([mixed_flat, grad_...]
where the time goes in v15:
time: 242 us; the launch traced here: 239 us
  waiting for transfers between devices  93.9 us (39%)
  blocking collectives  82.1 us (34%)
  local copies, waits for them, and re-layouts  28.2 us (12%)
  between operations  14.2 us (6%)
  matrix products  12.1 us (5%)
  starting transfers between devices  5.84 us (2%)
  other arithmetic  2.47 us (1%)
    all_gather x1, waiting for transfers between devices, per_device(): gathered = lax.all_gather(gathered, stage, axis=2, tiled=True)  78.8 us
    all_to_all x1, blocking collectives, segment_sum(): moved = lax.all_to_all(parts, axis, 0, 0, tiled=True)  23.3 us
    all_to_all x1, blocking collectives, segment_sum(): return lax.all_to_all(spread, axis, 0, 0, tiled=True).reshape(contrib.shape)  20 us
    reshape x2, local copies, waits for them, and re-layouts, head_sum(): rounded.reshape(count, tall, wide, width // (tall * wide), tokens)  15.3 us
    all_gather x1, blocking collectives, per_device(): gathered = lax.all_gather(gathered, stage, axis=2, tiled=True)  13.3 us
    all_gather x1, blocking collectives, per_device(): lax.all_gather(piece, 'sr', axis=0, tiled=True)  13.1 us
    all_to_all x1, blocking collectives, head_sum(): moved = lax.all_to_all(partial, axis[1], 0, 0, tiled=True)  12.4 us
    reduce_scatter x1, waiting for transfers between devices, head_sum(): lax.psum_scatter(parts, axis[0], scatter_dimension=0, tiled=True)[0]  7.94 us
  transfers between devices with their start and end apart: 7, of which 4 were waited for; matrix products, arithmetic and copies ran while one was open for 4% of the time, Pallas kernels for 0%

profile of v15, /device:TPU:1, one launch (start us, length us, event | category | flops | bytes accessed | tf_op | source)
XLA Modules:
  0.0 238.9 jit_solution(3224334287129383548)
XLA Ops:
  7.2 1.0 pad_maximum_fusion.2
  8.2 13.3 %all_gather.9 = bf16[3,128,1024]{2,1,0:T(8,128)(2,1)} all-gather(bf16[3,128,256]{2,1,0:T(8,128)(2,1)S(1)} %pad_maximum_fusion.2), channel_id=1, replica_groups=mesh['sg'=4,'sr'=4,'my'=8,'mx'=4] {'mx'}, dimensions={2}, use_global_device_ids=true | all-gather | bytes 983040 | tf_op jit(solution)/shard_map/all_gather | solution.py:80
  21.6 0.7 compare_select_fusion.1
  22.5 3.8 %slice_bitcast_fusion.2 = (bf16[8192,128]{1,0:T(8,128)(2,1)}, bf16[8192,128]{1,0:T(8,128)(2,1)S(1)}) fusion(bf16[1,2,8192,128]{3,2,1,0:T(8,128)(2,1)} %param.8), kind=kLoop, calls=%fused_computation.13 | loop fusion | bytes 8388608 | tf_op jit(solution)/shard_map/squeeze | solution.py:86
  26.3 78.8 %all-gather.2.cloned.1.call-done = bf16[3,128,8192]{2,1,0:T(8,128)(2,1)} async-done(((bf16[3,128,1024]{2,1,0:T(8,128)(2,1)}), bf16[3,128,8192]{2,1,0:T(8,128)(2,1)}) %all-gather.2.cloned.1.call-update) | async-done | bytes 6291472 | tf_op jit(solution)/shard_map/all_gather | solution.py:80
  105.1 2.2 slice-done
  107.3 0.7 copy-done
  108.0 1.3 conditional.1
  108.0 1.3 convolution_convert_fusion
  109.3 1.3 collective-permute-start.2
  110.6 0.7 collective-permute-start.1
  111.3 0.7 collective-permute-start
  112.0 2.9 %fusion.12 = bf16[128,128]{1,0:T(8,128)(2,1)S(1)} fusion(bf16[3,128,8192]{2,1,0:T(8,128)(2,1)} %all-gather.2.cloned.1.call-done, bf16[1,2,8192,128]{3,2,1,0:T(8,128)(2,1)} %param.8), kind=kOutput, calls=%fused_computation.27 | convolution fusion | flops 268451840 | bytes 4227072 | tf_op jit(solution)/shard_map/dot_general | solution.py:129
  114.9 5.2 %collective-permute-done.2 = bf16[256,256]{1,0:T(8,128)(2,1)S(1)} collective-permute-done((bf16[256,256]{1,0:T(8,128)(2,1)S(1)}, bf16[256,256]{1,0:T(8,128)(2,1)S(1)}, u32[]{:S(2)}, u32[]{:S(2)}) %collective-permute-start.2) | collective-permute-done | bytes 131104 | tf_op jit(solution)/shard_map/ppermute | solution.py:110
  120.1 13.1 %all_gather.11 = bf16[1024,256]{1,0:T(8,128)(2,1)S(1)} all-gather(bf16[256,256]{1,0:T(8,128)(2,1)S(1)} %select_select_fusion), channel_id=1, replica_groups=mesh['sg'=4,'sr'=4,'my'=8,'mx'=4] {'sr'}, dimensions={0}, use_global_device_ids=true | all-gather | bytes 655360 | tf_op jit(solution)/shard_map/all_gather | solution.py:112
  133.3 0.6 gather_fusion.1
  133.8 0.6 gather_fusion
  136.2 5.4 %fusion.2 = bf16[2,8192,128]{1,2,0:T(8,128)(2,1)} fusion(bf16[1,2,8192,128]{3,2,1,0:T(8,128)(2,1)} %param.8, bf16[1,128,128]{2,1,0:T(8,128)(2,1)S(1)} %bitcast.93, bf16[1,128,128]{2,1,0:T(8,128)(2,1)S(1)} %bitcast.92), kind=kOutput, calls=%fused_computation.9 | convolution fusion | flops 539000832 | bytes 8454144 | tf_op jit(solution)/shard_map/kfd,ktd->kft/dot_general | solution.py:139
  141.6 7.8 %reshape.123 = bf16[2,8,4,256,128]{3,2,1,4,0:T(4,128)(2,1)} reshape(bf16[2,8192,128]{1,2,0:T(8,128)(2,1)} %fusion.2) | data formatting | bytes 8388608 | tf_op jit(solution)/shard_map/reshape | solution.py:46
  149.5 7.5 %copy.15 = bf16[2,8,4,256,128]{4,3,0,2,1:T(8,128)(2,1)} copy(bf16[2,8,4,256,128]{3,2,1,4,0:T(4,128)(2,1)} %reshape.123) | data formatting | bytes 8388608 | tf_op jit(solution)/shard_map/reshape | solution.py:46
  157.0 0.7 copy-done.3
  159.7 23.3 %all_to_all.15 = bf16[16,64,256]{2,1,0:T(8,128)(2,1)S(1)} all-to-all(bf16[16,64,256]{2,1,0:T(8,128)(2,1)S(1)} %bitcast.81), channel_id=1, replica_groups=mesh['sg'=4,'sr'=4,'my'=8,'mx'=4] {'sg','sr'}, dimensions={0} | all-to-all | bytes 1048576 | tf_op jit(solution)/shard_map/all_to_all | solution.py:62
  183.1 20.0 %all_to_all.16 = bf16[16,64,256]{2,1,0:T(8,128)(2,1)S(1)} all-to-all(bf16[16,64,256]{2,1,0:T(8,128)(2,1)S(1)} %broadcast_in_dim.5), channel_id=1, replica_groups=mesh['sg'=4,'sr'=4,'my'=8,'mx'=4] {'sg','sr'}, dimensions={0} | all-to-all | bytes 1048576 | tf_op jit(solution)/shard_map/all_to_all | solution.py:65
  203.2 0.9 reshape_reshape.7
  204.1 7.9 %reduce-scatter.2.cloned.1.call-done = bf16[1,4,2,256,128]{4,3,2,1,0:T(8,128)(2,1)} async-done(((bf16[8,4,2,256,128]{4,3,2,1,0:T(8,128)(2,1)}), bf16[1,4,2,256,128]{4,3,2,1,0:T(8,128)(2,1)}) %reduce-scatter.2.cloned.1.call-update) | async-done | bytes 524304 | tf_op jit(solution)/shard_map/reduce_scatter | solution.py:47
  212.0 1.2 copy.19
  213.3 12.4 %all_to_all.17 = bf16[4,2,256,128]{2,3,1,0:T(8,128)(2,1)S(1)} all-to-all(bf16[4,2,256,128]{2,3,1,0:T(8,128)(2,1)S(1)} %copy.19), channel_id=1, replica_groups=mesh['sg'=4,'sr'=4,'my'=8,'mx'=4] {'mx'}, dimensions={0} | all-to-all | bytes 1048576 | tf_op jit(solution)/shard_map/all_to_all | solution.py:49
  225.8 1.8 collective-permute-start.4
  227.6 1.3 collective-permute-start.3
  228.9 1.9 collective-permute-done.4
  230.8 0.6 copy.29
  231.5 0.6 copy.30
  (41 shorter events, 4.4 us)
Async XLA Ops:
  7.2 97.9 %all-gather.2.cloned.1.call-start = ((), (), s32[]{:S(2)}) async-start(), calls=%async_computation.4 | async-start | bytes 7077888 | tf_op jit(solution)/shard_map/all_gather | solution.py:80
  21.5 190.5 %reduce-scatter.2.cloned.1.call-start = ((), (), s32[]{:S(2)}) async-start(), calls=%async_computation.5 | async-start | bytes 4718592 | tf_op jit(solution)/shard_map/reduce_scatter | solution.py:47
  105.1 2.2 slice-start
  105.1 2.9 %copy-start = (bf16[8192,128]{1,0:T(8,128)(2,1)S(1)}, bf16[8192,128]{1,0:T(8,128)(2,1)}, u32[]{:S(2)}) copy-start(bf16[8192,128]{1,0:T(8,128)(2,1)} %get-tuple-element.54) | copy-start | bytes 6291460
  109.3 10.8 %collective-permute-start.2 = (bf16[256,256]{1,0:T(8,128)(2,1)S(1)}, bf16[256,256]{1,0:T(8,128)(2,1)S(1)}, u32[]{:S(2)}, u32[]{:S(2)}) collective-permute-start(bf16[256,256]{1,0:T(8,128)(2,1)S(1)} %get-tuple-element.39), channel_id=1, source_target_pairs={{384,0},{385,1},{386,2},{387,3},{388,4},{389,5},{390,6},{391,7},{3... | collective-permute-start | bytes 393224 | tf_op jit(solution)/shard_map/ppermute | solution.py:110
  110.6 9.5 %collective-permute-start.1 = (bf16[256,256]{1,0:T(8,128)(2,1)S(1)}, bf16[256,256]{1,0:T(8,128)(2,1)S(1)}, u32[]{:S(2)}, u32[]{:S(2)}) collective-permute-start(bf16[256,256]{1,0:T(8,128)(2,1)S(1)} %get-tuple-element.39), channel_id=1, source_target_pairs={{384,128},{385,129},{386,130},{387,131},{388,132},{389,133},{390,1... | collective-permute-start | bytes 393224 | tf_op jit(solution)/shard_map/ppermute | solution.py:110
  111.3 8.8 %collective-permute-start = (bf16[256,256]{1,0:T(8,128)(2,1)S(1)}, bf16[256,256]{1,0:T(8,128)(2,1)S(1)}, u32[]{:S(2)}, u32[]{:S(2)}) collective-permute-start(bf16[256,256]{1,0:T(8,128)(2,1)S(1)} %get-tuple-element.39), channel_id=1, source_target_pairs={{384,256},{385,257},{386,258},{387,259},{388,260},{389,261},{390,2... | collective-permute-start | bytes 393224 | tf_op jit(solution)/shard_map/ppermute | solution.py:110
  157.0 0.7 copy-start.3
  159.6 66.1 %copy-start.1 = (bf16[1,2,128,256]{3,2,1,0:T(8,128)(2,1)S(1)}, bf16[1,2,128,256]{3,2,1,0:T(8,128)(2,1)}, u32[]{:S(2)}) copy-start(bf16[1,2,128,256]{3,2,1,0:T(8,128)(2,1)} %param.6) | copy-start | bytes 393220
  159.6 66.1 %copy-start.2 = (bf16[1,128,256]{2,1,0:T(8,128)(2,1)S(1)}, bf16[1,128,256]{2,1,0:T(8,128)(2,1)}, u32[]{:S(2)}) copy-start(bf16[1,128,256]{2,1,0:T(8,128)(2,1)} %param.7) | copy-start | bytes 196612
  225.8 5.1 %collective-permute-start.4 = (bf16[1,128,256]{2,1,0:T(8,128)(2,1)S(1)}, bf16[1,128,256]{2,1,0:T(8,128)(2,1)S(1)}, u32[]{:S(2)}, u32[]{:S(2)}) collective-permute-start(bf16[1,128,256]{2,1,0:T(8,128)(2,1)S(1)} %get-tuple-element.56), channel_id=1, source_target_pairs={{0,480},{32,0},{64,32},{96,64},{128,96},{160,128},{192,160},{224,1... | collective-permute-start | bytes 196616 | tf_op jit(solution)/shard_map/ppermute | solution.py:18
  227.6 3.2 %collective-permute-start.3 = (bf16[1,128,256]{2,1,0:T(8,128)(2,1)S(1)}, bf16[1,128,256]{2,1,0:T(8,128)(2,1)S(1)}, u32[]{:S(2)}, u32[]{:S(2)}) collective-permute-start(bf16[1,128,256]{2,1,0:T(8,128)(2,1)S(1)} %get-tuple-element.57), channel_id=1, source_target_pairs={{0,32},{32,64},{64,96},{96,128},{128,160},{160,192},{192,224},{224... | collective-permute-start | bytes 196616 | tf_op jit(solution)/shard_map/ppermute | solution.py:18
Sparse Core Ops, SparseCore 0:
  21.7 83.3 all-gather.1
  157.1 54.8 reduce-scatter.1
